TPU v7x, 256 devices: a whole 4x4x8 slice. The times are simulated.
256 devices in a mesh: seq: 32 (over x, z), row: 2 (over core), col: 4 (over y).
Axes of the slice: x: 4, y: 4, z: 8, core: 2. Of those that a mesh axis runs over, the one named last changes fastest.
Arguments:
- hidden: bfloat16 [16384, 4096], P(('seq', 'row'), 'col'), may hold values from -6 to 6
- w_x: bfloat16 [4096, 4, 1024], P('col', None, 'row'), may hold values from -0.09375 to 0.09375
- w_z: bfloat16 [4096, 4, 1024], P('col', None, 'row'), may hold values from -0.09375 to 0.09375
- w_bc: bfloat16 [4096, 4, 256], P('col'), may hold values from -0.09375 to 0.09375
- w_dt: bfloat16 [4096, 4, 16], P('col', None, 'row'), may hold values from -0.09375 to 0.09375
- conv_x_w: bfloat16 [4, 4, 1024], P(None, 'col', 'row'), may hold values from -3 to 3
- conv_bc_w: bfloat16 [4, 4, 256], P(None, 'col'), may hold values from -3 to 3
- conv_x_bias: bfloat16 [4, 1024], P('col', 'row'), may hold values from -3 to 3
- conv_bc_bias: bfloat16 [4, 256], P('col'), may hold values from -3 to 3
- dt_bias: float32 [4, 16], P('col', 'row'), may hold values from -5 to -2
- decay_rate: float32 [4, 16], P('col', 'row'), may hold values from 0.005 to 2
- d_skip: float32 [4, 16], P('col', 'row'), may hold values from 0.5 to 1.5
- norm_gain: float32 [4, 1024], P('col', 'row'), may hold values from 0.5 to 1.5
- starts: int32 [16384], P('seq'), may hold values from 0 to 1, as said below
- init_states: float32 [96, 4, 16, 64, 128], P('seq', 'col', 'row'), may hold values from -1.2 to 1.2
- conv_x_edges: bfloat16 [96, 3, 4, 1024], P('seq', None, 'col', 'row'), may hold values from -6 to 6
- conv_bc_edges: bfloat16 [96, 3, 4, 256], P('seq', None, 'col'), may hold values from -6 to 6
Outputs:
- gated_out: bfloat16 [16384, 4, 1024], P('seq', 'col', 'row')
- final_states: float32 [96, 4, 16, 64, 128], P('seq', 'col', 'row')
Inputs may be any that keep to these rules, and one draw needn't show every extreme that they name: The first token of all has starts 1. The 512 tokens of one index of seq hold at most 3 ones, and some index holds exactly 3. The last two indices of seq each hold one or more ones. Slot j of an index of seq in init_states, conv_x_edges, conv_bc_edges and final_states belongs to the j-th request that begins among its tokens; the others are not read.
All inputs are finite; a program needn't handle non-finite values.
Results may differ from a plain program's by a relative error of at most 0.0057.
Values may be sent and summed in bfloat16 or wider, within the bound.
No kernel may reach another device: no remote copies, remote signals or barrier semaphores. Data moves between devices by JAX's collectives and lax.ppermute only.
A program may use at most 128 MiB of HBM per device.

v0:
```python
import jax
import jax.numpy as jnp
from jax import lax
from jax.sharding import PartitionSpec as P

P_SIZE = 64
N = 128


PRECISE = lax.Precision.HIGHEST
EPSILON = 1e-05


def from_behind(value, axis, steps):
    count = lax.axis_size(axis)
    first, last = (max(0, -steps), min(count, count - steps))
    return lax.ppermute(value, axis, [(source, source + steps) for source in range(first, last)])


def local_terms(x_vals, b_proj, c_proj, dt_vals, flag_vals, init_vals, rate_vals):
    rows_here = x_vals.shape[0]
    slot_total = init_vals.shape[0]
    positions = jnp.arange(rows_here, dtype=jnp.int32)
    segment = jnp.cumsum(flag_vals.astype(jnp.int32))
    started = segment[rows_here - 1]
    log_decay = -dt_vals * rate_vals[None, :]
    cumulative = jnp.cumsum(log_decay, axis=0)
    preceding = cumulative - log_decay
    start_at = lax.cummax(jnp.where(flag_vals, positions, 0), axis=0)
    baseline = jnp.where((segment > 0)[:, None], preceding[start_at], 0.0)
    joined = (segment[:, None] == segment[None, :]) & (positions[:, None] >= positions[None, :])
    intersection = jnp.dot(c_proj, b_proj.T, preferred_element_type=jnp.float32)
    cumul_t = cumulative.T
    spread = jnp.where(joined[None], cumul_t[:, :, None] - cumul_t[:, None, :], 0.0)
    mixing = (
        jnp.where(joined[None], jnp.exp(spread), 0.0) * intersection[None] * dt_vals.T[:, None, :]
    )
    internal = jnp.einsum("hij,jhp->ihp", mixing, x_vals.astype(jnp.float32), precision=PRECISE)
    from_slot = jnp.einsum(
        "tn,shpn->tshp", c_proj.astype(jnp.float32), init_vals, precision=PRECISE
    )
    slot_ids = jnp.arange(1, slot_total + 1, dtype=jnp.int32)
    chosen = (segment[:, None] == slot_ids[None, :]).astype(jnp.float32)
    restarted = jnp.einsum("ts,tshp->thp", chosen, from_slot, precision=PRECISE)
    y_part = internal + jnp.exp(cumulative - baseline)[:, :, None] * restarted
    carried = jnp.where((segment == 0)[:, None], jnp.exp(cumulative), 0.0)
    indices = jnp.arange(slot_total + 1, dtype=jnp.int32)
    belongs = segment[:, None] == indices[None, :]
    last_at = jnp.max(jnp.where(belongs, positions[:, None], -1), axis=0)
    first_at = jnp.min(jnp.where(belongs, positions[:, None], rows_here), axis=0)
    cumul_end = jnp.where((last_at >= 0)[:, None], cumulative[jnp.maximum(last_at, 0)], 0.0)
    lag_spread = jnp.where(belongs.T[:, :, None], cumul_end[:, None, :] - cumulative[None], 0.0)
    weights = jnp.where(belongs.T[:, :, None], jnp.exp(lag_spread), 0.0) * dt_vals[None]
    weighted = weights[..., None] * x_vals.astype(jnp.float32)[None]
    gathered = jnp.einsum("sthp,tn->shpn", weighted, b_proj.astype(jnp.float32), precision=PRECISE)
    base_slot = preceding[jnp.minimum(first_at, rows_here - 1)]
    factor = jnp.exp(jnp.where((slot_ids <= started)[:, None], cumul_end[1:] - base_slot[1:], 0.0))
    in_use = slot_ids <= started
    seg_rest = gathered[1:] + jnp.where(
        in_use[:, None, None, None], factor[..., None, None] * init_vals, 0.0
    )
    seg_ends = jnp.concatenate([gathered[:1], seg_rest], axis=0)
    decay_all = jnp.where(started == 0, jnp.exp(cumulative[rows_here - 1]), 0.0)
    state_add = jnp.sum(jnp.where((indices == started)[:, None, None, None], seg_ends, 0.0), axis=0)
    return (y_part, carried, seg_ends, decay_all, state_add, cumul_end[0], started)


def tail_rows(raw, edges, start_last, segment_last, lagged):
    rows_here = raw.shape[0]
    source = jnp.arange(rows_here - lagged, rows_here, dtype=jnp.int32)
    inside = source >= start_last
    row_pick = jnp.clip(lagged - start_last + source, 0, lagged - 1)
    from_edge = edges[jnp.maximum(segment_last - 1, 0), row_pick]
    return jnp.where(inside[:, None], raw[rows_here - lagged :], from_edge)


def convolve(raw, prior, edges, kernel, offset_bias, start_at, segment, positions, lagged):
    rows_here = raw.shape[0]
    slot_total = edges.shape[0]
    extended = jnp.concatenate([prior, raw], axis=0)
    table = edges.reshape(slot_total * lagged, edges.shape[-1])
    total = offset_bias[None].astype(jnp.float32) + kernel[lagged][None].astype(
        jnp.float32
    ) * raw.astype(jnp.float32)
    for offset in range(1, lagged + 1):
        source = positions - offset
        inside = source >= start_at
        row_pick = jnp.clip(lagged - start_at + source, 0, lagged - 1)
        which = jnp.maximum(segment - 1, 0) * lagged + row_pick
        picker = (
            which[:, None] == jnp.arange(slot_total * lagged, dtype=jnp.int32)[None, :]
        ).astype(jnp.bfloat16)
        from_edge = jnp.dot(picker, table, preferred_element_type=jnp.float32)
        earlier = extended[lagged - offset : lagged - offset + rows_here].astype(jnp.float32)
        total = total + kernel[lagged - offset][None].astype(jnp.float32) * jnp.where(
            inside[:, None], earlier, from_edge
        )
    return jax.nn.silu(total).astype(jnp.bfloat16)


def shards(
    hidden,
    w_x,
    w_z,
    w_bc,
    w_dt,
    conv_x_w,
    conv_bc_w,
    conv_x_bias,
    conv_bc_bias,
    dt_bias,
    decay_rate,
    d_skip,
    norm_gain,
    starts,
    init_states,
    conv_x_edges,
    conv_bc_edges,
):
    tokens = lax.all_gather(hidden, "row", axis=0, tiled=True)
    rows_here = tokens.shape[0]
    channels = w_x.shape[2]
    heads_here = w_dt.shape[2]
    lagged = conv_x_w.shape[0] - 1
    pieces = [
        jnp.einsum("td,dgc->gtc", tokens, weight, preferred_element_type=jnp.float32)
        for weight in (w_x, w_z, w_bc, w_dt)
    ]
    summed = lax.psum_scatter(
        jnp.concatenate(pieces, axis=2), "col", scatter_dimension=0, tiled=True
    )
    mixed = summed[0].astype(jnp.bfloat16)
    x_raw = mixed[:, :channels]
    z_gate = mixed[:, channels : 2 * channels]
    bc_raw = mixed[:, 2 * channels : 2 * channels + 2 * N]
    dt_raw = mixed[:, 2 * channels + 2 * N :]
    positions = jnp.arange(rows_here, dtype=jnp.int32)
    flag_vals = starts == 1
    segment = jnp.cumsum(starts)
    start_at = lax.cummax(jnp.where(flag_vals, positions, -lagged), axis=0)
    x_edges = conv_x_edges[:, :, 0]
    bc_edges = conv_bc_edges[:, :, 0]
    start_last = start_at[rows_here - 1]
    segment_last = segment[rows_here - 1]
    send_x = tail_rows(x_raw, x_edges, start_last, segment_last, lagged)
    send_bc = tail_rows(bc_raw, bc_edges, start_last, segment_last, lagged)
    prior_x, prior_bc = from_behind((send_x, send_bc), "seq", 1)
    x_conv = convolve(
        x_raw,
        prior_x,
        x_edges,
        conv_x_w[:, 0],
        conv_x_bias[0],
        start_at,
        segment,
        positions,
        lagged,
    )
    bc_conv = convolve(
        bc_raw,
        prior_bc,
        bc_edges,
        conv_bc_w[:, 0],
        conv_bc_bias[0],
        start_at,
        segment,
        positions,
        lagged,
    )
    x_heads = x_conv.reshape(rows_here, heads_here, P_SIZE)
    b_proj = bc_conv[:, :N]
    c_proj = bc_conv[:, N:]
    dt_vals = jax.nn.softplus(dt_raw.astype(jnp.float32) + dt_bias[0][None, :])
    init_vals = init_states[:, 0]
    y_part, carried, seg_ends, decay_all, state_add, end_zero, started = local_terms(
        x_heads, b_proj, c_proj, dt_vals, flag_vals, init_vals, decay_rate[0]
    )

    def advance(turn, carry):
        return from_behind(decay_all[:, None, None] * carry + state_add, "seq", 1)

    state_in = lax.fori_loop(0, lax.axis_size("seq") - 1, advance, jnp.zeros_like(state_add))
    carried_in = jnp.einsum("tn,hpn->thp", c_proj.astype(jnp.float32), state_in, precision=PRECISE)
    y_full = (
        y_part
        + carried[:, :, None] * carried_in
        + d_skip[0][None, :, None] * x_heads.astype(jnp.float32)
    )
    entering = seg_ends[0] + jnp.exp(end_zero)[:, None, None] * state_in
    has_start = jnp.where(started > 0, 1.0, 0.0).astype(jnp.float32).reshape(1)

    def retreat(turn, carry):
        send_mark = jnp.maximum(has_start, carry[0])
        send_value = jnp.where(has_start[0] > 0.5, entering, carry[1])
        return from_behind((send_mark, send_value), "seq", -1)

    mark_right, value_right = lax.fori_loop(
        0, lax.axis_size("seq") - 1, retreat, (jnp.zeros_like(has_start), jnp.zeros_like(entering))
    )
    tail_state = jnp.where(mark_right[0] > 0.5, value_right, state_add)
    slot_ids = jnp.arange(1, init_vals.shape[0] + 1, dtype=jnp.int32)
    finals = jnp.where(
        (slot_ids < started)[:, None, None, None],
        seg_ends[1:],
        jnp.where((slot_ids == started)[:, None, None, None], tail_state[None], 0.0),
    )
    gated = y_full.reshape(rows_here, channels) * jax.nn.silu(z_gate.astype(jnp.float32))
    partial_sq = jnp.sum(gated * gated, axis=-1)
    total_sq = lax.psum(partial_sq, "row")
    mean_sq = total_sq / (channels * lax.axis_size("row"))
    gated_out = (gated * lax.rsqrt(mean_sq + EPSILON)[:, None] * norm_gain[0][None, :]).astype(
        jnp.bfloat16
    )
    return (gated_out.reshape(rows_here, 1, channels), finals[:, None])


def solution(mesh):
    placed = (
        P(("seq", "row"), "col"),
        P("col", None, "row"),
        P("col", None, "row"),
        P("col", None, None),
        P("col", None, "row"),
        P(None, "col", "row"),
        P(None, "col", None),
        P("col", "row"),
        P("col", None),
        P("col", "row"),
        P("col", "row"),
        P("col", "row"),
        P("col", "row"),
        P("seq"),
        P("seq", "col", "row", None, None),
        P("seq", None, "col", "row"),
        P("seq", None, "col", None),
    )
    return jax.shard_map(
        shards,
        mesh=mesh,
        in_specs=placed,
        out_specs=(P("seq", "col", "row"), P("seq", "col", "row", None, None)),
        check_vma=False,
    )
```

profile of v0, /device:TPU:2, one launch (start us, length us, event | category | flops | bytes accessed | tf_op | source)
XLA Modules:
  0.0 911.3 jit_solution(1194930417800551898)
XLA Ops:
  8.0 19.2 %all-gather.2.cloned.1.call-done = bf16[512,1024]{1,0:T(8,128)(2,1)} async-done(((bf16[256,1024]{1,0:T(8,128)(2,1)}), bf16[512,1024]{1,0:T(8,128)(2,1)}) %all-gather.2.cloned.1.call-update) | async-done | bytes 1048592 | tf_op jit(solution)/shard_map/all_gather | solution.py:120
  63.5 80.7 %reduce-scatter.2.cloned.1.call-done = f32[1,512,1288]{1,2,0:T(8,128)} async-done(((f32[4,512,1288]{1,2,0:T(8,128)}), f32[1,512,1288]{1,2,0:T(8,128)}) %reduce-scatter.2.cloned.1.call-update) | async-done | bytes 2637840 | tf_op jit(solution)/shard_map/reduce_scatter | solution.py:129
  180.1 348.6 %while.24 = (s32[]{:T(128)}, f32[8,64,128]{2,1,0:T(8,128)S(1)}, f32[8]{0:T(128)S(1)}, f32[8,64,128]{2,1,0:T(8,128)S(1)}, s32[]{:T(128)}) while((s32[]{:T(128)}, f32[8,64,128]{2,1,0:T(8,128)S(1)}, f32[8]{0:T(128)S(1)}, f32[8,64,128]{2,1,0:T(8,128)S(1)}, s32[]{:T(128)}) %tuple.64), condition=%wide.region_15.16_spmd, body=%wide.region_14.15_spmd.sunk | while | flops 131074 | bytes 1835141 | solution.py:182
  192.9 8.4 collective-permute-done
  203.3 8.4 collective-permute-done
  224.3 8.9 collective-permute-done
  235.2 10.0 %collective-permute-done = f32[8,64,128]{2,1,0:T(8,128)S(1)} collective-permute-done((f32[8,64,128]{2,1,0:T(8,128)S(1)}, f32[8,64,128]{2,1,0:T(8,128)S(1)}, u32[]{:S(2)}, u32[]{:S(2)}) %collective-permute-start) | collective-permute-done | bytes 262176 | tf_op jit(solution)/shard_map/while/body/eval_jaxpr/ppermute | solution.py:17
  247.2 11.2 %collective-permute-done = f32[8,64,128]{2,1,0:T(8,128)S(1)} collective-permute-done((f32[8,64,128]{2,1,0:T(8,128)S(1)}, f32[8,64,128]{2,1,0:T(8,128)S(1)}, u32[]{:S(2)}, u32[]{:S(2)}) %collective-permute-start) | collective-permute-done | bytes 262176 | tf_op jit(solution)/shard_map/while/body/eval_jaxpr/ppermute | solution.py:17
  260.4 10.4 %collective-permute-done = f32[8,64,128]{2,1,0:T(8,128)S(1)} collective-permute-done((f32[8,64,128]{2,1,0:T(8,128)S(1)}, f32[8,64,128]{2,1,0:T(8,128)S(1)}, u32[]{:S(2)}, u32[]{:S(2)}) %collective-permute-start) | collective-permute-done | bytes 262176 | tf_op jit(solution)/shard_map/while/body/eval_jaxpr/ppermute | solution.py:17
  272.9 9.5 %collective-permute-done = f32[8,64,128]{2,1,0:T(8,128)S(1)} collective-permute-done((f32[8,64,128]{2,1,0:T(8,128)S(1)}, f32[8,64,128]{2,1,0:T(8,128)S(1)}, u32[]{:S(2)}, u32[]{:S(2)}) %collective-permute-start) | collective-permute-done | bytes 262176 | tf_op jit(solution)/shard_map/while/body/eval_jaxpr/ppermute | solution.py:17
  284.4 8.7 collective-permute-done
  326.6 8.8 collective-permute-done
  337.4 9.9 %collective-permute-done = f32[8,64,128]{2,1,0:T(8,128)S(1)} collective-permute-done((f32[8,64,128]{2,1,0:T(8,128)S(1)}, f32[8,64,128]{2,1,0:T(8,128)S(1)}, u32[]{:S(2)}, u32[]{:S(2)}) %collective-permute-start) | collective-permute-done | bytes 262176 | tf_op jit(solution)/shard_map/while/body/eval_jaxpr/ppermute | solution.py:17
  349.4 11.1 %collective-permute-done = f32[8,64,128]{2,1,0:T(8,128)S(1)} collective-permute-done((f32[8,64,128]{2,1,0:T(8,128)S(1)}, f32[8,64,128]{2,1,0:T(8,128)S(1)}, u32[]{:S(2)}, u32[]{:S(2)}) %collective-permute-start) | collective-permute-done | bytes 262176 | tf_op jit(solution)/shard_map/while/body/eval_jaxpr/ppermute | solution.py:17
  362.5 10.4 %collective-permute-done = f32[8,64,128]{2,1,0:T(8,128)S(1)} collective-permute-done((f32[8,64,128]{2,1,0:T(8,128)S(1)}, f32[8,64,128]{2,1,0:T(8,128)S(1)}, u32[]{:S(2)}, u32[]{:S(2)}) %collective-permute-start) | collective-permute-done | bytes 262176 | tf_op jit(solution)/shard_map/while/body/eval_jaxpr/ppermute | solution.py:17
  374.9 9.5 %collective-permute-done = f32[8,64,128]{2,1,0:T(8,128)S(1)} collective-permute-done((f32[8,64,128]{2,1,0:T(8,128)S(1)}, f32[8,64,128]{2,1,0:T(8,128)S(1)}, u32[]{:S(2)}, u32[]{:S(2)}) %collective-permute-start) | collective-permute-done | bytes 262176 | tf_op jit(solution)/shard_map/while/body/eval_jaxpr/ppermute | solution.py:17
  386.5 8.7 collective-permute-done
  428.6 8.8 collective-permute-done
  439.4 9.9 %collective-permute-done = f32[8,64,128]{2,1,0:T(8,128)S(1)} collective-permute-done((f32[8,64,128]{2,1,0:T(8,128)S(1)}, f32[8,64,128]{2,1,0:T(8,128)S(1)}, u32[]{:S(2)}, u32[]{:S(2)}) %collective-permute-start) | collective-permute-done | bytes 262176 | tf_op jit(solution)/shard_map/while/body/eval_jaxpr/ppermute | solution.py:17
  451.4 11.1 %collective-permute-done = f32[8,64,128]{2,1,0:T(8,128)S(1)} collective-permute-done((f32[8,64,128]{2,1,0:T(8,128)S(1)}, f32[8,64,128]{2,1,0:T(8,128)S(1)}, u32[]{:S(2)}, u32[]{:S(2)}) %collective-permute-start) | collective-permute-done | bytes 262176 | tf_op jit(solution)/shard_map/while/body/eval_jaxpr/ppermute | solution.py:17
  464.5 10.4 %collective-permute-done = f32[8,64,128]{2,1,0:T(8,128)S(1)} collective-permute-done((f32[8,64,128]{2,1,0:T(8,128)S(1)}, f32[8,64,128]{2,1,0:T(8,128)S(1)}, u32[]{:S(2)}, u32[]{:S(2)}) %collective-permute-start) | collective-permute-done | bytes 262176 | tf_op jit(solution)/shard_map/while/body/eval_jaxpr/ppermute | solution.py:17
  477.0 9.5 %collective-permute-done = f32[8,64,128]{2,1,0:T(8,128)S(1)} collective-permute-done((f32[8,64,128]{2,1,0:T(8,128)S(1)}, f32[8,64,128]{2,1,0:T(8,128)S(1)}, u32[]{:S(2)}, u32[]{:S(2)}) %collective-permute-start) | collective-permute-done | bytes 262176 | tf_op jit(solution)/shard_map/while/body/eval_jaxpr/ppermute | solution.py:17
  488.5 8.7 collective-permute-done
  536.0 367.4 %while.25 = (s32[]{:T(128)}, f32[1]{0:T(128)}, f32[8,64,128]{2,1,0:T(8,128)S(1)}, f32[1]{0:T(128)}, pred[]{:T(512)}, /*index=5*/f32[8,64,128]{2,1,0:T(8,128)S(1)}, s32[]{:T(128)}) while((s32[]{:T(128)}, f32[1]{0:T(128)}, f32[8,64,128]{2,1,0:T(8,128)S(1)}, f32[1]{0:T(128)}, pred[]{:T(512)}, /*index=5*/f32[8,64,128]{2,1,0:T(8,128)S(1)}, ...), condition=%wide.region_19.20_spmd, body=%wide.region_18.19_spmd.sunk | while | flops 65539 | bytes 1835194 | solution.py:197
  (428 shorter events, 580.4 us)
Async XLA Ops:
  7.2 20.0 %all-gather.2.cloned.1.call-start = ((), (), s32[]{:S(2)}) async-start(), calls=%async_computation.1 | async-start | bytes 1572864 | tf_op jit(solution)/shard_map/all_gather | solution.py:120
  7.9 136.3 %reduce-scatter.2.cloned.1.call-start = ((), (), s32[]{:S(2)}) async-start(), calls=%async_computation.2 | async-start | bytes 13189120 | tf_op jit(solution)/shard_map/reduce_scatter | solution.py:129
  149.4 16.6 %collective-permute-start.3 = (bf16[3,512]{0,1:T(8,128)(2,1)}, bf16[3,512]{0,1:T(8,128)(2,1)}, u32[]{:S(2)}, u32[]{:S(2)}) collective-permute-start(bf16[3,512]{0,1:T(8,128)(2,1)} %slice_select_fusion), channel_id=1, source_target_pairs={{0,8},{8,16},{16,24},{24,32},{32,40},{40,48},{48,56},{56,64},{64,7... | collective-permute-start | bytes 9224 | tf_op jit(solution)/shard_map/ppermute | solution.py:17
  233.3 12.0 %collective-permute-start = (f32[8,64,128]{2,1,0:T(8,128)S(1)}, f32[8,64,128]{2,1,0:T(8,128)S(1)}, u32[]{:S(2)}, u32[]{:S(2)}) collective-permute-start(f32[8,64,128]{2,1,0:T(8,128)S(1)} %multiply_add_fusion.2), channel_id=1, source_target_pairs={{0,8},{8,16},{16,24},{24,32},{32,40},{40,48},{48,56},{56,64},{64,7... | collective-permute-start | bytes 786440 | tf_op jit(solution)/shard_map/while/body/eval_jaxpr/ppermute | solution.py:17
  245.3 13.1 %collective-permute-start = (f32[8,64,128]{2,1,0:T(8,128)S(1)}, f32[8,64,128]{2,1,0:T(8,128)S(1)}, u32[]{:S(2)}, u32[]{:S(2)}) collective-permute-start(f32[8,64,128]{2,1,0:T(8,128)S(1)} %multiply_add_fusion.2), channel_id=1, source_target_pairs={{0,8},{8,16},{16,24},{24,32},{32,40},{40,48},{48,56},{56,64},{64,7... | collective-permute-start | bytes 786440 | tf_op jit(solution)/shard_map/while/body/eval_jaxpr/ppermute | solution.py:17
  258.5 12.3 %collective-permute-start = (f32[8,64,128]{2,1,0:T(8,128)S(1)}, f32[8,64,128]{2,1,0:T(8,128)S(1)}, u32[]{:S(2)}, u32[]{:S(2)}) collective-permute-start(f32[8,64,128]{2,1,0:T(8,128)S(1)} %multiply_add_fusion.2), channel_id=1, source_target_pairs={{0,8},{8,16},{16,24},{24,32},{32,40},{40,48},{48,56},{56,64},{64,7... | collective-permute-start | bytes 786440 | tf_op jit(solution)/shard_map/while/body/eval_jaxpr/ppermute | solution.py:17
  335.5 11.9 %collective-permute-start = (f32[8,64,128]{2,1,0:T(8,128)S(1)}, f32[8,64,128]{2,1,0:T(8,128)S(1)}, u32[]{:S(2)}, u32[]{:S(2)}) collective-permute-start(f32[8,64,128]{2,1,0:T(8,128)S(1)} %multiply_add_fusion.2), channel_id=1, source_target_pairs={{0,8},{8,16},{16,24},{24,32},{32,40},{40,48},{48,56},{56,64},{64,7... | collective-permute-start | bytes 786440 | tf_op jit(solution)/shard_map/while/body/eval_jaxpr/ppermute | solution.py:17
  347.4 13.0 %collective-permute-start = (f32[8,64,128]{2,1,0:T(8,128)S(1)}, f32[8,64,128]{2,1,0:T(8,128)S(1)}, u32[]{:S(2)}, u32[]{:S(2)}) collective-permute-start(f32[8,64,128]{2,1,0:T(8,128)S(1)} %multiply_add_fusion.2), channel_id=1, source_target_pairs={{0,8},{8,16},{16,24},{24,32},{32,40},{40,48},{48,56},{56,64},{64,7... | collective-permute-start | bytes 786440 | tf_op jit(solution)/shard_map/while/body/eval_jaxpr/ppermute | solution.py:17
  360.6 12.3 %collective-permute-start = (f32[8,64,128]{2,1,0:T(8,128)S(1)}, f32[8,64,128]{2,1,0:T(8,128)S(1)}, u32[]{:S(2)}, u32[]{:S(2)}) collective-permute-start(f32[8,64,128]{2,1,0:T(8,128)S(1)} %multiply_add_fusion.2), channel_id=1, source_target_pairs={{0,8},{8,16},{16,24},{24,32},{32,40},{40,48},{48,56},{56,64},{64,7... | collective-permute-start | bytes 786440 | tf_op jit(solution)/shard_map/while/body/eval_jaxpr/ppermute | solution.py:17
  437.5 11.9 %collective-permute-start = (f32[8,64,128]{2,1,0:T(8,128)S(1)}, f32[8,64,128]{2,1,0:T(8,128)S(1)}, u32[]{:S(2)}, u32[]{:S(2)}) collective-permute-start(f32[8,64,128]{2,1,0:T(8,128)S(1)} %multiply_add_fusion.2), channel_id=1, source_target_pairs={{0,8},{8,16},{16,24},{24,32},{32,40},{40,48},{48,56},{56,64},{64,7... | collective-permute-start | bytes 786440 | tf_op jit(solution)/shard_map/while/body/eval_jaxpr/ppermute | solution.py:17
  449.5 13.0 %collective-permute-start = (f32[8,64,128]{2,1,0:T(8,128)S(1)}, f32[8,64,128]{2,1,0:T(8,128)S(1)}, u32[]{:S(2)}, u32[]{:S(2)}) collective-permute-start(f32[8,64,128]{2,1,0:T(8,128)S(1)} %multiply_add_fusion.2), channel_id=1, source_target_pairs={{0,8},{8,16},{16,24},{24,32},{32,40},{40,48},{48,56},{56,64},{64,7... | collective-permute-start | bytes 786440 | tf_op jit(solution)/shard_map/while/body/eval_jaxpr/ppermute | solution.py:17
  462.6 12.3 %collective-permute-start = (f32[8,64,128]{2,1,0:T(8,128)S(1)}, f32[8,64,128]{2,1,0:T(8,128)S(1)}, u32[]{:S(2)}, u32[]{:S(2)}) collective-permute-start(f32[8,64,128]{2,1,0:T(8,128)S(1)} %multiply_add_fusion.2), channel_id=1, source_target_pairs={{0,8},{8,16},{16,24},{24,32},{32,40},{40,48},{48,56},{56,64},{64,7... | collective-permute-start | bytes 786440 | tf_op jit(solution)/shard_map/while/body/eval_jaxpr/ppermute | solution.py:17
  557.7 11.8 %collective-permute-start.2 = (f32[8,64,128]{2,1,0:T(8,128)S(1)}, f32[8,64,128]{2,1,0:T(8,128)S(1)}, u32[]{:S(2)}, u32[]{:S(2)}) collective-permute-start(f32[8,64,128]{2,1,0:T(8,128)S(1)} %broadcast_select_fusion.4), channel_id=1, source_target_pairs={{8,0},{16,8},{24,16},{32,24},{40,32},{48,40},{56,48},{64,56},{72,6... | collective-permute-start | bytes 786440 | tf_op jit(solution)/shard_map/while/body/eval_jaxpr/ppermute | solution.py:17
  626.3 12.3 %collective-permute-start.2 = (f32[8,64,128]{2,1,0:T(8,128)S(1)}, f32[8,64,128]{2,1,0:T(8,128)S(1)}, u32[]{:S(2)}, u32[]{:S(2)}) collective-permute-start(f32[8,64,128]{2,1,0:T(8,128)S(1)} %broadcast_select_fusion.4), channel_id=1, source_target_pairs={{8,0},{16,8},{24,16},{32,24},{40,32},{48,40},{56,48},{64,56},{72,6... | collective-permute-start | bytes 786440 | tf_op jit(solution)/shard_map/while/body/eval_jaxpr/ppermute | solution.py:17
  639.3 12.5 %collective-permute-start.2 = (f32[8,64,128]{2,1,0:T(8,128)S(1)}, f32[8,64,128]{2,1,0:T(8,128)S(1)}, u32[]{:S(2)}, u32[]{:S(2)}) collective-permute-start(f32[8,64,128]{2,1,0:T(8,128)S(1)} %broadcast_select_fusion.4), channel_id=1, source_target_pairs={{8,0},{16,8},{24,16},{32,24},{40,32},{48,40},{56,48},{64,56},{72,6... | collective-permute-start | bytes 786440 | tf_op jit(solution)/shard_map/while/body/eval_jaxpr/ppermute | solution.py:17
  652.6 12.1 %collective-permute-start.2 = (f32[8,64,128]{2,1,0:T(8,128)S(1)}, f32[8,64,128]{2,1,0:T(8,128)S(1)}, u32[]{:S(2)}, u32[]{:S(2)}) collective-permute-start(f32[8,64,128]{2,1,0:T(8,128)S(1)} %broadcast_select_fusion.4), channel_id=1, source_target_pairs={{8,0},{16,8},{24,16},{32,24},{40,32},{48,40},{56,48},{64,56},{72,6... | collective-permute-start | bytes 786440 | tf_op jit(solution)/shard_map/while/body/eval_jaxpr/ppermute | solution.py:17
  665.4 11.6 %collective-permute-start.2 = (f32[8,64,128]{2,1,0:T(8,128)S(1)}, f32[8,64,128]{2,1,0:T(8,128)S(1)}, u32[]{:S(2)}, u32[]{:S(2)}) collective-permute-start(f32[8,64,128]{2,1,0:T(8,128)S(1)} %broadcast_select_fusion.4), channel_id=1, source_target_pairs={{8,0},{16,8},{24,16},{32,24},{40,32},{48,40},{56,48},{64,56},{72,6... | collective-permute-start | bytes 786440 | tf_op jit(solution)/shard_map/while/body/eval_jaxpr/ppermute | solution.py:17
  733.8 12.8 %collective-permute-start.2 = (f32[8,64,128]{2,1,0:T(8,128)S(1)}, f32[8,64,128]{2,1,0:T(8,128)S(1)}, u32[]{:S(2)}, u32[]{:S(2)}) collective-permute-start(f32[8,64,128]{2,1,0:T(8,128)S(1)} %broadcast_select_fusion.4), channel_id=1, source_target_pairs={{8,0},{16,8},{24,16},{32,24},{40,32},{48,40},{56,48},{64,56},{72,6... | collective-permute-start | bytes 786440 | tf_op jit(solution)/shard_map/while/body/eval_jaxpr/ppermute | solution.py:17
  747.2 12.4 %collective-permute-start.2 = (f32[8,64,128]{2,1,0:T(8,128)S(1)}, f32[8,64,128]{2,1,0:T(8,128)S(1)}, u32[]{:S(2)}, u32[]{:S(2)}) collective-permute-start(f32[8,64,128]{2,1,0:T(8,128)S(1)} %broadcast_select_fusion.4), channel_id=1, source_target_pairs={{8,0},{16,8},{24,16},{32,24},{40,32},{48,40},{56,48},{64,56},{72,6... | collective-permute-start | bytes 786440 | tf_op jit(solution)/shard_map/while/body/eval_jaxpr/ppermute | solution.py:17
  760.4 12.1 %collective-permute-start.2 = (f32[8,64,128]{2,1,0:T(8,128)S(1)}, f32[8,64,128]{2,1,0:T(8,128)S(1)}, u32[]{:S(2)}, u32[]{:S(2)}) collective-permute-start(f32[8,64,128]{2,1,0:T(8,128)S(1)} %broadcast_select_fusion.4), channel_id=1, source_target_pairs={{8,0},{16,8},{24,16},{32,24},{40,32},{48,40},{56,48},{64,56},{72,6... | collective-permute-start | bytes 786440 | tf_op jit(solution)/shard_map/while/body/eval_jaxpr/ppermute | solution.py:17
  773.2 11.5 %collective-permute-start.2 = (f32[8,64,128]{2,1,0:T(8,128)S(1)}, f32[8,64,128]{2,1,0:T(8,128)S(1)}, u32[]{:S(2)}, u32[]{:S(2)}) collective-permute-start(f32[8,64,128]{2,1,0:T(8,128)S(1)} %broadcast_select_fusion.4), channel_id=1, source_target_pairs={{8,0},{16,8},{24,16},{32,24},{40,32},{48,40},{56,48},{64,56},{72,6... | collective-permute-start | bytes 786440 | tf_op jit(solution)/shard_map/while/body/eval_jaxpr/ppermute | solution.py:17
  841.5 13.0 %collective-permute-start.2 = (f32[8,64,128]{2,1,0:T(8,128)S(1)}, f32[8,64,128]{2,1,0:T(8,128)S(1)}, u32[]{:S(2)}, u32[]{:S(2)}) collective-permute-start(f32[8,64,128]{2,1,0:T(8,128)S(1)} %broadcast_select_fusion.4), channel_id=1, source_target_pairs={{8,0},{16,8},{24,16},{32,24},{40,32},{48,40},{56,48},{64,56},{72,6... | collective-permute-start | bytes 786440 | tf_op jit(solution)/shard_map/while/body/eval_jaxpr/ppermute | solution.py:17
  855.1 12.4 %collective-permute-start.2 = (f32[8,64,128]{2,1,0:T(8,128)S(1)}, f32[8,64,128]{2,1,0:T(8,128)S(1)}, u32[]{:S(2)}, u32[]{:S(2)}) collective-permute-start(f32[8,64,128]{2,1,0:T(8,128)S(1)} %broadcast_select_fusion.4), channel_id=1, source_target_pairs={{8,0},{16,8},{24,16},{32,24},{40,32},{48,40},{56,48},{64,56},{72,6... | collective-permute-start | bytes 786440 | tf_op jit(solution)/shard_map/while/body/eval_jaxpr/ppermute | solution.py:17
  868.2 12.1 %collective-permute-start.2 = (f32[8,64,128]{2,1,0:T(8,128)S(1)}, f32[8,64,128]{2,1,0:T(8,128)S(1)}, u32[]{:S(2)}, u32[]{:S(2)}) collective-permute-start(f32[8,64,128]{2,1,0:T(8,128)S(1)} %broadcast_select_fusion.4), channel_id=1, source_target_pairs={{8,0},{16,8},{24,16},{32,24},{40,32},{48,40},{56,48},{64,56},{72,6... | collective-permute-start | bytes 786440 | tf_op jit(solution)/shard_map/while/body/eval_jaxpr/ppermute | solution.py:17
  (114 other events, 3150.4 us)
Sparse Core Ops, SparseCore 0:
  9.8 17.3 all-gather.1
  42.3 101.9 reduce-scatter.1
where the time goes:
time: 915 us; the launch traced here: 911 us
  waiting for transfers between devices  421 us (46%)
  starting transfers between devices  379 us (41%)
  matrix products  31.6 us (3%)
  other arithmetic  27.6 us (3%)
  loops' own time  20.9 us (2%)
  between operations  17.6 us (2%)
  local copies, waits for them, and re-layouts  11 us (1%)
    ppermute x95, starting transfers between devices, from_behind(): lax.ppermute(value, axis, [(source, source + steps) for source in range(f...  379 us
    ppermute x95, waiting for transfers between devices, from_behind(): lax.ppermute(value, axis, [(source, source + steps) for source in range(f...  320 us
    reduce_scatter x1, waiting for transfers between devices, shards(): lax.psum_scatter(jnp.concatenate(pieces, axis=2), 'col', scatter_dimensio...  80.7 us
    another operation x1, loops' own time, shards(): lax.fori_loop(0, lax.axis_size('seq') - 1, retreat, (jnp.zeros_like(has_s...  20.4 us
    all_gather x1, waiting for transfers between devices, shards(): tokens = lax.all_gather(hidden, 'row', axis=0, tiled=True)  19.2 us
  transfers between devices with their start and end apart: 97, of which 59 were waited for; matrix products, arithmetic and copies ran while one was open for 3% of the time, Pallas kernels for 0%

commit v1 on v0

--- a/solution.py
+++ b/solution.py
@@ -176,28 +176,67 @@
         x_heads, b_proj, c_proj, dt_vals, flag_vals, init_vals, decay_rate[0]
     )
 
-    def advance(turn, carry):
-        return from_behind(decay_all[:, None, None] * carry + state_add, "seq", 1)
-
-    state_in = lax.fori_loop(0, lax.axis_size("seq") - 1, advance, jnp.zeros_like(state_add))
+    seq_count = lax.axis_size("seq")
+    seq_at = lax.axis_index("seq")
+    heads_n, p_n, n_n = state_add.shape
+    ones = jnp.ones((heads_n,), jnp.float32)
+    zeros_state = jnp.zeros_like(state_add)
+    has_start = jnp.where(started > 0, 1.0, 0.0).astype(jnp.float32)
+
+    def pack(decay, state, mark):
+        aux = jnp.concatenate(
+            [
+                jnp.broadcast_to(decay[:, None], (heads_n, n_n // 2)),
+                jnp.broadcast_to(mark, (heads_n, n_n - n_n // 2)),
+            ],
+            axis=1,
+        )
+        return jnp.concatenate([state, aux[:, None, :]], axis=1)
+
+    def unpack(packed):
+        return packed[:, p_n, 0], packed[:, :p_n], packed[0, p_n, n_n - 1]
+
+    fwd_in = (decay_all * ones, state_add)
+    fwd_ex = (ones, zeros_state)
+    bwd_in = (jnp.exp(end_zero), seg_ends[0], has_start)
+    bwd_ex = (ones, zeros_state, jnp.zeros((), jnp.float32))
+    shift = 1
+    while shift < seq_count:
+        last = 2 * shift >= seq_count
+        got_f = from_behind(pack(fwd_in[0], fwd_in[1], 0.0), "seq", shift)
+        got_b = from_behind(pack(*bwd_in), "seq", -shift)
+        early_a, early_b, _ = unpack(got_f)
+        late_a, late_b, late_m = unpack(got_b)
+        late_ok = seq_at + shift < seq_count
+        fwd_ex = (
+            fwd_ex[0] * early_a,
+            fwd_ex[0][:, None, None] * early_b + fwd_ex[1],
+        )
+
+        def near_far(near, far_a, far_b, far_m):
+            keep = (near[2] > 0.5) | jnp.logical_not(late_ok)
+            return (
+                jnp.where(keep, near[0], far_a * near[0]),
+                jnp.where(keep, near[1], far_a[:, None, None] * near[1] + far_b),
+                jnp.where(keep, near[2], far_m),
+            )
+
+        bwd_ex = near_far(bwd_ex, late_a, late_b, late_m)
+        if not last:
+            fwd_in = (
+                fwd_in[0] * early_a,
+                fwd_in[0][:, None, None] * early_b + fwd_in[1],
+            )
+            bwd_in = near_far(bwd_in, late_a, late_b, late_m)
+        shift *= 2
+    state_in = fwd_ex[1]
     carried_in = jnp.einsum("tn,hpn->thp", c_proj.astype(jnp.float32), state_in, precision=PRECISE)
     y_full = (
         y_part
         + carried[:, :, None] * carried_in
         + d_skip[0][None, :, None] * x_heads.astype(jnp.float32)
     )
-    entering = seg_ends[0] + jnp.exp(end_zero)[:, None, None] * state_in
-    has_start = jnp.where(started > 0, 1.0, 0.0).astype(jnp.float32).reshape(1)
-
-    def retreat(turn, carry):
-        send_mark = jnp.maximum(has_start, carry[0])
-        send_value = jnp.where(has_start[0] > 0.5, entering, carry[1])
-        return from_behind((send_mark, send_value), "seq", -1)
-
-    mark_right, value_right = lax.fori_loop(
-        0, lax.axis_size("seq") - 1, retreat, (jnp.zeros_like(has_start), jnp.zeros_like(entering))
-    )
-    tail_state = jnp.where(mark_right[0] > 0.5, value_right, state_add)
+    tail_state = bwd_ex[0][:, None, None] * state_add + bwd_ex[1]
     slot_ids = jnp.arange(1, init_vals.shape[0] + 1, dtype=jnp.int32)
     finals = jnp.where(
         (slot_ids < started)[:, None, None, None],

time: 915 us -> 340 us (0.37)
  the two profiles are of different devices: /device:TPU:2 before, /device:TPU:101 now
where the time goes in v1:
time: 340 us; the launch traced here: 338 us
  waiting for transfers between devices  164 us (48%)
  other arithmetic  51.4 us (15%)
  starting transfers between devices  42.1 us (12%)
  matrix products  31.3 us (9%)
  between operations  22.6 us (7%)
  local copies, waits for them, and re-layouts  22 us (6%)
  blocking collectives  4.56 us (1%)
    reduce_scatter x1, waiting for transfers between devices, shards(): lax.psum_scatter(jnp.concatenate(pieces, axis=2), 'col', scatter_dimensio...  74.4 us
    ppermute x12, waiting for transfers between devices, from_behind(): lax.ppermute(value, axis, [(source, source + steps) for source in range(f...  70.8 us
    ppermute x12, starting transfers between devices, from_behind(): lax.ppermute(value, axis, [(source, source + steps) for source in range(f...  42 us
    all_gather x1, waiting for transfers between devices, shards(): tokens = lax.all_gather(hidden, 'row', axis=0, tiled=True)  18.5 us
    dot_general x4, matrix products, shards(): jnp.einsum('td,dgc->gtc', tokens, weight, preferred_element_type=jnp.floa...  10.4 us
    dot_general x6, matrix products, convolve(): from_edge = jnp.dot(picker, table, preferred_element_type=jnp.float32)  7.59 us
    slice x9, local copies, waits for them, and re-layouts, unpack(): return (packed[:, p_n, 0], packed[:, :p_n], packed[0, p_n, n_n - 1])  7.41 us
    dot_general x1, matrix products, local_terms(): jnp.einsum('hij,jhp->ihp', mixing, x_vals.astype(jnp.float32), precision=...  6.86 us
  transfers between devices with their start and end apart: 14, of which 9 were waited for; matrix products, arithmetic and copies ran while one was open for 18% of the time, Pallas kernels for 0%

profile of v1, /device:TPU:101, one launch (start us, length us, event | category | flops | bytes accessed | tf_op | source)
XLA Modules:
  0.0 338.3 jit_solution(753345638524201628)
XLA Ops:
  8.0 18.5 %all-gather.2.cloned.1.call-done = bf16[512,1024]{1,0:T(8,128)(2,1)} async-done(((bf16[256,1024]{1,0:T(8,128)(2,1)}), bf16[512,1024]{1,0:T(8,128)(2,1)}) %all-gather.2.cloned.1.call-update) | async-done | bytes 1048592 | tf_op jit(solution)/shard_map/all_gather | solution.py:120
  28.1 3.3 fusion.30
  31.6 2.7 fusion.23
  34.3 2.7 fusion.20
  37.0 4.4 %pad_maximum_fusion = f32[4,512,1288]{1,2,0:T(8,128)} fusion(f32[4,512,8]{1,2,0:T(8,128)S(1)} %convolution_bitcast_fusion, f32[4,512,256]{1,2,0:T(8,128)S(1)} %fusion.30, f32[4,512,512]{1,2,0:T(8,128)S(1)} %fusion.23, f32[4,512,512]{1,2,0:T(8,128)S(1)} %fusion.20), kind=kLoop, calls=%fused_computation.5 | loop fusion | flops 7913472 | bytes 21102592 | tf_op jit(solution)/shard_map/concatenate | solution.py:130
  68.7 74.4 %reduce-scatter.2.cloned.1.call-done = f32[1,512,1288]{1,2,0:T(8,128)} async-done(((f32[4,512,1288]{1,2,0:T(8,128)}), f32[1,512,1288]{1,2,0:T(8,128)}) %reduce-scatter.2.cloned.1.call-update) | async-done | bytes 2637840 | tf_op jit(solution)/shard_map/reduce_scatter | solution.py:129
  146.6 4.4 %collective-permute-start = (bf16[3,512]{0,1:T(8,128)(2,1)}, bf16[3,512]{0,1:T(8,128)(2,1)}, u32[]{:S(2)}, u32[]{:S(2)}) collective-permute-start(bf16[3,512]{0,1:T(8,128)(2,1)} %slice_select_fusion), channel_id=1, source_target_pairs={{0,8},{8,16},{16,24},{24,32},{32,40},{40,48},{48,56},{56,64},{64,7... | collective-permute-start | bytes 9224 | tf_op jit(solution)/shard_map/ppermute | solution.py:17
  151.7 2.5 collective-permute-start.1
  164.3 2.5 multiply_convert_fusion.1
  167.0 2.2 fusion.11
  169.9 3.0 collective-permute-start.7
  174.6 5.7 %collective-permute-done.7 = f32[8,65,128]{2,1,0:T(8,128)S(1)} collective-permute-done((f32[8,65,128]{2,1,0:T(8,128)S(1)}, f32[8,65,128]{2,1,0:T(8,128)S(1)}, u32[]{:S(2)}, u32[]{:S(2)}) %collective-permute-start.7) | collective-permute-done | bytes 266272 | tf_op jit(solution)/shard_map/ppermute | solution.py:17
  188.8 12.3 %collective-permute-done.8 = f32[8,65,128]{2,1,0:T(8,128)} collective-permute-done((f32[8,65,128]{2,1,0:T(8,128)}, f32[8,65,128]{2,1,0:T(8,128)}, u32[]{:S(2)}, u32[]{:S(2)}) %collective-permute-start.8) | collective-permute-done | bytes 266272 | tf_op jit(solution)/shard_map/ppermute | solution.py:17
  206.6 4.4 %collective-permute-start.9 = (f32[8,65,128]{2,1,0:T(8,128)}, f32[8,65,128]{2,1,0:T(8,128)}, u32[]{:S(2)}, u32[]{:S(2)}) collective-permute-start(f32[8,65,128]{2,1,0:T(8,128)} %pad_maximum_fusion.9), channel_id=1, source_target_pairs={{32,0},{40,8},{48,16},{56,24},{64,32},{72,40},{80,48},{88,56},{96,... | collective-permute-start | bytes 798728 | tf_op jit(solution)/shard_map/ppermute | solution.py:17
  212.4 15.0 %collective-permute-done.9 = f32[8,65,128]{2,1,0:T(8,128)} collective-permute-done((f32[8,65,128]{2,1,0:T(8,128)}, f32[8,65,128]{2,1,0:T(8,128)}, u32[]{:S(2)}, u32[]{:S(2)}) %collective-permute-start.9) | collective-permute-done | bytes 266272 | tf_op jit(solution)/shard_map/ppermute | solution.py:17
  238.4 4.0 %collective-permute-done.10 = f32[8,65,128]{2,1,0:T(8,128)} collective-permute-done((f32[8,65,128]{2,1,0:T(8,128)}, f32[8,65,128]{2,1,0:T(8,128)}, u32[]{:S(2)}, u32[]{:S(2)}) %collective-permute-start.10) | collective-permute-done | bytes 266272 | tf_op jit(solution)/shard_map/ppermute | solution.py:17
  258.5 2.3 fusion.51
  260.8 13.4 %collective-permute-done.3 = f32[8,65,128]{2,1,0:T(8,128)S(1)} collective-permute-done((f32[8,65,128]{2,1,0:T(8,128)S(1)}, f32[8,65,128]{2,1,0:T(8,128)S(1)}, u32[]{:S(2)}, u32[]{:S(2)}) %collective-permute-start.3) | collective-permute-done | bytes 266272 | tf_op jit(solution)/shard_map/ppermute | solution.py:17
  275.4 3.2 collective-permute-start.4
  279.4 12.3 %collective-permute-done.4 = f32[8,65,128]{2,1,0:T(8,128)S(1)} collective-permute-done((f32[8,65,128]{2,1,0:T(8,128)S(1)}, f32[8,65,128]{2,1,0:T(8,128)S(1)}, u32[]{:S(2)}, u32[]{:S(2)}) %collective-permute-start.4) | collective-permute-done | bytes 266272 | tf_op jit(solution)/shard_map/ppermute | solution.py:17
  292.1 13.5 %collective-permute-start.5 = (f32[8,65,128]{2,1,0:T(8,128)S(1)}, f32[8,65,128]{2,1,0:T(8,128)S(1)}, u32[]{:S(2)}, u32[]{:S(2)}) collective-permute-start(f32[8,65,128]{2,1,0:T(8,128)S(1)} %pad_maximum_fusion.5), channel_id=1, source_target_pairs={{0,64},{8,72},{16,80},{24,88},{32,96},{40,104},{48,112},{56,120},{... | collective-permute-start | bytes 798728 | tf_op jit(solution)/shard_map/ppermute | solution.py:17
  305.8 6.9 %fusion.38 = f32[512,8,64]{0,2,1:T(8,128)S(1)} fusion(bf16[512,8,64]{0,2,1:T(8,128)(2,1)S(1)} %bitcast.150, f32[8,512]{1,0:T(8,128)S(1)} %copy-done.18, f32[512,512]{1,0:T(8,128)S(1)} %fusion.93, f32[8,512]{1,0:T(8,128)S(1)} %copy-done.20, pred[512,512]{1,0:T(8,128)(4,1)S(1)} %copy-done.8, f32[512,8,64]{0,2,1:T(8,128)S(1)} %bitcast.152, ...), kind=kOutput, calls=%fused_computation.38 | convolution fusion | flops 1621622784 | bytes 3981312 | tf_op jit(solution)/shard_map/hij,jhp->ihp/dot_general | solution.py:38
  315.4 8.0 %collective-permute-done.6 = f32[8,65,128]{2,1,0:T(8,128)S(1)} collective-permute-done((f32[8,65,128]{2,1,0:T(8,128)S(1)}, f32[8,65,128]{2,1,0:T(8,128)S(1)}, u32[]{:S(2)}, u32[]{:S(2)}) %collective-permute-start.6) | collective-permute-done | bytes 266272 | tf_op jit(solution)/shard_map/ppermute | solution.py:17
  325.5 4.6 %psum.7 = f32[512]{0:T(512)S(1)} all-reduce(f32[512]{0:T(512)S(1)} %multiply_reduce_fusion), channel_id=1, replica_groups=mesh['seq'=32,'row'=2,'col'=4] {'row'}, use_global_device_ids=true, to_apply=%region_15.16 | all-reduce | flops 512 | bytes 4096 | tf_op jit(solution)/shard_map/psum | solution.py:248
  (264 shorter events, 89.6 us)
Async XLA Ops:
  7.2 19.3 %all-gather.2.cloned.1.call-start = ((), (), s32[]{:S(2)}) async-start(), calls=%async_computation.1 | async-start | bytes 1572864 | tf_op jit(solution)/shard_map/all_gather | solution.py:120
  7.9 135.1 %reduce-scatter.2.cloned.1.call-start = ((), (), s32[]{:S(2)}) async-start(), calls=%async_computation.2 | async-start | bytes 13189120 | tf_op jit(solution)/shard_map/reduce_scatter | solution.py:129
  146.6 17.6 %collective-permute-start = (bf16[3,512]{0,1:T(8,128)(2,1)}, bf16[3,512]{0,1:T(8,128)(2,1)}, u32[]{:S(2)}, u32[]{:S(2)}) collective-permute-start(bf16[3,512]{0,1:T(8,128)(2,1)} %slice_select_fusion), channel_id=1, source_target_pairs={{0,8},{8,16},{16,24},{24,32},{32,40},{40,48},{48,56},{56,64},{64,7... | collective-permute-start | bytes 9224 | tf_op jit(solution)/shard_map/ppermute | solution.py:17
  151.7 10.5 %collective-permute-start.1 = (bf16[3,256]{0,1:T(8,128)(2,1)}, bf16[3,256]{0,1:T(8,128)(2,1)}, u32[]{:S(2)}, u32[]{:S(2)}) collective-permute-start(bf16[3,256]{0,1:T(8,128)(2,1)} %slice_select_fusion.1), channel_id=1, source_target_pairs={{0,8},{8,16},{16,24},{24,32},{32,40},{40,48},{48,56},{56,64},{64,7... | collective-permute-start | bytes 4616 | tf_op jit(solution)/shard_map/ppermute | solution.py:17
  169.9 10.4 %collective-permute-start.7 = (f32[8,65,128]{2,1,0:T(8,128)S(1)}, f32[8,65,128]{2,1,0:T(8,128)S(1)}, u32[]{:S(2)}, u32[]{:S(2)}) collective-permute-start(f32[8,65,128]{2,1,0:T(8,128)S(1)} %pad_maximum_fusion.7), channel_id=1, source_target_pairs={{8,0},{16,8},{24,16},{32,24},{40,32},{48,40},{56,48},{64,56},{72,6... | collective-permute-start | bytes 798728 | tf_op jit(solution)/shard_map/ppermute | solution.py:17
  183.1 18.0 %collective-permute-start.8 = (f32[8,65,128]{2,1,0:T(8,128)}, f32[8,65,128]{2,1,0:T(8,128)}, u32[]{:S(2)}, u32[]{:S(2)}) collective-permute-start(f32[8,65,128]{2,1,0:T(8,128)} %pad_maximum_fusion.8), channel_id=1, source_target_pairs={{16,0},{24,8},{32,16},{40,24},{48,32},{56,40},{64,48},{72,56},{80,... | collective-permute-start | bytes 798728 | tf_op jit(solution)/shard_map/ppermute | solution.py:17
  188.8 60.3 %copy-start.17 = (f32[8,4]{0,1:T(4,128)S(1)}, f32[8,4]{0,1:T(4,128)}, u32[]{:S(2)}) copy-start(f32[8,4]{0,1:T(4,128)} %copy-done.16) | copy-start | bytes 388
  204.8 29.8 %copy-start.40 = (pred[4]{0:T(512)(128)(4,1)S(1)}, pred[4]{0:T(512)(128)(4,1)}, u32[]{:S(2)}) copy-start(pred[4]{0:T(512)(128)(4,1)} %iota_compare_fusion.16) | copy-start | bytes 16
  204.8 46.9 %copy-start.27 = (f32[8]{0:T(128)S(1)}, f32[8]{0:T(128)}, u32[]{:S(2)}) copy-start(f32[8]{0:T(128)} %get-tuple-element.21) | copy-start | bytes 100
  204.8 49.9 %copy-start.34 = (f32[8]{0:T(128)S(1)}, f32[8]{0:T(128)}, u32[]{:S(2)}) copy-start(f32[8]{0:T(128)} %get-tuple-element.54) | copy-start | bytes 100
  206.6 20.8 %collective-permute-start.9 = (f32[8,65,128]{2,1,0:T(8,128)}, f32[8,65,128]{2,1,0:T(8,128)}, u32[]{:S(2)}, u32[]{:S(2)}) collective-permute-start(f32[8,65,128]{2,1,0:T(8,128)} %pad_maximum_fusion.9), channel_id=1, source_target_pairs={{32,0},{40,8},{48,16},{56,24},{64,32},{72,40},{80,48},{88,56},{96,... | collective-permute-start | bytes 798728 | tf_op jit(solution)/shard_map/ppermute | solution.py:17
  212.4 46.1 %copy-start.1 = (f32[3,1,8,64,128]{4,3,2,1,0:T(8,128)S(1)}, f32[3,1,8,64,128]{4,3,2,1,0:T(8,128)}, u32[]{:S(2)}) copy-start(f32[3,1,8,64,128]{4,3,2,1,0:T(8,128)} %param.31) | copy-start | bytes 2359300
  232.7 9.7 %collective-permute-start.10 = (f32[8,65,128]{2,1,0:T(8,128)}, f32[8,65,128]{2,1,0:T(8,128)}, u32[]{:S(2)}, u32[]{:S(2)}) collective-permute-start(f32[8,65,128]{2,1,0:T(8,128)} %pad_maximum_fusion.10), channel_id=1, source_target_pairs={{64,0},{72,8},{80,16},{88,24},{96,32},{104,40},{112,48},{120,56},{... | collective-permute-start | bytes 798728 | tf_op jit(solution)/shard_map/ppermute | solution.py:17
  236.5 13.8 %collective-permute-start.2 = (f32[8,65,128]{2,1,0:T(8,128)}, f32[8,65,128]{2,1,0:T(8,128)}, u32[]{:S(2)}, u32[]{:S(2)}) collective-permute-start(f32[8,65,128]{2,1,0:T(8,128)} %pad_maximum_fusion.2), channel_id=1, source_target_pairs={{0,8},{8,16},{16,24},{24,32},{32,40},{40,48},{48,56},{56,64},{64,7... | collective-permute-start | bytes 798728 | tf_op jit(solution)/shard_map/ppermute | solution.py:17
  247.0 6.6 %collective-permute-start.11 = (f32[8,65,128]{2,1,0:T(8,128)}, f32[8,65,128]{2,1,0:T(8,128)}, u32[]{:S(2)}, u32[]{:S(2)}) collective-permute-start(f32[8,65,128]{2,1,0:T(8,128)} %pad_maximum_fusion.11), channel_id=1, source_target_pairs={{128,0},{136,8},{144,16},{152,24},{160,32},{168,40},{176,48},{184,... | collective-permute-start | bytes 798728 | tf_op jit(solution)/shard_map/ppermute | solution.py:17
  256.4 17.8 %collective-permute-start.3 = (f32[8,65,128]{2,1,0:T(8,128)S(1)}, f32[8,65,128]{2,1,0:T(8,128)S(1)}, u32[]{:S(2)}, u32[]{:S(2)}) collective-permute-start(f32[8,65,128]{2,1,0:T(8,128)S(1)} %pad_maximum_fusion.3), channel_id=1, source_target_pairs={{0,16},{8,24},{16,32},{24,40},{32,48},{40,56},{48,64},{56,72},{64,... | collective-permute-start | bytes 798728 | tf_op jit(solution)/shard_map/ppermute | solution.py:17
  260.8 44.9 %copy-start.3 = (bf16[512,512]{0,1:T(8,128)(2,1)S(1)}, bf16[512,512]{0,1:T(8,128)(2,1)}, u32[]{:S(2)}) copy-start(bf16[512,512]{0,1:T(8,128)(2,1)} %copy-done.2) | copy-start | bytes 1572868
  260.8 44.9 %copy-start.8 = (pred[512,512]{1,0:T(8,128)(4,1)S(1)}, pred[512,512]{1,0:T(8,128)(4,1)}, u32[]{:S(2)}) copy-start(pred[512,512]{1,0:T(8,128)(4,1)} %fusion.50) | copy-start | bytes 786436
  260.8 44.9 %copy-start.18 = (f32[8,512]{1,0:T(8,128)S(1)}, f32[8,512]{1,0:T(8,128)}, u32[]{:S(2)}) copy-start(f32[8,512]{1,0:T(8,128)} %get-tuple-element.34) | copy-start | bytes 49156
  260.8 44.9 %copy-start.19 = (f32[512,8]{0,1:T(8,128)S(1)}, f32[512,8]{0,1:T(8,128)}, u32[]{:S(2)}) copy-start(f32[512,8]{0,1:T(8,128)} %subtract_exponential_fusion) | copy-start | bytes 49156
  260.8 44.9 %copy-start.20 = (f32[8,512]{1,0:T(8,128)S(1)}, f32[8,512]{1,0:T(8,128)}, u32[]{:S(2)}) copy-start(f32[8,512]{1,0:T(8,128)} %add_bitcast_fusion.1) | copy-start | bytes 49156
  275.4 16.4 %collective-permute-start.4 = (f32[8,65,128]{2,1,0:T(8,128)S(1)}, f32[8,65,128]{2,1,0:T(8,128)S(1)}, u32[]{:S(2)}, u32[]{:S(2)}) collective-permute-start(f32[8,65,128]{2,1,0:T(8,128)S(1)} %pad_maximum_fusion.4), channel_id=1, source_target_pairs={{0,32},{8,40},{16,48},{24,56},{32,64},{40,72},{48,80},{56,88},{64,... | collective-permute-start | bytes 798728 | tf_op jit(solution)/shard_map/ppermute | solution.py:17
  292.1 20.5 %collective-permute-start.5 = (f32[8,65,128]{2,1,0:T(8,128)S(1)}, f32[8,65,128]{2,1,0:T(8,128)S(1)}, u32[]{:S(2)}, u32[]{:S(2)}) collective-permute-start(f32[8,65,128]{2,1,0:T(8,128)S(1)} %pad_maximum_fusion.5), channel_id=1, source_target_pairs={{0,64},{8,72},{16,80},{24,88},{32,96},{40,104},{48,112},{56,120},{... | collective-permute-start | bytes 798728 | tf_op jit(solution)/shard_map/ppermute | solution.py:17
  313.0 10.4 %collective-permute-start.6 = (f32[8,65,128]{2,1,0:T(8,128)S(1)}, f32[8,65,128]{2,1,0:T(8,128)S(1)}, u32[]{:S(2)}, u32[]{:S(2)}) collective-permute-start(f32[8,65,128]{2,1,0:T(8,128)S(1)} %pad_maximum_fusion.6), channel_id=1, source_target_pairs={{0,128},{8,136},{16,144},{24,152},{32,160},{40,168},{48,176},{56,1... | collective-permute-start | bytes 798728 | tf_op jit(solution)/shard_map/ppermute | solution.py:17
  (36 other events, 412.7 us)
Sparse Core Ops, SparseCore 0:
  9.8 16.6 all-gather.1
  41.6 101.4 reduce-scatter.1

commit v2 on v1

--- a/solution.py
+++ b/solution.py
@@ -228,6 +228,7 @@
                 fwd_in[0][:, None, None] * early_b + fwd_in[1],
             )
             bwd_in = near_far(bwd_in, late_a, late_b, late_m)
+        fwd_in, fwd_ex, bwd_in, bwd_ex = lax.optimization_barrier((fwd_in, fwd_ex, bwd_in, bwd_ex))
         shift *= 2
     state_in = fwd_ex[1]
     carried_in = jnp.einsum("tn,hpn->thp", c_proj.astype(jnp.float32), state_in, precision=PRECISE)

time: 340 us -> 318 us (0.935)
  the two profiles are of different devices: /device:TPU:101 before, /device:TPU:103 now
where the time goes in v2:
time: 318 us; the launch traced here: 316 us
  waiting for transfers between devices  140 us (44%)
  starting transfers between devices  50.8 us (16%)
  other arithmetic  42.4 us (13%)
  matrix products  34.8 us (11%)
  between operations  22.5 us (7%)
  local copies, waits for them, and re-layouts  20.8 us (7%)
  blocking collectives  5.12 us (2%)
    reduce_scatter x1, waiting for transfers between devices, shards(): lax.psum_scatter(jnp.concatenate(pieces, axis=2), 'col', scatter_dimensio...  82.2 us
    ppermute x12, starting transfers between devices, from_behind(): lax.ppermute(value, axis, [(source, source + steps) for source in range(f...  50.8 us
    ppermute x12, waiting for transfers between devices, from_behind(): lax.ppermute(value, axis, [(source, source + steps) for source in range(f...  38.2 us
    all_gather x1, waiting for transfers between devices, shards(): tokens = lax.all_gather(hidden, 'row', axis=0, tiled=True)  18.5 us
    dot_general x4, matrix products, shards(): jnp.einsum('td,dgc->gtc', tokens, weight, preferred_element_type=jnp.floa...  10.4 us
    slice x13, local copies, waits for them, and re-layouts, unpack(): return (packed[:, p_n, 0], packed[:, :p_n], packed[0, p_n, n_n - 1])  8.85 us
    dot_general x1, matrix products, local_terms(): jnp.einsum('hij,jhp->ihp', mixing, x_vals.astype(jnp.float32), precision=...  8.75 us
    dot_general x6, matrix products, convolve(): from_edge = jnp.dot(picker, table, preferred_element_type=jnp.float32)  8.44 us
  transfers between devices with their start and end apart: 14, of which 9 were waited for; matrix products, arithmetic and copies ran while one was open for 14% of the time, Pallas kernels for 0%

profile of v2, /device:TPU:103, one launch (start us, length us, event | category | flops | bytes accessed | tf_op | source)
XLA Modules:
  0.0 316.0 jit_solution(318258473700123528)
XLA Ops:
  8.0 18.5 %all-gather.2.cloned.1.call-done = bf16[512,1024]{1,0:T(8,128)(2,1)} async-done(((bf16[256,1024]{1,0:T(8,128)(2,1)}), bf16[512,1024]{1,0:T(8,128)(2,1)}) %all-gather.2.cloned.1.call-update) | async-done | bytes 1048592 | tf_op jit(solution)/shard_map/all_gather | solution.py:120
  28.1 3.3 %fusion.30 = f32[4,512,256]{1,2,0:T(8,128)S(1)} fusion(bf16[1024,4,256]{2,1,0:T(4,128)(2,1)} %param.20, bf16[512,1024]{1,0:T(8,128)(2,1)} %all-gather.2.cloned.1.call-done), kind=kOutput, calls=%fused_computation.33 | convolution fusion | flops 1073741824 | bytes 5242880 | tf_op jit(solution)/shard_map/td,dgc->gtc/dot_general | solution.py:126
  31.6 2.7 fusion.23
  34.3 2.7 fusion.20
  37.0 4.4 %pad_maximum_fusion = f32[4,512,1288]{1,2,0:T(8,128)} fusion(f32[4,512,8]{1,2,0:T(8,128)S(1)} %convolution_bitcast_fusion, f32[4,512,256]{1,2,0:T(8,128)S(1)} %fusion.30, f32[4,512,512]{1,2,0:T(8,128)S(1)} %fusion.23, f32[4,512,512]{1,2,0:T(8,128)S(1)} %fusion.20), kind=kLoop, calls=%fused_computation.5 | loop fusion | flops 7913472 | bytes 21102592 | tf_op jit(solution)/shard_map/concatenate | solution.py:130
  60.9 82.2 %reduce-scatter.2.cloned.1.call-done = f32[1,512,1288]{1,2,0:T(8,128)} async-done(((f32[4,512,1288]{1,2,0:T(8,128)}), f32[1,512,1288]{1,2,0:T(8,128)}) %reduce-scatter.2.cloned.1.call-update) | async-done | bytes 2637840 | tf_op jit(solution)/shard_map/reduce_scatter | solution.py:129
  147.5 4.4 %collective-permute-start = (bf16[3,512]{0,1:T(8,128)(2,1)}, bf16[3,512]{0,1:T(8,128)(2,1)}, u32[]{:S(2)}, u32[]{:S(2)}) collective-permute-start(bf16[3,512]{0,1:T(8,128)(2,1)} %slice_select_fusion), channel_id=1, source_target_pairs={{0,8},{8,16},{16,24},{24,32},{32,40},{40,48},{48,56},{56,64},{64,7... | collective-permute-start | bytes 9224 | tf_op jit(solution)/shard_map/ppermute | solution.py:17
  152.0 2.5 collective-permute-start.1
  159.4 2.4 multiply_convert_fusion.1
  165.5 4.0 %collective-permute-start.2 = (f32[8,65,128]{2,1,0:T(8,128)S(1)}, f32[8,65,128]{2,1,0:T(8,128)S(1)}, u32[]{:S(2)}, u32[]{:S(2)}) collective-permute-start(f32[8,65,128]{2,1,0:T(8,128)S(1)} %pad_maximum_fusion.2), channel_id=1, source_target_pairs={{0,8},{8,16},{16,24},{24,32},{32,40},{40,48},{48,56},{56,64},{64,7... | collective-permute-start | bytes 798728 | tf_op jit(solution)/shard_map/ppermute | solution.py:17
  174.8 4.9 %collective-permute-done.3 = f32[8,65,128]{2,1,0:T(8,128)S(1)} collective-permute-done((f32[8,65,128]{2,1,0:T(8,128)S(1)}, f32[8,65,128]{2,1,0:T(8,128)S(1)}, u32[]{:S(2)}, u32[]{:S(2)}) %collective-permute-start.3) | collective-permute-done | bytes 266272 | tf_op jit(solution)/shard_map/ppermute | solution.py:17
  185.6 4.3 %collective-permute-start.5 = (f32[8,65,128]{2,1,0:T(8,128)S(1)}, f32[8,65,128]{2,1,0:T(8,128)S(1)}, u32[]{:S(2)}, u32[]{:S(2)}) collective-permute-start(f32[8,65,128]{2,1,0:T(8,128)S(1)} %pad_maximum_fusion.5), channel_id=1, source_target_pairs={{16,0},{24,8},{32,16},{40,24},{48,32},{56,40},{64,48},{72,56},{80,... | collective-permute-start | bytes 798728 | tf_op jit(solution)/shard_map/ppermute | solution.py:17
  192.4 10.4 %collective-permute-done.5 = f32[8,65,128]{2,1,0:T(8,128)S(1)} collective-permute-done((f32[8,65,128]{2,1,0:T(8,128)S(1)}, f32[8,65,128]{2,1,0:T(8,128)S(1)}, u32[]{:S(2)}, u32[]{:S(2)}) %collective-permute-start.5) | collective-permute-done | bytes 266272 | tf_op jit(solution)/shard_map/ppermute | solution.py:17
  212.1 8.2 %collective-permute-start.7 = (f32[8,65,128]{2,1,0:T(8,128)}, f32[8,65,128]{2,1,0:T(8,128)}, u32[]{:S(2)}, u32[]{:S(2)}) collective-permute-start(f32[8,65,128]{2,1,0:T(8,128)} %pad_maximum_fusion.7), channel_id=1, source_target_pairs={{32,0},{40,8},{48,16},{56,24},{64,32},{72,40},{80,48},{88,56},{96,... | collective-permute-start | bytes 798728 | tf_op jit(solution)/shard_map/ppermute | solution.py:17
  220.2 2.6 fusion.51
  222.9 4.7 %collective-permute-done.7 = f32[8,65,128]{2,1,0:T(8,128)} collective-permute-done((f32[8,65,128]{2,1,0:T(8,128)}, f32[8,65,128]{2,1,0:T(8,128)}, u32[]{:S(2)}, u32[]{:S(2)}) %collective-permute-start.7) | collective-permute-done | bytes 266272 | tf_op jit(solution)/shard_map/ppermute | solution.py:17
  230.2 7.2 %collective-permute-done.6 = f32[8,65,128]{2,1,0:T(8,128)} collective-permute-done((f32[8,65,128]{2,1,0:T(8,128)}, f32[8,65,128]{2,1,0:T(8,128)}, u32[]{:S(2)}, u32[]{:S(2)}) %collective-permute-start.6) | collective-permute-done | bytes 266272 | tf_op jit(solution)/shard_map/ppermute | solution.py:17
  246.2 12.7 %collective-permute-start.9 = (f32[8,65,128]{2,1,0:T(8,128)}, f32[8,65,128]{2,1,0:T(8,128)}, u32[]{:S(2)}, u32[]{:S(2)}) collective-permute-start(f32[8,65,128]{2,1,0:T(8,128)} %pad_maximum_fusion.9), channel_id=1, source_target_pairs={{64,0},{72,8},{80,16},{88,24},{96,32},{104,40},{112,48},{120,56},{... | collective-permute-start | bytes 798728 | tf_op jit(solution)/shard_map/ppermute | solution.py:17
  260.8 3.4 %collective-permute-done.9 = f32[8,65,128]{2,1,0:T(8,128)} collective-permute-done((f32[8,65,128]{2,1,0:T(8,128)}, f32[8,65,128]{2,1,0:T(8,128)}, u32[]{:S(2)}, u32[]{:S(2)}) %collective-permute-start.9) | collective-permute-done | bytes 266272 | tf_op jit(solution)/shard_map/ppermute | solution.py:17
  270.9 6.3 %collective-permute-start.11 = (f32[8,65,128]{2,1,0:T(8,128)S(1)}, f32[8,65,128]{2,1,0:T(8,128)}, u32[]{:S(2)}, u32[]{:S(2)}) collective-permute-start(f32[8,65,128]{2,1,0:T(8,128)S(1)} %pad_maximum_fusion.11), channel_id=1, source_target_pairs={{128,0},{136,8},{144,16},{152,24},{160,32},{168,40},{176,48},{184,... | collective-permute-start | bytes 798728 | tf_op jit(solution)/shard_map/ppermute | solution.py:17
  277.2 8.8 %fusion.38 = f32[512,8,64]{0,2,1:T(8,128)} fusion(bf16[512,8,64]{0,2,1:T(8,128)(2,1)} %bitcast.150, f32[8,512]{1,0:T(8,128)S(1)} %get-tuple-element.107, f32[512,512]{1,0:T(8,128)S(1)} %fusion.77, f32[8,512]{1,0:T(8,128)S(1)} %copy-done.20, pred[512,512]{1,0:T(8,128)(4,1)} %fusion.50, f32[512,8,64]{0,2,1:T(8,128)S(1)} %bitcast.152, ...), kind=kOutput, calls=%fused_computation.38 | convolution fusion | flops 1621622784 | bytes 3981312 | tf_op jit(solution)/shard_map/hij,jhp->ihp/dot_general | solution.py:38
  290.2 5.8 %collective-permute-done.10 = f32[8,65,128]{2,1,0:T(8,128)S(1)} collective-permute-done((f32[8,65,128]{2,1,0:T(8,128)S(1)}, f32[8,65,128]{2,1,0:T(8,128)S(1)}, u32[]{:S(2)}, u32[]{:S(2)}) %collective-permute-start.10) | collective-permute-done | bytes 266272 | tf_op jit(solution)/shard_map/ppermute | solution.py:17
  296.2 2.2 fusion.37
  298.7 5.1 %psum.7 = f32[512]{0:T(512)S(1)} all-reduce(f32[512]{0:T(512)S(1)} %multiply_reduce_fusion), channel_id=1, replica_groups=mesh['seq'=32,'row'=2,'col'=4] {'row'}, use_global_device_ids=true, to_apply=%region_15.16 | all-reduce | flops 512 | bytes 4096 | tf_op jit(solution)/shard_map/psum | solution.py:249
  (260 shorter events, 80.0 us)
Async XLA Ops:
  7.2 19.3 %copy-start = (bf16[1024,4,8]{0,2,1:T(8,128)(2,1)S(1)}, bf16[1024,4,8]{0,2,1:T(8,128)(2,1)}, u32[]{:S(2)}) copy-start(bf16[1024,4,8]{0,2,1:T(8,128)(2,1)} %param.21) | copy-start | bytes 196612
  7.2 19.3 %all-gather.2.cloned.1.call-start = ((), (), s32[]{:S(2)}) async-start(), calls=%async_computation.1 | async-start | bytes 1572864 | tf_op jit(solution)/shard_map/all_gather | solution.py:120
  7.9 135.1 %reduce-scatter.2.cloned.1.call-start = ((), (), s32[]{:S(2)}) async-start(), calls=%async_computation.2 | async-start | bytes 13189120 | tf_op jit(solution)/shard_map/reduce_scatter | solution.py:129
  42.1 102.9 %copy-start.29 = (f32[1,8]{1,0:T(1,128)S(1)}, f32[1,8]{1,0:T(1,128)}, u32[]{:S(2)}) copy-start(f32[1,8]{1,0:T(1,128)} %param.26) | copy-start | bytes 100
  42.1 102.9 %copy-start.30 = (f32[1,8]{1,0:T(1,128)S(1)}, f32[1,8]{1,0:T(1,128)}, u32[]{:S(2)}) copy-start(f32[1,8]{1,0:T(1,128)} %param.27) | copy-start | bytes 100
  147.5 11.9 %collective-permute-start = (bf16[3,512]{0,1:T(8,128)(2,1)}, bf16[3,512]{0,1:T(8,128)(2,1)}, u32[]{:S(2)}, u32[]{:S(2)}) collective-permute-start(bf16[3,512]{0,1:T(8,128)(2,1)} %slice_select_fusion), channel_id=1, source_target_pairs={{0,8},{8,16},{16,24},{24,32},{32,40},{40,48},{48,56},{56,64},{64,7... | collective-permute-start | bytes 9224 | tf_op jit(solution)/shard_map/ppermute | solution.py:17
  152.0 5.5 %collective-permute-start.1 = (bf16[3,256]{0,1:T(8,128)(2,1)S(1)}, bf16[3,256]{0,1:T(8,128)(2,1)S(1)}, u32[]{:S(2)}, u32[]{:S(2)}) collective-permute-start(bf16[3,256]{0,1:T(8,128)(2,1)S(1)} %slice_select_fusion.1), channel_id=1, source_target_pairs={{0,8},{8,16},{16,24},{24,32},{32,40},{40,48},{48,56},{56,64},{64,7... | collective-permute-start | bytes 4616 | tf_op jit(solution)/shard_map/ppermute | solution.py:17
  165.5 9.1 %collective-permute-start.2 = (f32[8,65,128]{2,1,0:T(8,128)S(1)}, f32[8,65,128]{2,1,0:T(8,128)S(1)}, u32[]{:S(2)}, u32[]{:S(2)}) collective-permute-start(f32[8,65,128]{2,1,0:T(8,128)S(1)} %pad_maximum_fusion.2), channel_id=1, source_target_pairs={{0,8},{8,16},{16,24},{24,32},{32,40},{40,48},{48,56},{56,64},{64,7... | collective-permute-start | bytes 798728 | tf_op jit(solution)/shard_map/ppermute | solution.py:17
  169.6 10.1 %collective-permute-start.3 = (f32[8,65,128]{2,1,0:T(8,128)S(1)}, f32[8,65,128]{2,1,0:T(8,128)S(1)}, u32[]{:S(2)}, u32[]{:S(2)}) collective-permute-start(f32[8,65,128]{2,1,0:T(8,128)S(1)} %pad_maximum_fusion.3), channel_id=1, source_target_pairs={{8,0},{16,8},{24,16},{32,24},{40,32},{48,40},{56,48},{64,56},{72,6... | collective-permute-start | bytes 798728 | tf_op jit(solution)/shard_map/ppermute | solution.py:17
  174.8 16.7 %copy-start.27 = (f32[8]{0:T(128)}, f32[8]{0:T(128)S(1)}, u32[]{:S(2)}) copy-start(f32[8]{0:T(128)S(1)} %mul.423) | copy-start | bytes 100
  182.3 23.2 %copy-start.31 = (f32[8]{0:T(128)S(1)}, f32[8]{0:T(128)}, u32[]{:S(2)}) copy-start(f32[8]{0:T(128)} %get-tuple-element.53) | copy-start | bytes 100
  183.5 21.0 %collective-permute-start.4 = (f32[8,65,128]{2,1,0:T(8,128)S(1)}, f32[8,65,128]{2,1,0:T(8,128)S(1)}, u32[]{:S(2)}, u32[]{:S(2)}) collective-permute-start(f32[8,65,128]{2,1,0:T(8,128)S(1)} %pad_maximum_fusion.4), channel_id=1, source_target_pairs={{0,16},{8,24},{16,32},{24,40},{32,48},{40,56},{48,64},{56,72},{64,... | collective-permute-start | bytes 798728 | tf_op jit(solution)/shard_map/ppermute | solution.py:17
  185.6 17.2 %collective-permute-start.5 = (f32[8,65,128]{2,1,0:T(8,128)S(1)}, f32[8,65,128]{2,1,0:T(8,128)S(1)}, u32[]{:S(2)}, u32[]{:S(2)}) collective-permute-start(f32[8,65,128]{2,1,0:T(8,128)S(1)} %pad_maximum_fusion.5), channel_id=1, source_target_pairs={{16,0},{24,8},{32,16},{40,24},{48,32},{56,40},{64,48},{72,56},{80,... | collective-permute-start | bytes 798728 | tf_op jit(solution)/shard_map/ppermute | solution.py:17
  209.3 28.1 %collective-permute-start.6 = (f32[8,65,128]{2,1,0:T(8,128)}, f32[8,65,128]{2,1,0:T(8,128)}, u32[]{:S(2)}, u32[]{:S(2)}) collective-permute-start(f32[8,65,128]{2,1,0:T(8,128)} %pad_maximum_fusion.6), channel_id=1, source_target_pairs={{0,32},{8,40},{16,48},{24,56},{32,64},{40,72},{48,80},{56,88},{64,... | collective-permute-start | bytes 798728 | tf_op jit(solution)/shard_map/ppermute | solution.py:17
  212.1 15.4 %collective-permute-start.7 = (f32[8,65,128]{2,1,0:T(8,128)}, f32[8,65,128]{2,1,0:T(8,128)}, u32[]{:S(2)}, u32[]{:S(2)}) collective-permute-start(f32[8,65,128]{2,1,0:T(8,128)} %pad_maximum_fusion.7), channel_id=1, source_target_pairs={{32,0},{40,8},{48,16},{56,24},{64,32},{72,40},{80,48},{88,56},{96,... | collective-permute-start | bytes 798728 | tf_op jit(solution)/shard_map/ppermute | solution.py:17
  230.2 30.2 %copy-start.13 = (bf16[512,256]{0,1:T(8,128)(2,1)S(1)}, bf16[512,256]{0,1:T(8,128)(2,1)}, u32[]{:S(2)}) copy-start(bf16[512,256]{0,1:T(8,128)(2,1)} %copy-done.12) | copy-start | bytes 786436
  244.1 22.4 %collective-permute-start.8 = (f32[8,65,128]{2,1,0:T(8,128)}, f32[8,65,128]{2,1,0:T(8,128)}, u32[]{:S(2)}, u32[]{:S(2)}) collective-permute-start(f32[8,65,128]{2,1,0:T(8,128)} %pad_maximum_fusion.8), channel_id=1, source_target_pairs={{0,64},{8,72},{16,80},{24,88},{32,96},{40,104},{48,112},{56,120},{... | collective-permute-start | bytes 798728 | tf_op jit(solution)/shard_map/ppermute | solution.py:17
  246.2 31.1 %copy-start.20 = (f32[8,512]{1,0:T(8,128)S(1)}, f32[8,512]{1,0:T(8,128)}, u32[]{:S(2)}) copy-start(f32[8,512]{1,0:T(8,128)} %add_bitcast_fusion.1) | copy-start | bytes 49156
  246.2 18.0 %collective-permute-start.9 = (f32[8,65,128]{2,1,0:T(8,128)}, f32[8,65,128]{2,1,0:T(8,128)}, u32[]{:S(2)}, u32[]{:S(2)}) collective-permute-start(f32[8,65,128]{2,1,0:T(8,128)} %pad_maximum_fusion.9), channel_id=1, source_target_pairs={{64,0},{72,8},{80,16},{88,24},{96,32},{104,40},{112,48},{120,56},{... | collective-permute-start | bytes 798728 | tf_op jit(solution)/shard_map/ppermute | solution.py:17
  260.4 16.8 %copy-start.16 = (f32[512,512]{0,1:T(8,128)S(1)}, f32[512,512]{0,1:T(8,128)}, u32[]{:S(2)}) copy-start(f32[512,512]{0,1:T(8,128)} %fusion.19) | copy-start | bytes 3145732
  270.9 16.6 %collective-permute-start.11 = (f32[8,65,128]{2,1,0:T(8,128)S(1)}, f32[8,65,128]{2,1,0:T(8,128)}, u32[]{:S(2)}, u32[]{:S(2)}) collective-permute-start(f32[8,65,128]{2,1,0:T(8,128)S(1)} %pad_maximum_fusion.11), channel_id=1, source_target_pairs={{128,0},{136,8},{144,16},{152,24},{160,32},{168,40},{176,48},{184,... | collective-permute-start | bytes 798728 | tf_op jit(solution)/shard_map/ppermute | solution.py:17
  277.2 18.9 %copy-start.35 = (f32[1,8]{1,0:T(1,128)S(1)}, f32[1,8]{1,0:T(1,128)}, u32[]{:S(2)}) copy-start(f32[1,8]{1,0:T(1,128)} %param.28) | copy-start | bytes 100
  286.0 17.9 %copy-start.33 = (f32[1,512]{1,0:T(1,128)S(1)}, f32[1,512]{1,0:T(1,128)}, u32[]{:S(2)}) copy-start(f32[1,512]{1,0:T(1,128)} %param.29) | copy-start | bytes 6148
  286.1 10.0 %collective-permute-start.10 = (f32[8,65,128]{2,1,0:T(8,128)S(1)}, f32[8,65,128]{2,1,0:T(8,128)S(1)}, u32[]{:S(2)}, u32[]{:S(2)}) collective-permute-start(f32[8,65,128]{2,1,0:T(8,128)S(1)} %pad_maximum_fusion.10), channel_id=1, source_target_pairs={{0,128},{8,136},{16,144},{24,152},{32,160},{40,168},{48,176},{56,1... | collective-permute-start | bytes 798728 | tf_op jit(solution)/shard_map/ppermute | solution.py:17
  (32 other events, 218.2 us)
Sparse Core Ops, SparseCore 0:
  9.8 16.6 all-gather.1
  41.6 101.3 reduce-scatter.1

commit v3 on v2

--- a/solution.py
+++ b/solution.py
@@ -122,18 +122,18 @@
     channels = w_x.shape[2]
     heads_here = w_dt.shape[2]
     lagged = conv_x_w.shape[0] - 1
-    pieces = [
+    x_part, z_part, bc_part, dt_part = [
         jnp.einsum("td,dgc->gtc", tokens, weight, preferred_element_type=jnp.float32)
         for weight in (w_x, w_z, w_bc, w_dt)
     ]
-    summed = lax.psum_scatter(
-        jnp.concatenate(pieces, axis=2), "col", scatter_dimension=0, tiled=True
-    )
-    mixed = summed[0].astype(jnp.bfloat16)
-    x_raw = mixed[:, :channels]
-    z_gate = mixed[:, channels : 2 * channels]
-    bc_raw = mixed[:, 2 * channels : 2 * channels + 2 * N]
-    dt_raw = mixed[:, 2 * channels + 2 * N :]
+    first = lax.psum_scatter(
+        jnp.concatenate([x_part, bc_part, dt_part], axis=2), "col", scatter_dimension=0, tiled=True
+    )[0].astype(jnp.bfloat16)
+    first, z_part = lax.optimization_barrier((first, z_part))
+    z_gate = lax.psum_scatter(z_part, "col", scatter_dimension=0, tiled=True)[0].astype(jnp.bfloat16)
+    x_raw = first[:, :channels]
+    bc_raw = first[:, channels : channels + 2 * N]
+    dt_raw = first[:, channels + 2 * N :]
     positions = jnp.arange(rows_here, dtype=jnp.int32)
     flag_vals = starts == 1
     segment = jnp.cumsum(starts)

time: 318 us -> 313 us (0.984)
  the two profiles are of different devices: /device:TPU:103 before, /device:TPU:71 now
where the time goes in v3:
time: 313 us; the launch traced here: 311 us
  waiting for transfers between devices  109 us (35%)
  other arithmetic  55.8 us (18%)
  matrix products  43.4 us (14%)
  starting transfers between devices  38.5 us (12%)
  local copies, waits for them, and re-layouts  37.4 us (12%)
  between operations  21.9 us (7%)
  blocking collectives  4.3 us (1%)
    ppermute x12, waiting for transfers between devices, from_behind(): lax.ppermute(value, axis, [(source, source + steps) for source in range(f...  46.7 us
    reduce_scatter x1, waiting for transfers between devices, shards(): lax.psum_scatter(jnp.concatenate([x_part, bc_part, dt_part], axis=2), 'co...  43.2 us
    ppermute x12, starting transfers between devices, from_behind(): lax.ppermute(value, axis, [(source, source + steps) for source in range(f...  38.4 us
    all_gather x1, waiting for transfers between devices, shards(): tokens = lax.all_gather(hidden, 'row', axis=0, tiled=True)  18.9 us
    dot_general x4, matrix products, shards(): jnp.einsum('td,dgc->gtc', tokens, weight, preferred_element_type=jnp.floa...  14.2 us
    slice x13, local copies, waits for them, and re-layouts, unpack(): return (packed[:, p_n, 0], packed[:, :p_n], packed[0, p_n, n_n - 1])  11.6 us
    dot_general x1, matrix products, local_terms(): jnp.einsum('hij,jhp->ihp', mixing, x_vals.astype(jnp.float32), precision=...  9.11 us
    dot_general x6, matrix products, convolve(): from_edge = jnp.dot(picker, table, preferred_element_type=jnp.float32)  8.58 us
  transfers between devices with their start and end apart: 15, of which 9 were waited for; matrix products, arithmetic and copies ran while one was open for 36% of the time, Pallas kernels for 0%

profile of v3, /device:TPU:71, one launch (start us, length us, event | category | flops | bytes accessed | tf_op | source)
XLA Modules:
  0.0 310.7 jit_solution(7199822191038245810)
XLA Ops:
  8.0 18.9 %all-gather.2.cloned.1.call-done = bf16[512,1024]{1,0:T(8,128)(2,1)} async-done(((bf16[256,1024]{1,0:T(8,128)(2,1)}), bf16[512,1024]{1,0:T(8,128)(2,1)}) %all-gather.2.cloned.1.call-update) | async-done | bytes 1048592 | tf_op jit(solution)/shard_map/all_gather | solution.py:120
  28.8 2.6 fusion.30
  34.1 3.2 %pad_maximum_fusion = f32[4,512,776]{2,1,0:T(8,128)} fusion(f32[4,512,8]{2,1,0:T(8,128)S(1)} %convolution_bitcast_fusion, f32[4,512,256]{2,1,0:T(8,128)S(1)} %fusion.30, f32[4,512,512]{2,1,0:T(8,128)S(1)} %fusion.20), kind=kLoop, calls=%fused_computation.12 | loop fusion | flops 3178496 | bytes 12713984 | tf_op jit(solution)/shard_map/concatenate | solution.py:130
  63.2 7.1 %fusion.23 = f32[4,512,512]{1,2,0:T(8,128)} fusion(bf16[1024,4,512]{2,1,0:T(4,128)(2,1)} %param.19, bf16[512,1024]{1,0:T(8,128)(2,1)S(1)} %copy-done.53), kind=kOutput, calls=%fused_computation.28 | convolution fusion | flops 2147483648 | bytes 9437184 | tf_op jit(solution)/shard_map/td,dgc->gtc/dot_general | solution.py:126
  70.3 43.2 %reduce-scatter.3.cloned.1.call-done = f32[1,512,776]{2,1,0:T(8,128)} async-done(((f32[4,512,776]{2,1,0:T(8,128)}), f32[1,512,776]{2,1,0:T(8,128)}) %reduce-scatter.3.cloned.1.call-update) | async-done | bytes 1589264 | tf_op jit(solution)/shard_map/reduce_scatter | solution.py:129
  115.9 3.2 %collective-permute-start = (bf16[3,512]{1,0:T(4,128)(2,1)}, bf16[3,512]{1,0:T(4,128)(2,1)}, u32[]{:S(2)}, u32[]{:S(2)}) collective-permute-start(bf16[3,512]{1,0:T(4,128)(2,1)} %slice_select_fusion), channel_id=1, source_target_pairs={{0,8},{8,16},{16,24},{24,32},{32,40},{40,48},{48,56},{56,64},{64,7... | collective-permute-start | bytes 9224 | tf_op jit(solution)/shard_map/ppermute | solution.py:17
  122.2 4.6 %collective-permute-start.1 = (bf16[3,256]{1,0:T(4,128)(2,1)}, bf16[3,256]{1,0:T(4,128)(2,1)}, u32[]{:S(2)}, u32[]{:S(2)}) collective-permute-start(bf16[3,256]{1,0:T(4,128)(2,1)} %slice_select_fusion.1), channel_id=1, source_target_pairs={{0,8},{8,16},{16,24},{24,32},{32,40},{40,48},{48,56},{56,64},{64,7... | collective-permute-start | bytes 4616 | tf_op jit(solution)/shard_map/ppermute | solution.py:17
  146.4 2.6 multiply_convert_fusion.1
  149.1 3.1 %multiply_convert_fusion = bf16[512,512]{1,0:T(8,128)(2,1)} fusion(f32[512,512]{1,0:T(8,128)S(1)} %fusion.66, f32[512,512]{1,0:T(8,128)S(1)} %fusion.68, bf16[512,512]{1,0:T(8,128)(2,1)S(1)} %slice-done, bf16[3,512]{1,0:T(4,128)(2,1)} %collective-permute-done, f32[512]{0:T(512)S(1)} %bitcast.210, f32[512]{0:T(512)S(1)} %bitcast.211, f32[512]{0:T(512)S(1)} %bitcast.209, ...), kind=kOutput, calls=%fused_computation.56 | convolution fusion | flops 12325376 | bytes 3171840 | tf_op jit(solution)/shard_map/dot_general | solution.py:93
  154.6 3.0 fusion.11
  161.7 3.4 %collective-permute-start.2 = (f32[8,65,128]{2,1,0:T(8,128)S(1)}, f32[8,65,128]{2,1,0:T(8,128)S(1)}, u32[]{:S(2)}, u32[]{:S(2)}) collective-permute-start(f32[8,65,128]{2,1,0:T(8,128)S(1)} %pad_maximum_fusion.2), channel_id=1, source_target_pairs={{0,8},{8,16},{16,24},{24,32},{32,40},{40,48},{48,56},{56,64},{64,7... | collective-permute-start | bytes 798728 | tf_op jit(solution)/shard_map/ppermute | solution.py:17
  165.4 2.5 collective-permute-done.3
  175.5 5.1 %collective-permute-start.4 = (f32[8,65,128]{2,1,0:T(8,128)}, f32[8,65,128]{2,1,0:T(8,128)}, u32[]{:S(2)}, u32[]{:S(2)}) collective-permute-start(f32[8,65,128]{2,1,0:T(8,128)} %pad_maximum_fusion.4), channel_id=1, source_target_pairs={{0,16},{8,24},{16,32},{24,40},{32,48},{40,56},{48,64},{56,72},{64,... | collective-permute-start | bytes 798728 | tf_op jit(solution)/shard_map/ppermute | solution.py:17
  183.4 2.6 fusion.54
  186.0 12.5 %collective-permute-done.5 = f32[8,65,128]{2,1,0:T(8,128)} collective-permute-done((f32[8,65,128]{2,1,0:T(8,128)}, f32[8,65,128]{2,1,0:T(8,128)}, u32[]{:S(2)}, u32[]{:S(2)}) %collective-permute-start.5) | collective-permute-done | bytes 266272 | tf_op jit(solution)/shard_map/ppermute | solution.py:17
  207.6 7.5 %collective-permute-start.7 = (f32[8,65,128]{2,1,0:T(8,128)}, f32[8,65,128]{2,1,0:T(8,128)}, u32[]{:S(2)}, u32[]{:S(2)}) collective-permute-start(f32[8,65,128]{2,1,0:T(8,128)} %pad_maximum_fusion.7), channel_id=1, source_target_pairs={{32,0},{40,8},{48,16},{56,24},{64,32},{72,40},{80,48},{88,56},{96,... | collective-permute-start | bytes 798728 | tf_op jit(solution)/shard_map/ppermute | solution.py:17
  220.6 7.7 %collective-permute-done.7 = f32[8,65,128]{2,1,0:T(8,128)} collective-permute-done((f32[8,65,128]{2,1,0:T(8,128)}, f32[8,65,128]{2,1,0:T(8,128)}, u32[]{:S(2)}, u32[]{:S(2)}) %collective-permute-start.7) | collective-permute-done | bytes 266272 | tf_op jit(solution)/shard_map/ppermute | solution.py:17
  231.6 11.1 %collective-permute-done.6 = f32[8,65,128]{2,1,0:T(8,128)} collective-permute-done((f32[8,65,128]{2,1,0:T(8,128)}, f32[8,65,128]{2,1,0:T(8,128)}, u32[]{:S(2)}, u32[]{:S(2)}) %collective-permute-start.6) | collective-permute-done | bytes 266272 | tf_op jit(solution)/shard_map/ppermute | solution.py:17
  248.4 2.9 collective-permute-start.9
  265.6 3.0 collective-permute-start.11
  268.6 9.1 %fusion.38 = f32[512,8,64]{0,2,1:T(8,128)} fusion(bf16[512,8,64]{0,2,1:T(8,128)(2,1)} %bitcast.181, f32[8,512]{1,0:T(8,128)S(1)} %copy-done.24, f32[512,512]{1,0:T(8,128)} %fusion.79, f32[8,512]{1,0:T(8,128)S(1)} %copy-done.25, pred[512,512]{1,0:T(8,128)(4,1)} %fusion.53, f32[512,8,64]{0,2,1:T(8,128)} %bitcast.186, f32[512,8]{0,1:T(8,128)S(1)} %copy.117), kind=kOutput, calls=%fused_computation.39 | convolution fusion | flops 1621622784 | bytes 3981312 | tf_op jit(solution)/shard_map/hij,jhp->ihp/dot_general | solution.py:38
  279.4 9.0 %collective-permute-done.10 = f32[8,65,128]{2,1,0:T(8,128)S(1)} collective-permute-done((f32[8,65,128]{2,1,0:T(8,128)S(1)}, f32[8,65,128]{2,1,0:T(8,128)S(1)}, u32[]{:S(2)}, u32[]{:S(2)}) %collective-permute-start.10) | collective-permute-done | bytes 266272 | tf_op jit(solution)/shard_map/ppermute | solution.py:17
  291.8 3.6 %multiply_reduce_fusion = (f32[512]{0:T(512)S(1)}, f32[512,8,64]{0,2,1:T(8,128)}) fusion(f32[512,8,64]{0,2,1:T(8,128)S(1)} %bitcast.184, bf16[512,8,64]{0,2,1:T(8,128)(2,1)} %bitcast.182, f32[8]{0:T(128)S(1)} %bitcast.217, f32[512,8,64]{0,2,1:T(8,128)} %fusion.38, f32[8,64,128]{2,1,0:T(8,128)} %fusion.62, bf16[512,256]{1,0:T(8,128)(2,1)} %copy-done.14, ...), kind=kOutput, calls=%fused_computation.54 | convolution fusion | flops 405798400 | bytes 4081696 | tf_op jit(solution)/shard_map/tn,hpn->thp/dot_general | solution.py:234
  295.4 4.3 %psum.7 = f32[512]{0:T(512)S(1)} all-reduce(f32[512]{0:T(512)S(1)} %get-tuple-element.161), channel_id=1, replica_groups=mesh['seq'=32,'row'=2,'col'=4] {'row'}, use_global_device_ids=true, to_apply=%region_16.17 | all-reduce | flops 512 | bytes 4096 | tf_op jit(solution)/shard_map/psum | solution.py:249
  (293 shorter events, 113.0 us)
Async XLA Ops:
  7.2 21.6 %copy-start = (bf16[1024,4,256]{2,1,0:T(4,128)(2,1)S(1)}, bf16[1024,4,256]{2,1,0:T(4,128)(2,1)}, u32[]{:S(2)}) copy-start(bf16[1024,4,256]{2,1,0:T(4,128)(2,1)} %param.20) | copy-start | bytes 6291460
  7.2 19.6 %all-gather.2.cloned.1.call-start = ((), (), s32[]{:S(2)}) async-start(), calls=%async_computation.2 | async-start | bytes 1572864 | tf_op jit(solution)/shard_map/all_gather | solution.py:120
  7.9 105.5 %reduce-scatter.3.cloned.1.call-start = ((), (), s32[]{:S(2)}) async-start(), calls=%async_computation.3 | async-start | bytes 9175040 | tf_op jit(solution)/shard_map/reduce_scatter | solution.py:129
  37.3 21.4 %copy-start.26 = (bf16[4,1,512]{2,0,1:T(4,128)(2,1)S(1)}, bf16[4,1,512]{2,0,1:T(4,128)(2,1)}, u32[]{:S(2)}) copy-start(bf16[4,1,512]{2,0,1:T(4,128)(2,1)} %param.22) | copy-start | bytes 12292
  37.4 25.8 %copy-start.53 = (bf16[512,1024]{1,0:T(8,128)(2,1)S(1)}, bf16[512,1024]{1,0:T(8,128)(2,1)}, u32[]{:S(2)}) copy-start(bf16[512,1024]{1,0:T(8,128)(2,1)} %all-gather.2.cloned.1.call-done) | copy-start | bytes 3145732
  37.4 253.0 %reduce-scatter.5.cloned.1.call-start = ((), (), s32[]{:S(2)}) async-start(), calls=%async_computation.4 | async-start | bytes 5242880 | tf_op jit(solution)/shard_map/reduce_scatter | solution.py:133
  45.1 25.2 %copy-start.19 = (bf16[9,256]{1,0:T(8,128)(2,1)}, bf16[9,256]{1,0:T(8,128)(2,1)S(1)}, u32[]{:S(2)}) copy-start(bf16[9,256]{1,0:T(8,128)(2,1)S(1)} %reshape_squeeze.7) | copy-start | bytes 13828
  50.2 64.9 %copy-start.38 = (pred[3]{0:T(512)(128)(4,1)}, pred[3]{0:T(512)(128)(4,1)S(1)}, u32[]{:S(2)}) copy-start(pred[3]{0:T(512)(128)(4,1)S(1)} %add_compare_fusion) | copy-start | bytes 13
  70.3 48.8 %copy-start.31 = (f32[1,8]{1,0:T(1,128)S(1)}, f32[1,8]{1,0:T(1,128)}, u32[]{:S(2)}) copy-start(f32[1,8]{1,0:T(1,128)} %param.26) | copy-start | bytes 100
  70.3 48.8 %copy-start.32 = (f32[1,8]{1,0:T(1,128)S(1)}, f32[1,8]{1,0:T(1,128)}, u32[]{:S(2)}) copy-start(f32[1,8]{1,0:T(1,128)} %param.27) | copy-start | bytes 100
  115.0 23.8 %copy-start.4 = (bf16[512,776]{1,0:T(8,128)(2,1)}, bf16[512,776]{1,0:T(8,128)(2,1)S(1)}, u32[]{:S(2)}) copy-start(bf16[512,776]{1,0:T(8,128)(2,1)S(1)} %convert_bitcast_fusion) | copy-start | bytes 2383876
  115.9 33.2 %collective-permute-start = (bf16[3,512]{1,0:T(4,128)(2,1)}, bf16[3,512]{1,0:T(4,128)(2,1)}, u32[]{:S(2)}, u32[]{:S(2)}) collective-permute-start(bf16[3,512]{1,0:T(4,128)(2,1)} %slice_select_fusion), channel_id=1, source_target_pairs={{0,8},{8,16},{16,24},{24,32},{32,40},{40,48},{48,56},{56,64},{64,7... | collective-permute-start | bytes 9224 | tf_op jit(solution)/shard_map/ppermute | solution.py:17
  122.2 24.2 %collective-permute-start.1 = (bf16[3,256]{1,0:T(4,128)(2,1)}, bf16[3,256]{1,0:T(4,128)(2,1)}, u32[]{:S(2)}, u32[]{:S(2)}) collective-permute-start(bf16[3,256]{1,0:T(4,128)(2,1)} %slice_select_fusion.1), channel_id=1, source_target_pairs={{0,8},{8,16},{16,24},{24,32},{32,40},{40,48},{48,56},{56,64},{64,7... | collective-permute-start | bytes 4616 | tf_op jit(solution)/shard_map/ppermute | solution.py:17
  158.4 9.5 %collective-permute-start.3 = (f32[8,65,128]{2,1,0:T(8,128)}, f32[8,65,128]{2,1,0:T(8,128)}, u32[]{:S(2)}, u32[]{:S(2)}) collective-permute-start(f32[8,65,128]{2,1,0:T(8,128)} %pad_maximum_fusion.3), channel_id=1, source_target_pairs={{8,0},{16,8},{24,16},{32,24},{40,32},{48,40},{56,48},{64,56},{72,6... | collective-permute-start | bytes 798728 | tf_op jit(solution)/shard_map/ppermute | solution.py:17
  161.7 9.5 %collective-permute-start.2 = (f32[8,65,128]{2,1,0:T(8,128)S(1)}, f32[8,65,128]{2,1,0:T(8,128)S(1)}, u32[]{:S(2)}, u32[]{:S(2)}) collective-permute-start(f32[8,65,128]{2,1,0:T(8,128)S(1)} %pad_maximum_fusion.2), channel_id=1, source_target_pairs={{0,8},{8,16},{16,24},{24,32},{32,40},{40,48},{48,56},{56,64},{64,7... | collective-permute-start | bytes 798728 | tf_op jit(solution)/shard_map/ppermute | solution.py:17
  175.5 26.4 %collective-permute-start.4 = (f32[8,65,128]{2,1,0:T(8,128)}, f32[8,65,128]{2,1,0:T(8,128)}, u32[]{:S(2)}, u32[]{:S(2)}) collective-permute-start(f32[8,65,128]{2,1,0:T(8,128)} %pad_maximum_fusion.4), channel_id=1, source_target_pairs={{0,16},{8,24},{16,32},{24,40},{32,48},{40,56},{48,64},{56,72},{64,... | collective-permute-start | bytes 798728 | tf_op jit(solution)/shard_map/ppermute | solution.py:17
  181.4 17.1 %collective-permute-start.5 = (f32[8,65,128]{2,1,0:T(8,128)}, f32[8,65,128]{2,1,0:T(8,128)}, u32[]{:S(2)}, u32[]{:S(2)}) collective-permute-start(f32[8,65,128]{2,1,0:T(8,128)} %pad_maximum_fusion.5), channel_id=1, source_target_pairs={{16,0},{24,8},{32,16},{40,24},{48,32},{56,40},{64,48},{72,56},{80,... | collective-permute-start | bytes 798728 | tf_op jit(solution)/shard_map/ppermute | solution.py:17
  202.8 50.6 %copy-start.20 = (f32[512,3]{0,1:T(4,128)S(1)}, f32[512,3]{0,1:T(4,128)}, u32[]{:S(2)}) copy-start(f32[512,3]{0,1:T(4,128)} %copy.137) | copy-start | bytes 18436
  207.6 20.7 %collective-permute-start.7 = (f32[8,65,128]{2,1,0:T(8,128)}, f32[8,65,128]{2,1,0:T(8,128)}, u32[]{:S(2)}, u32[]{:S(2)}) collective-permute-start(f32[8,65,128]{2,1,0:T(8,128)} %pad_maximum_fusion.7), channel_id=1, source_target_pairs={{32,0},{40,8},{48,16},{56,24},{64,32},{72,40},{80,48},{88,56},{96,... | collective-permute-start | bytes 798728 | tf_op jit(solution)/shard_map/ppermute | solution.py:17
  215.9 26.8 %collective-permute-start.6 = (f32[8,65,128]{2,1,0:T(8,128)}, f32[8,65,128]{2,1,0:T(8,128)}, u32[]{:S(2)}, u32[]{:S(2)}) collective-permute-start(f32[8,65,128]{2,1,0:T(8,128)} %pad_maximum_fusion.6), channel_id=1, source_target_pairs={{0,32},{8,40},{16,48},{24,56},{32,64},{40,72},{48,80},{56,88},{64,... | collective-permute-start | bytes 798728 | tf_op jit(solution)/shard_map/ppermute | solution.py:17
  248.4 8.4 %collective-permute-start.9 = (f32[8,65,128]{2,1,0:T(8,128)}, f32[8,65,128]{2,1,0:T(8,128)}, u32[]{:S(2)}, u32[]{:S(2)}) collective-permute-start(f32[8,65,128]{2,1,0:T(8,128)} %pad_maximum_fusion.9), channel_id=1, source_target_pairs={{64,0},{72,8},{80,16},{88,24},{96,32},{104,40},{112,48},{120,56},{... | collective-permute-start | bytes 798728 | tf_op jit(solution)/shard_map/ppermute | solution.py:17
  252.1 10.0 %collective-permute-start.8 = (f32[8,65,128]{2,1,0:T(8,128)}, f32[8,65,128]{2,1,0:T(8,128)}, u32[]{:S(2)}, u32[]{:S(2)}) collective-permute-start(f32[8,65,128]{2,1,0:T(8,128)} %pad_maximum_fusion.8), channel_id=1, source_target_pairs={{0,64},{8,72},{16,80},{24,88},{32,96},{40,104},{48,112},{56,120},{... | collective-permute-start | bytes 798728 | tf_op jit(solution)/shard_map/ppermute | solution.py:17
  265.6 13.6 %collective-permute-start.11 = (f32[8,65,128]{2,1,0:T(8,128)S(1)}, f32[8,65,128]{2,1,0:T(8,128)S(1)}, u32[]{:S(2)}, u32[]{:S(2)}) collective-permute-start(f32[8,65,128]{2,1,0:T(8,128)S(1)} %pad_maximum_fusion.11), channel_id=1, source_target_pairs={{128,0},{136,8},{144,16},{152,24},{160,32},{168,40},{176,48},{184,... | collective-permute-start | bytes 798728 | tf_op jit(solution)/shard_map/ppermute | solution.py:17
  277.8 10.6 %collective-permute-start.10 = (f32[8,65,128]{2,1,0:T(8,128)S(1)}, f32[8,65,128]{2,1,0:T(8,128)S(1)}, u32[]{:S(2)}, u32[]{:S(2)}) collective-permute-start(f32[8,65,128]{2,1,0:T(8,128)S(1)} %pad_maximum_fusion.10), channel_id=1, source_target_pairs={{0,128},{8,136},{16,144},{24,152},{32,160},{40,168},{48,176},{56,1... | collective-permute-start | bytes 798728 | tf_op jit(solution)/shard_map/ppermute | solution.py:17
  (47 other events, 432.0 us)
Sparse Core Ops, SparseCore 0:
  9.8 16.9 all-gather.1
  37.5 75.8 reduce-scatter.2
  116.0 49.1 reduce-scatter.4

commit v4 on v3

--- a/solution.py
+++ b/solution.py
@@ -130,7 +130,9 @@
         jnp.concatenate([x_part, bc_part, dt_part], axis=2), "col", scatter_dimension=0, tiled=True
     )[0].astype(jnp.bfloat16)
     first, z_part = lax.optimization_barrier((first, z_part))
-    z_gate = lax.psum_scatter(z_part, "col", scatter_dimension=0, tiled=True)[0].astype(jnp.bfloat16)
+    z_gate = lax.optimization_barrier(
+        lax.psum_scatter(z_part, "col", scatter_dimension=0, tiled=True)[0].astype(jnp.bfloat16)
+    )
     x_raw = first[:, :channels]
     bc_raw = first[:, channels : channels + 2 * N]
     dt_raw = first[:, channels + 2 * N :]

time: 313 us -> 306 us (0.978)
  other arithmetic: 55.8 us -> 61.4 us
  waiting for transfers between devices: 109 us -> 104 us
  local copies, waits for them, and re-layouts: 37.4 us -> 32.8 us
  matrix products: 43.4 us -> 40.1 us
    ppermute x12, waiting for transfers between devices: 46.7 us -> 40.3 us  [from_behind(): lax.ppermute(value, axis, [(source, source + steps) for source in range(f...]
    unnamed x112 -> x119, local copies, waits for them, and re-layouts: 5.92 us -> 1.51 us
  transfers between devices with their start and end apart: 15 -> 15, of which waited for: 9 -> 10; matrix products, arithmetic and copies ran while one was open for 36% -> 38% of each run, Pallas kernels for 0% -> 0%
where the time goes in v4:
time: 306 us; the launch traced here: 304 us
  waiting for transfers between devices  104 us (34%)
  other arithmetic  61.4 us (20%)
  matrix products  40.1 us (13%)
  starting transfers between devices  39.6 us (13%)
  local copies, waits for them, and re-layouts  32.8 us (11%)
  between operations  22.3 us (7%)
  blocking collectives  4.33 us (1%)
    reduce_scatter x1, waiting for transfers between devices, shards(): lax.psum_scatter(jnp.concatenate([x_part, bc_part, dt_part], axis=2), 'co...  44.2 us
    ppermute x12, waiting for transfers between devices, from_behind(): lax.ppermute(value, axis, [(source, source + steps) for source in range(f...  40.3 us
    ppermute x12, starting transfers between devices, from_behind(): lax.ppermute(value, axis, [(source, source + steps) for source in range(f...  39.5 us
    all_gather x1, waiting for transfers between devices, shards(): tokens = lax.all_gather(hidden, 'row', axis=0, tiled=True)  18.9 us
    dot_general x4, matrix products, shards(): jnp.einsum('td,dgc->gtc', tokens, weight, preferred_element_type=jnp.floa...  13.8 us
    slice x13, local copies, waits for them, and re-layouts, unpack(): return (packed[:, p_n, 0], packed[:, :p_n], packed[0, p_n, n_n - 1])  11.1 us
    select_n x5, other arithmetic, near_far(): jnp.where(keep, near[1], far_a[:, None, None] * near[1] + far_b)  8.75 us
    dot_general x1, matrix products, local_terms(): jnp.einsum('hij,jhp->ihp', mixing, x_vals.astype(jnp.float32), precision=...  8.22 us
  transfers between devices with their start and end apart: 15, of which 10 were waited for; matrix products, arithmetic and copies ran while one was open for 38% of the time, Pallas kernels for 0%

profile of v4, /device:TPU:71, one launch (start us, length us, event | category | flops | bytes accessed | tf_op | source)
XLA Modules:
  0.0 304.4 jit_solution(8838376656690389574)
XLA Ops:
  8.0 18.9 %all-gather.2.cloned.1.call-done = bf16[512,1024]{1,0:T(8,128)(2,1)} async-done(((bf16[256,1024]{1,0:T(8,128)(2,1)}), bf16[512,1024]{1,0:T(8,128)(2,1)}) %all-gather.2.cloned.1.call-update) | async-done | bytes 1048592 | tf_op jit(solution)/shard_map/all_gather | solution.py:120
  26.8 5.1 %fusion.20 = f32[4,512,512]{2,1,0:T(8,128)S(1)} fusion(bf16[1024,4,512]{2,1,0:T(4,128)(2,1)} %param.18, bf16[512,1024]{1,0:T(8,128)(2,1)} %all-gather.2.cloned.1.call-done), kind=kOutput, calls=%fused_computation.27 | convolution fusion | flops 2147483648 | bytes 9437184 | tf_op jit(solution)/shard_map/td,dgc->gtc/dot_general | solution.py:126
  33.9 3.2 %pad_maximum_fusion = f32[4,512,776]{2,1,0:T(8,128)} fusion(f32[4,512,8]{2,1,0:T(8,128)S(1)} %convolution_bitcast_fusion, f32[4,512,256]{2,1,0:T(8,128)S(1)} %fusion.30, f32[4,512,512]{2,1,0:T(8,128)S(1)} %fusion.20), kind=kLoop, calls=%fused_computation.12 | loop fusion | flops 3178496 | bytes 12713984 | tf_op jit(solution)/shard_map/concatenate | solution.py:130
  62.3 6.8 %fusion.23 = f32[4,512,512]{2,1,0:T(8,128)} fusion(bf16[1024,4,512]{2,1,0:T(4,128)(2,1)} %param.19, bf16[512,1024]{1,0:T(8,128)(2,1)S(1)} %copy-done.57), kind=kOutput, calls=%fused_computation.28 | convolution fusion | flops 2147483648 | bytes 9437184 | tf_op jit(solution)/shard_map/td,dgc->gtc/dot_general | solution.py:126
  69.1 44.2 %reduce-scatter.3.cloned.1.call-done = f32[1,512,776]{2,1,0:T(8,128)} async-done(((f32[4,512,776]{2,1,0:T(8,128)}), f32[1,512,776]{2,1,0:T(8,128)}) %reduce-scatter.3.cloned.1.call-update) | async-done | bytes 1589264 | tf_op jit(solution)/shard_map/reduce_scatter | solution.py:129
  115.6 3.2 %collective-permute-start.1 = (bf16[3,256]{1,0:T(4,128)(2,1)}, bf16[3,256]{1,0:T(4,128)(2,1)}, u32[]{:S(2)}, u32[]{:S(2)}) collective-permute-start(bf16[3,256]{1,0:T(4,128)(2,1)} %slice_select_fusion.1), channel_id=1, source_target_pairs={{0,8},{8,16},{16,24},{24,32},{32,40},{40,48},{48,56},{56,64},{64,7... | collective-permute-start | bytes 4616 | tf_op jit(solution)/shard_map/ppermute | solution.py:17
  119.5 4.5 %collective-permute-start = (bf16[3,512]{1,0:T(4,128)(2,1)}, bf16[3,512]{1,0:T(4,128)(2,1)}, u32[]{:S(2)}, u32[]{:S(2)}) collective-permute-start(bf16[3,512]{1,0:T(4,128)(2,1)} %slice_select_fusion), channel_id=1, source_target_pairs={{0,8},{8,16},{16,24},{24,32},{32,40},{40,48},{48,56},{56,64},{64,7... | collective-permute-start | bytes 9224 | tf_op jit(solution)/shard_map/ppermute | solution.py:17
  150.8 3.0 fusion.11
  158.3 3.4 %collective-permute-start.2 = (f32[8,65,128]{2,1,0:T(8,128)S(1)}, f32[8,65,128]{2,1,0:T(8,128)S(1)}, u32[]{:S(2)}, u32[]{:S(2)}) collective-permute-start(f32[8,65,128]{2,1,0:T(8,128)S(1)} %pad_maximum_fusion.2), channel_id=1, source_target_pairs={{0,8},{8,16},{16,24},{24,32},{32,40},{40,48},{48,56},{56,64},{64,7... | collective-permute-start | bytes 798728 | tf_op jit(solution)/shard_map/ppermute | solution.py:17
  164.0 3.6 %collective-permute-done.2 = f32[8,65,128]{2,1,0:T(8,128)S(1)} collective-permute-done((f32[8,65,128]{2,1,0:T(8,128)S(1)}, f32[8,65,128]{2,1,0:T(8,128)S(1)}, u32[]{:S(2)}, u32[]{:S(2)}) %collective-permute-start.2) | collective-permute-done | bytes 266272 | tf_op jit(solution)/shard_map/ppermute | solution.py:17
  173.0 4.6 %collective-permute-start.5 = (f32[8,65,128]{2,1,0:T(8,128)}, f32[8,65,128]{2,1,0:T(8,128)}, u32[]{:S(2)}, u32[]{:S(2)}) collective-permute-start(f32[8,65,128]{2,1,0:T(8,128)} %pad_maximum_fusion.5), channel_id=1, source_target_pairs={{16,0},{24,8},{32,16},{40,24},{48,32},{56,40},{64,48},{72,56},{80,... | collective-permute-start | bytes 798728 | tf_op jit(solution)/shard_map/ppermute | solution.py:17
  178.4 2.8 collective-permute-start.4
  181.2 2.6 fusion.51
  183.9 7.6 %collective-permute-done.5 = f32[8,65,128]{2,1,0:T(8,128)} collective-permute-done((f32[8,65,128]{2,1,0:T(8,128)}, f32[8,65,128]{2,1,0:T(8,128)}, u32[]{:S(2)}, u32[]{:S(2)}) %collective-permute-start.5) | collective-permute-done | bytes 266272 | tf_op jit(solution)/shard_map/ppermute | solution.py:17
  200.6 6.2 %collective-permute-start.7 = (f32[8,65,128]{2,1,0:T(8,128)}, f32[8,65,128]{2,1,0:T(8,128)}, u32[]{:S(2)}, u32[]{:S(2)}) collective-permute-start(f32[8,65,128]{2,1,0:T(8,128)} %pad_maximum_fusion.7), channel_id=1, source_target_pairs={{32,0},{40,8},{48,16},{56,24},{64,32},{72,40},{80,48},{88,56},{96,... | collective-permute-start | bytes 798728 | tf_op jit(solution)/shard_map/ppermute | solution.py:17
  207.7 3.7 %collective-permute-start.6 = (f32[8,65,128]{2,1,0:T(8,128)}, f32[8,65,128]{2,1,0:T(8,128)}, u32[]{:S(2)}, u32[]{:S(2)}) collective-permute-start(f32[8,65,128]{2,1,0:T(8,128)} %pad_maximum_fusion.6), channel_id=1, source_target_pairs={{0,32},{8,40},{16,48},{24,56},{32,64},{40,72},{48,80},{56,88},{64,... | collective-permute-start | bytes 798728 | tf_op jit(solution)/shard_map/ppermute | solution.py:17
  213.7 7.4 %collective-permute-done.7 = f32[8,65,128]{2,1,0:T(8,128)} collective-permute-done((f32[8,65,128]{2,1,0:T(8,128)}, f32[8,65,128]{2,1,0:T(8,128)}, u32[]{:S(2)}, u32[]{:S(2)}) %collective-permute-start.7) | collective-permute-done | bytes 266272 | tf_op jit(solution)/shard_map/ppermute | solution.py:17
  224.5 9.8 %collective-permute-done.6 = f32[8,65,128]{2,1,0:T(8,128)} collective-permute-done((f32[8,65,128]{2,1,0:T(8,128)}, f32[8,65,128]{2,1,0:T(8,128)}, u32[]{:S(2)}, u32[]{:S(2)}) %collective-permute-start.6) | collective-permute-done | bytes 266272 | tf_op jit(solution)/shard_map/ppermute | solution.py:17
  240.0 3.1 %collective-permute-start.9 = (f32[8,65,128]{2,1,0:T(8,128)}, f32[8,65,128]{2,1,0:T(8,128)}, u32[]{:S(2)}, u32[]{:S(2)}) collective-permute-start(f32[8,65,128]{2,1,0:T(8,128)} %pad_maximum_fusion.9), channel_id=1, source_target_pairs={{64,0},{72,8},{80,16},{88,24},{96,32},{104,40},{112,48},{120,56},{... | collective-permute-start | bytes 798728 | tf_op jit(solution)/shard_map/ppermute | solution.py:17
  257.4 3.6 %collective-permute-start.11 = (f32[8,65,128]{2,1,0:T(8,128)S(1)}, f32[8,65,128]{2,1,0:T(8,128)}, u32[]{:S(2)}, u32[]{:S(2)}) collective-permute-start(f32[8,65,128]{2,1,0:T(8,128)S(1)} %pad_maximum_fusion.11), channel_id=1, source_target_pairs={{128,0},{136,8},{144,16},{152,24},{160,32},{168,40},{176,48},{184,... | collective-permute-start | bytes 798728 | tf_op jit(solution)/shard_map/ppermute | solution.py:17
  261.0 8.2 %fusion.38 = f32[512,8,64]{0,2,1:T(8,128)S(1)} fusion(bf16[512,8,64]{0,2,1:T(8,128)(2,1)} %bitcast.19, f32[8,512]{1,0:T(8,128)S(1)} %copy-done.24, f32[512,512]{1,0:T(8,128)} %fusion.77, f32[8,512]{1,0:T(8,128)S(1)} %copy-done.25, pred[512,512]{1,0:T(8,128)(4,1)} %fusion.50, f32[512,8,64]{0,2,1:T(8,128)} %bitcast.160, f32[512,8]{0,1:T(8,128)S(1)} %copy-done.23), kind=kOutput, calls=%fused_computation.39 | convolution fusion | flops 1621622784 | bytes 3981312 | tf_op jit(solution)/shard_map/hij,jhp->ihp/dot_general | solution.py:38
  273.3 6.6 %collective-permute-done.10 = f32[8,65,128]{2,1,0:T(8,128)S(1)} collective-permute-done((f32[8,65,128]{2,1,0:T(8,128)S(1)}, f32[8,65,128]{2,1,0:T(8,128)S(1)}, u32[]{:S(2)}, u32[]{:S(2)}) %collective-permute-start.10) | collective-permute-done | bytes 266272 | tf_op jit(solution)/shard_map/ppermute | solution.py:17
  280.1 2.7 fusion.37
  291.3 4.3 %psum.7 = f32[512]{0:T(512)S(1)} all-reduce(f32[512]{0:T(512)S(1)} %multiply_reduce_fusion), channel_id=1, replica_groups=mesh['seq'=32,'row'=2,'col'=4] {'row'}, use_global_device_ids=true, to_apply=%region_16.17 | all-reduce | flops 512 | bytes 4096 | tf_op jit(solution)/shard_map/psum | solution.py:251
  (302 shorter events, 113.2 us)
Async XLA Ops:
  7.2 24.7 %copy-start = (bf16[1024,4,256]{2,1,0:T(4,128)(2,1)S(1)}, bf16[1024,4,256]{2,1,0:T(4,128)(2,1)}, u32[]{:S(2)}) copy-start(bf16[1024,4,256]{2,1,0:T(4,128)(2,1)} %param.20) | copy-start | bytes 6291460
  7.2 19.6 %all-gather.2.cloned.1.call-start = ((), (), s32[]{:S(2)}) async-start(), calls=%async_computation.2 | async-start | bytes 1572864 | tf_op jit(solution)/shard_map/all_gather | solution.py:120
  7.9 105.3 %reduce-scatter.3.cloned.1.call-start = ((), (), s32[]{:S(2)}) async-start(), calls=%async_computation.3 | async-start | bytes 9175040 | tf_op jit(solution)/shard_map/reduce_scatter | solution.py:129
  37.2 25.1 %copy-start.57 = (bf16[512,1024]{1,0:T(8,128)(2,1)S(1)}, bf16[512,1024]{1,0:T(8,128)(2,1)}, u32[]{:S(2)}) copy-start(bf16[512,1024]{1,0:T(8,128)(2,1)} %all-gather.2.cloned.1.call-done) | copy-start | bytes 3145732
  37.2 250.6 %reduce-scatter.5.cloned.1.call-start = ((), (), s32[]{:S(2)}) async-start(), calls=%async_computation.4 | async-start | bytes 5242880 | tf_op jit(solution)/shard_map/reduce_scatter | solution.py:134
  44.4 24.7 %copy-start.15 = (bf16[9,256]{1,0:T(8,128)(2,1)}, bf16[9,256]{1,0:T(8,128)(2,1)S(1)}, u32[]{:S(2)}) copy-start(bf16[9,256]{1,0:T(8,128)(2,1)S(1)} %reshape_squeeze.7) | copy-start | bytes 13828
  62.3 61.8 %copy-start.33 = (f32[1,8]{1,0:T(1,128)S(1)}, f32[1,8]{1,0:T(1,128)}, u32[]{:S(2)}) copy-start(f32[1,8]{1,0:T(1,128)} %param.26) | copy-start | bytes 100
  62.3 61.8 %copy-start.34 = (f32[1,8]{1,0:T(1,128)S(1)}, f32[1,8]{1,0:T(1,128)}, u32[]{:S(2)}) copy-start(f32[1,8]{1,0:T(1,128)} %param.27) | copy-start | bytes 100
  114.9 27.5 %copy-start.2 = (bf16[512,776]{1,0:T(8,128)(2,1)}, bf16[512,776]{1,0:T(8,128)(2,1)S(1)}, u32[]{:S(2)}) copy-start(bf16[512,776]{1,0:T(8,128)(2,1)S(1)} %convert_bitcast_fusion) | copy-start | bytes 2383876
  115.6 28.1 %collective-permute-start.1 = (bf16[3,256]{1,0:T(4,128)(2,1)}, bf16[3,256]{1,0:T(4,128)(2,1)}, u32[]{:S(2)}, u32[]{:S(2)}) collective-permute-start(bf16[3,256]{1,0:T(4,128)(2,1)} %slice_select_fusion.1), channel_id=1, source_target_pairs={{0,8},{8,16},{16,24},{24,32},{32,40},{40,48},{48,56},{56,64},{64,7... | collective-permute-start | bytes 4616 | tf_op jit(solution)/shard_map/ppermute | solution.py:17
  119.5 26.4 %collective-permute-start = (bf16[3,512]{1,0:T(4,128)(2,1)}, bf16[3,512]{1,0:T(4,128)(2,1)}, u32[]{:S(2)}, u32[]{:S(2)}) collective-permute-start(bf16[3,512]{1,0:T(4,128)(2,1)} %slice_select_fusion), channel_id=1, source_target_pairs={{0,8},{8,16},{16,24},{24,32},{32,40},{40,48},{48,56},{56,64},{64,7... | collective-permute-start | bytes 9224 | tf_op jit(solution)/shard_map/ppermute | solution.py:17
  153.9 9.3 %collective-permute-start.3 = (f32[8,65,128]{2,1,0:T(8,128)S(1)}, f32[8,65,128]{2,1,0:T(8,128)S(1)}, u32[]{:S(2)}, u32[]{:S(2)}) collective-permute-start(f32[8,65,128]{2,1,0:T(8,128)S(1)} %pad_maximum_fusion.3), channel_id=1, source_target_pairs={{8,0},{16,8},{24,16},{32,24},{40,32},{48,40},{56,48},{64,56},{72,6... | collective-permute-start | bytes 798728 | tf_op jit(solution)/shard_map/ppermute | solution.py:17
  158.3 9.3 %collective-permute-start.2 = (f32[8,65,128]{2,1,0:T(8,128)S(1)}, f32[8,65,128]{2,1,0:T(8,128)S(1)}, u32[]{:S(2)}, u32[]{:S(2)}) collective-permute-start(f32[8,65,128]{2,1,0:T(8,128)S(1)} %pad_maximum_fusion.2), channel_id=1, source_target_pairs={{0,8},{8,16},{16,24},{24,32},{32,40},{40,48},{48,56},{56,64},{64,7... | collective-permute-start | bytes 798728 | tf_op jit(solution)/shard_map/ppermute | solution.py:17
  173.0 18.5 %collective-permute-start.5 = (f32[8,65,128]{2,1,0:T(8,128)}, f32[8,65,128]{2,1,0:T(8,128)}, u32[]{:S(2)}, u32[]{:S(2)}) collective-permute-start(f32[8,65,128]{2,1,0:T(8,128)} %pad_maximum_fusion.5), channel_id=1, source_target_pairs={{16,0},{24,8},{32,16},{40,24},{48,32},{56,40},{64,48},{72,56},{80,... | collective-permute-start | bytes 798728 | tf_op jit(solution)/shard_map/ppermute | solution.py:17
  178.4 16.5 %collective-permute-start.4 = (f32[8,65,128]{2,1,0:T(8,128)}, f32[8,65,128]{2,1,0:T(8,128)}, u32[]{:S(2)}, u32[]{:S(2)}) collective-permute-start(f32[8,65,128]{2,1,0:T(8,128)} %pad_maximum_fusion.4), channel_id=1, source_target_pairs={{0,16},{8,24},{16,32},{24,40},{32,48},{40,56},{48,64},{56,72},{64,... | collective-permute-start | bytes 798728 | tf_op jit(solution)/shard_map/ppermute | solution.py:17
  195.9 49.3 %copy-start.19 = (f32[512,3]{0,1:T(4,128)S(1)}, f32[512,3]{0,1:T(4,128)}, u32[]{:S(2)}) copy-start(f32[512,3]{0,1:T(4,128)} %copy.140) | copy-start | bytes 18436
  200.6 20.4 %collective-permute-start.7 = (f32[8,65,128]{2,1,0:T(8,128)}, f32[8,65,128]{2,1,0:T(8,128)}, u32[]{:S(2)}, u32[]{:S(2)}) collective-permute-start(f32[8,65,128]{2,1,0:T(8,128)} %pad_maximum_fusion.7), channel_id=1, source_target_pairs={{32,0},{40,8},{48,16},{56,24},{64,32},{72,40},{80,48},{88,56},{96,... | collective-permute-start | bytes 798728 | tf_op jit(solution)/shard_map/ppermute | solution.py:17
  207.7 26.6 %collective-permute-start.6 = (f32[8,65,128]{2,1,0:T(8,128)}, f32[8,65,128]{2,1,0:T(8,128)}, u32[]{:S(2)}, u32[]{:S(2)}) collective-permute-start(f32[8,65,128]{2,1,0:T(8,128)} %pad_maximum_fusion.6), channel_id=1, source_target_pairs={{0,32},{8,40},{16,48},{24,56},{32,64},{40,72},{48,80},{56,88},{64,... | collective-permute-start | bytes 798728 | tf_op jit(solution)/shard_map/ppermute | solution.py:17
  239.2 21.7 %copy-start.24 = (f32[8,512]{1,0:T(8,128)S(1)}, f32[8,512]{1,0:T(8,128)}, u32[]{:S(2)}) copy-start(f32[8,512]{1,0:T(8,128)} %copy.118) | copy-start | bytes 49156
  239.2 21.7 %copy-start.25 = (f32[8,512]{1,0:T(8,128)S(1)}, f32[8,512]{1,0:T(8,128)}, u32[]{:S(2)}) copy-start(f32[8,512]{1,0:T(8,128)} %copy.116) | copy-start | bytes 49156
  240.0 8.6 %collective-permute-start.9 = (f32[8,65,128]{2,1,0:T(8,128)}, f32[8,65,128]{2,1,0:T(8,128)}, u32[]{:S(2)}, u32[]{:S(2)}) collective-permute-start(f32[8,65,128]{2,1,0:T(8,128)} %pad_maximum_fusion.9), channel_id=1, source_target_pairs={{64,0},{72,8},{80,16},{88,24},{96,32},{104,40},{112,48},{120,56},{... | collective-permute-start | bytes 798728 | tf_op jit(solution)/shard_map/ppermute | solution.py:17
  243.9 10.0 %collective-permute-start.8 = (f32[8,65,128]{2,1,0:T(8,128)}, f32[8,65,128]{2,1,0:T(8,128)}, u32[]{:S(2)}, u32[]{:S(2)}) collective-permute-start(f32[8,65,128]{2,1,0:T(8,128)} %pad_maximum_fusion.8), channel_id=1, source_target_pairs={{0,64},{8,72},{16,80},{24,88},{32,96},{40,104},{48,112},{56,120},{... | collective-permute-start | bytes 798728 | tf_op jit(solution)/shard_map/ppermute | solution.py:17
  257.4 13.3 %collective-permute-start.11 = (f32[8,65,128]{2,1,0:T(8,128)S(1)}, f32[8,65,128]{2,1,0:T(8,128)}, u32[]{:S(2)}, u32[]{:S(2)}) collective-permute-start(f32[8,65,128]{2,1,0:T(8,128)S(1)} %pad_maximum_fusion.11), channel_id=1, source_target_pairs={{128,0},{136,8},{144,16},{152,24},{160,32},{168,40},{176,48},{184,... | collective-permute-start | bytes 798728 | tf_op jit(solution)/shard_map/ppermute | solution.py:17
  269.4 10.6 %collective-permute-start.10 = (f32[8,65,128]{2,1,0:T(8,128)S(1)}, f32[8,65,128]{2,1,0:T(8,128)S(1)}, u32[]{:S(2)}, u32[]{:S(2)}) collective-permute-start(f32[8,65,128]{2,1,0:T(8,128)S(1)} %pad_maximum_fusion.10), channel_id=1, source_target_pairs={{0,128},{8,136},{16,144},{24,152},{32,160},{40,168},{48,176},{56,1... | collective-permute-start | bytes 798728 | tf_op jit(solution)/shard_map/ppermute | solution.py:17
  (51 other events, 424.6 us)
Sparse Core Ops, SparseCore 0:
  9.8 16.9 all-gather.1
  37.3 75.8 reduce-scatter.2
  140.9 46.7 reduce-scatter.4

commit v5 on v4

--- a/solution.py
+++ b/solution.py
@@ -117,7 +117,11 @@
     conv_x_edges,
     conv_bc_edges,
 ):
-    tokens = lax.all_gather(hidden, "row", axis=0, tiled=True)
+    other = lax.ppermute(hidden, "row", [(0, 1), (1, 0)])
+    row_first = lax.axis_index("row") == 0
+    tokens = jnp.concatenate(
+        [jnp.where(row_first, hidden, other), jnp.where(row_first, other, hidden)], axis=0
+    )
     rows_here = tokens.shape[0]
     channels = w_x.shape[2]
     heads_here = w_dt.shape[2]

time: 306 us -> 300 us (0.980)
  waiting for transfers between devices: 104 us -> 86.2 us
  other arithmetic: 61.4 us -> 66.3 us
    all_gather x1 -> x0, waiting for transfers between devices: 18.9 us -> none  [shards(): tokens = lax.all_gather(hidden, 'row', axis=0, tiled=True)]
    dot_general x4 -> x3, matrix products: 13.8 us -> 16.5 us  [shards(): jnp.einsum('td,dgc->gtc', tokens, weight, preferred_element_type=jnp.floa...]
  transfers between devices with their start and end apart: 15 -> 15, of which waited for: 10 -> 10; matrix products, arithmetic and copies ran while one was open for 38% -> 37% of each run, Pallas kernels for 0% -> 0%
where the time goes in v5:
time: 300 us; the launch traced here: 297 us
  waiting for transfers between devices  86.2 us (29%)
  other arithmetic  66.3 us (22%)
  matrix products  43.1 us (14%)
  starting transfers between devices  40 us (13%)
  local copies, waits for them, and re-layouts  35 us (12%)
  between operations  22.5 us (8%)
  blocking collectives  4.33 us (1%)
    reduce_scatter x1, waiting for transfers between devices, shards(): lax.psum_scatter(jnp.concatenate([x_part, bc_part, dt_part], axis=2), 'co...  43.8 us
    ppermute x12, waiting for transfers between devices, from_behind(): lax.ppermute(value, axis, [(source, source + steps) for source in range(f...  40.6 us
    ppermute x12, starting transfers between devices, from_behind(): lax.ppermute(value, axis, [(source, source + steps) for source in range(f...  39.1 us
    dot_general x3, matrix products, shards(): jnp.einsum('td,dgc->gtc', tokens, weight, preferred_element_type=jnp.floa...  16.5 us
    slice x13, local copies, waits for them, and re-layouts, unpack(): return (packed[:, p_n, 0], packed[:, :p_n], packed[0, p_n, n_n - 1])  11.1 us
    select_n x5, other arithmetic, near_far(): jnp.where(keep, near[1], far_a[:, None, None] * near[1] + far_b)  8.75 us
    dot_general x1, matrix products, local_terms(): jnp.einsum('hij,jhp->ihp', mixing, x_vals.astype(jnp.float32), precision=...  8.22 us
    dot_general x6, matrix products, convolve(): from_edge = jnp.dot(picker, table, preferred_element_type=jnp.float32)  7.41 us
  transfers between devices with their start and end apart: 15, of which 10 were waited for; matrix products, arithmetic and copies ran while one was open for 37% of the time, Pallas kernels for 0%

profile of v5, /device:TPU:71, one launch (start us, length us, event | category | flops | bytes accessed | tf_op | source)
XLA Modules:
  0.0 297.4 jit_solution(15451457012753214712)
XLA Ops:
  10.9 7.1 %fusion.20 = f32[4,512,512]{2,1,0:T(8,128)} fusion(bf16[1024,4,512]{2,1,0:T(4,128)(2,1)} %param.18, bf16[256,1024]{1,0:T(8,128)(2,1)S(1)} %get-tuple-element.114, bf16[256,1024]{1,0:T(8,128)(2,1)S(1)} %get-tuple-element.113), kind=kOutput, calls=%fused_computation.27 | convolution fusion | flops 2149580800 | bytes 9437184 | tf_op jit(solution)/shard_map/td,dgc->gtc/dot_general | solution.py:130
  17.9 2.6 fusion.30
  22.1 4.8 %pad_maximum_fusion = f32[4,512,776]{2,1,0:T(8,128)} fusion(f32[4,512,8]{2,1,0:T(8,128)S(1)} %bitcast.159, f32[4,512,256]{2,1,0:T(8,128)S(1)} %copy-done.10, f32[4,512,512]{2,1,0:T(8,128)} %fusion.20), kind=kLoop, calls=%fused_computation.12 | loop fusion | flops 3178496 | bytes 12713984 | tf_op jit(solution)/shard_map/concatenate | solution.py:134
  53.5 6.8 %fusion.23 = f32[4,512,512]{2,1,0:T(8,128)} fusion(bf16[1024,4,512]{2,1,0:T(4,128)(2,1)} %param.19, bf16[256,1024]{1,0:T(8,128)(2,1)S(1)} %copy-done.16, bf16[256,1024]{1,0:T(8,128)(2,1)S(1)} %copy-done.14), kind=kOutput, calls=%fused_computation.28 | convolution fusion | flops 2149580800 | bytes 9437184 | tf_op jit(solution)/shard_map/td,dgc->gtc/dot_general | solution.py:130
  60.3 43.8 %reduce-scatter.3.cloned.1.call-done = f32[1,512,776]{2,1,0:T(8,128)} async-done(((f32[4,512,776]{2,1,0:T(8,128)}), f32[1,512,776]{2,1,0:T(8,128)}) %reduce-scatter.3.cloned.1.call-update) | async-done | bytes 1589264 | tf_op jit(solution)/shard_map/reduce_scatter | solution.py:133
  114.9 3.2 %collective-permute-start.2 = (bf16[3,256]{1,0:T(4,128)(2,1)}, bf16[3,256]{1,0:T(4,128)(2,1)}, u32[]{:S(2)}, u32[]{:S(2)}) collective-permute-start(bf16[3,256]{1,0:T(4,128)(2,1)} %slice_select_fusion.1), channel_id=1, source_target_pairs={{0,8},{8,16},{16,24},{24,32},{32,40},{40,48},{48,56},{56,64},{64,7... | collective-permute-start | bytes 4616 | tf_op jit(solution)/shard_map/ppermute | solution.py:17
  119.5 4.5 %collective-permute-start.1 = (bf16[3,512]{1,0:T(4,128)(2,1)}, bf16[3,512]{1,0:T(4,128)(2,1)}, u32[]{:S(2)}, u32[]{:S(2)}) collective-permute-start(bf16[3,512]{1,0:T(4,128)(2,1)} %slice_select_fusion), channel_id=1, source_target_pairs={{0,8},{8,16},{16,24},{24,32},{32,40},{40,48},{48,56},{56,64},{64,7... | collective-permute-start | bytes 9224 | tf_op jit(solution)/shard_map/ppermute | solution.py:17
  143.5 3.0 %fusion.11 = f32[4,8,64,128]{3,2,1,0:T(8,128)S(1)} fusion(f32[512,8,64]{0,2,1:T(8,128)S(1)} %convert_element_type.190, f32[4,512,8]{1,2,0:T(8,128)} %select_multiply_fusion, bf16[512,256]{1,0:T(8,128)(2,1)S(1)} %multiply_convert_fusion.2), kind=kOutput, calls=%fused_computation.17 | convolution fusion | flops 1611661312 | bytes 2293760 | tf_op jit(solution)/shard_map/sthp,tn->shpn/dot_general | solution.py:55
  151.0 3.4 %collective-permute-start.3 = (f32[8,65,128]{2,1,0:T(8,128)S(1)}, f32[8,65,128]{2,1,0:T(8,128)S(1)}, u32[]{:S(2)}, u32[]{:S(2)}) collective-permute-start(f32[8,65,128]{2,1,0:T(8,128)S(1)} %pad_maximum_fusion.3), channel_id=1, source_target_pairs={{0,8},{8,16},{16,24},{24,32},{32,40},{40,48},{48,56},{56,64},{64,7... | collective-permute-start | bytes 798728 | tf_op jit(solution)/shard_map/ppermute | solution.py:17
  156.7 3.6 %collective-permute-done.3 = f32[8,65,128]{2,1,0:T(8,128)S(1)} collective-permute-done((f32[8,65,128]{2,1,0:T(8,128)S(1)}, f32[8,65,128]{2,1,0:T(8,128)S(1)}, u32[]{:S(2)}, u32[]{:S(2)}) %collective-permute-start.3) | collective-permute-done | bytes 266272 | tf_op jit(solution)/shard_map/ppermute | solution.py:17
  165.8 4.5 %collective-permute-start.6 = (f32[8,65,128]{2,1,0:T(8,128)}, f32[8,65,128]{2,1,0:T(8,128)}, u32[]{:S(2)}, u32[]{:S(2)}) collective-permute-start(f32[8,65,128]{2,1,0:T(8,128)} %pad_maximum_fusion.6), channel_id=1, source_target_pairs={{16,0},{24,8},{32,16},{40,24},{48,32},{56,40},{64,48},{72,56},{80,... | collective-permute-start | bytes 798728 | tf_op jit(solution)/shard_map/ppermute | solution.py:17
  171.2 2.8 collective-permute-start.5
  174.1 2.6 fusion.50
  176.7 7.5 %collective-permute-done.6 = f32[8,65,128]{2,1,0:T(8,128)} collective-permute-done((f32[8,65,128]{2,1,0:T(8,128)}, f32[8,65,128]{2,1,0:T(8,128)}, u32[]{:S(2)}, u32[]{:S(2)}) %collective-permute-start.6) | collective-permute-done | bytes 266272 | tf_op jit(solution)/shard_map/ppermute | solution.py:17
  193.3 6.2 %collective-permute-start.8 = (f32[8,65,128]{2,1,0:T(8,128)}, f32[8,65,128]{2,1,0:T(8,128)}, u32[]{:S(2)}, u32[]{:S(2)}) collective-permute-start(f32[8,65,128]{2,1,0:T(8,128)} %pad_maximum_fusion.8), channel_id=1, source_target_pairs={{32,0},{40,8},{48,16},{56,24},{64,32},{72,40},{80,48},{88,56},{96,... | collective-permute-start | bytes 798728 | tf_op jit(solution)/shard_map/ppermute | solution.py:17
  200.3 3.7 %collective-permute-start.7 = (f32[8,65,128]{2,1,0:T(8,128)}, f32[8,65,128]{2,1,0:T(8,128)}, u32[]{:S(2)}, u32[]{:S(2)}) collective-permute-start(f32[8,65,128]{2,1,0:T(8,128)} %pad_maximum_fusion.7), channel_id=1, source_target_pairs={{0,32},{8,40},{16,48},{24,56},{32,64},{40,72},{48,80},{56,88},{64,... | collective-permute-start | bytes 798728 | tf_op jit(solution)/shard_map/ppermute | solution.py:17
  206.3 7.4 %collective-permute-done.8 = f32[8,65,128]{2,1,0:T(8,128)} collective-permute-done((f32[8,65,128]{2,1,0:T(8,128)}, f32[8,65,128]{2,1,0:T(8,128)}, u32[]{:S(2)}, u32[]{:S(2)}) %collective-permute-start.8) | collective-permute-done | bytes 266272 | tf_op jit(solution)/shard_map/ppermute | solution.py:17
  217.2 10.0 %collective-permute-done.7 = f32[8,65,128]{2,1,0:T(8,128)} collective-permute-done((f32[8,65,128]{2,1,0:T(8,128)}, f32[8,65,128]{2,1,0:T(8,128)}, u32[]{:S(2)}, u32[]{:S(2)}) %collective-permute-start.7) | collective-permute-done | bytes 266272 | tf_op jit(solution)/shard_map/ppermute | solution.py:17
  233.0 2.8 collective-permute-start.10
  250.0 3.5 %collective-permute-start.12 = (f32[8,65,128]{2,1,0:T(8,128)S(1)}, f32[8,65,128]{2,1,0:T(8,128)}, u32[]{:S(2)}, u32[]{:S(2)}) collective-permute-start(f32[8,65,128]{2,1,0:T(8,128)S(1)} %pad_maximum_fusion.12), channel_id=1, source_target_pairs={{128,0},{136,8},{144,16},{152,24},{160,32},{168,40},{176,48},{184,... | collective-permute-start | bytes 798728 | tf_op jit(solution)/shard_map/ppermute | solution.py:17
  253.6 8.2 %fusion.38 = f32[512,8,64]{0,2,1:T(8,128)S(1)} fusion(bf16[512,8,64]{0,2,1:T(8,128)(2,1)} %bitcast.21, f32[8,512]{1,0:T(8,128)S(1)} %copy-done.29, f32[512,512]{1,0:T(8,128)} %fusion.76, f32[8,512]{1,0:T(8,128)S(1)} %copy-done.30, pred[512,512]{1,0:T(8,128)(4,1)} %fusion.49, f32[512,8,64]{0,2,1:T(8,128)} %bitcast.162, f32[512,8]{0,1:T(8,128)S(1)} %copy-done.28), kind=kOutput, calls=%fused_computation.38 | convolution fusion | flops 1621622784 | bytes 3981312 | tf_op jit(solution)/shard_map/hij,jhp->ihp/dot_general | solution.py:38
  265.9 6.6 %collective-permute-done.11 = f32[8,65,128]{2,1,0:T(8,128)S(1)} collective-permute-done((f32[8,65,128]{2,1,0:T(8,128)S(1)}, f32[8,65,128]{2,1,0:T(8,128)S(1)}, u32[]{:S(2)}, u32[]{:S(2)}) %collective-permute-start.11) | collective-permute-done | bytes 266272 | tf_op jit(solution)/shard_map/ppermute | solution.py:17
  272.7 2.7 fusion.37
  284.0 4.3 %psum.7 = f32[512]{0:T(512)S(1)} all-reduce(f32[512]{0:T(512)S(1)} %multiply_reduce_fusion), channel_id=1, replica_groups=mesh['seq'=32,'row'=2,'col'=4] {'row'}, use_global_device_ids=true, to_apply=%region_16.17 | all-reduce | flops 512 | bytes 4096 | tf_op jit(solution)/shard_map/psum | solution.py:255
  (305 shorter events, 119.1 us)
Async XLA Ops:
  7.2 96.9 %reduce-scatter.3.cloned.1.call-start = ((), (), s32[]{:S(2)}) async-start(), calls=%async_computation.2 | async-start | bytes 9175040 | tf_op jit(solution)/shard_map/reduce_scatter | solution.py:133
  7.2 2.5 collective-permute-start
  26.9 21.5 %copy-start.36 = (bf16[4,1,256]{2,0,1:T(4,128)(2,1)S(1)}, bf16[4,1,256]{2,0,1:T(4,128)(2,1)}, u32[]{:S(2)}) copy-start(bf16[4,1,256]{2,0,1:T(4,128)(2,1)} %param.23) | copy-start | bytes 6148
  27.0 22.1 %copy-start.31 = (bf16[4,1,512]{2,0,1:T(4,128)(2,1)S(1)}, bf16[4,1,512]{2,0,1:T(4,128)(2,1)}, u32[]{:S(2)}) copy-start(bf16[4,1,512]{2,0,1:T(4,128)(2,1)} %param.22) | copy-start | bytes 12292
  27.0 26.5 %copy-start.14 = (bf16[256,1024]{1,0:T(8,128)(2,1)S(1)}, bf16[256,1024]{1,0:T(8,128)(2,1)}, u32[]{:S(2)}) copy-start(bf16[256,1024]{1,0:T(8,128)(2,1)} %copy-done.13) | copy-start | bytes 1572868
  27.0 26.5 %copy-start.16 = (bf16[256,1024]{1,0:T(8,128)(2,1)S(1)}, bf16[256,1024]{1,0:T(8,128)(2,1)}, u32[]{:S(2)}) copy-start(bf16[256,1024]{1,0:T(8,128)(2,1)} %copy-done.15) | copy-start | bytes 1572868
  27.0 253.4 %reduce-scatter.5.cloned.1.call-start = ((), (), s32[]{:S(2)}) async-start(), calls=%async_computation.3 | async-start | bytes 5242880 | tf_op jit(solution)/shard_map/reduce_scatter | solution.py:138
  34.0 26.3 %copy-start.20 = (bf16[9,256]{1,0:T(8,128)(2,1)}, bf16[9,256]{1,0:T(8,128)(2,1)S(1)}, u32[]{:S(2)}) copy-start(bf16[9,256]{1,0:T(8,128)(2,1)S(1)} %reshape_squeeze.7) | copy-start | bytes 13828
  105.7 29.4 %copy-start.2 = (bf16[512,776]{1,0:T(8,128)(2,1)}, bf16[512,776]{1,0:T(8,128)(2,1)S(1)}, u32[]{:S(2)}) copy-start(bf16[512,776]{1,0:T(8,128)(2,1)S(1)} %convert_bitcast_fusion) | copy-start | bytes 2383876
  114.9 21.5 %collective-permute-start.2 = (bf16[3,256]{1,0:T(4,128)(2,1)}, bf16[3,256]{1,0:T(4,128)(2,1)}, u32[]{:S(2)}, u32[]{:S(2)}) collective-permute-start(bf16[3,256]{1,0:T(4,128)(2,1)} %slice_select_fusion.1), channel_id=1, source_target_pairs={{0,8},{8,16},{16,24},{24,32},{32,40},{40,48},{48,56},{56,64},{64,7... | collective-permute-start | bytes 4616 | tf_op jit(solution)/shard_map/ppermute | solution.py:17
  119.5 19.1 %collective-permute-start.1 = (bf16[3,512]{1,0:T(4,128)(2,1)}, bf16[3,512]{1,0:T(4,128)(2,1)}, u32[]{:S(2)}, u32[]{:S(2)}) collective-permute-start(bf16[3,512]{1,0:T(4,128)(2,1)} %slice_select_fusion), channel_id=1, source_target_pairs={{0,8},{8,16},{16,24},{24,32},{32,40},{40,48},{48,56},{56,64},{64,7... | collective-permute-start | bytes 9224 | tf_op jit(solution)/shard_map/ppermute | solution.py:17
  146.6 9.4 %collective-permute-start.4 = (f32[8,65,128]{2,1,0:T(8,128)S(1)}, f32[8,65,128]{2,1,0:T(8,128)S(1)}, u32[]{:S(2)}, u32[]{:S(2)}) collective-permute-start(f32[8,65,128]{2,1,0:T(8,128)S(1)} %pad_maximum_fusion.4), channel_id=1, source_target_pairs={{8,0},{16,8},{24,16},{32,24},{40,32},{48,40},{56,48},{64,56},{72,6... | collective-permute-start | bytes 798728 | tf_op jit(solution)/shard_map/ppermute | solution.py:17
  151.0 9.4 %collective-permute-start.3 = (f32[8,65,128]{2,1,0:T(8,128)S(1)}, f32[8,65,128]{2,1,0:T(8,128)S(1)}, u32[]{:S(2)}, u32[]{:S(2)}) collective-permute-start(f32[8,65,128]{2,1,0:T(8,128)S(1)} %pad_maximum_fusion.3), channel_id=1, source_target_pairs={{0,8},{8,16},{16,24},{24,32},{32,40},{40,48},{48,56},{56,64},{64,7... | collective-permute-start | bytes 798728 | tf_op jit(solution)/shard_map/ppermute | solution.py:17
  165.8 18.4 %collective-permute-start.6 = (f32[8,65,128]{2,1,0:T(8,128)}, f32[8,65,128]{2,1,0:T(8,128)}, u32[]{:S(2)}, u32[]{:S(2)}) collective-permute-start(f32[8,65,128]{2,1,0:T(8,128)} %pad_maximum_fusion.6), channel_id=1, source_target_pairs={{16,0},{24,8},{32,16},{40,24},{48,32},{56,40},{64,48},{72,56},{80,... | collective-permute-start | bytes 798728 | tf_op jit(solution)/shard_map/ppermute | solution.py:17
  171.2 16.3 %collective-permute-start.5 = (f32[8,65,128]{2,1,0:T(8,128)}, f32[8,65,128]{2,1,0:T(8,128)}, u32[]{:S(2)}, u32[]{:S(2)}) collective-permute-start(f32[8,65,128]{2,1,0:T(8,128)} %pad_maximum_fusion.5), channel_id=1, source_target_pairs={{0,16},{8,24},{16,32},{24,40},{32,48},{40,56},{48,64},{56,72},{64,... | collective-permute-start | bytes 798728 | tf_op jit(solution)/shard_map/ppermute | solution.py:17
  188.5 49.4 %copy-start.24 = (f32[512,3]{0,1:T(4,128)S(1)}, f32[512,3]{0,1:T(4,128)}, u32[]{:S(2)}) copy-start(f32[512,3]{0,1:T(4,128)} %copy.139) | copy-start | bytes 18436
  193.3 20.4 %collective-permute-start.8 = (f32[8,65,128]{2,1,0:T(8,128)}, f32[8,65,128]{2,1,0:T(8,128)}, u32[]{:S(2)}, u32[]{:S(2)}) collective-permute-start(f32[8,65,128]{2,1,0:T(8,128)} %pad_maximum_fusion.8), channel_id=1, source_target_pairs={{32,0},{40,8},{48,16},{56,24},{64,32},{72,40},{80,48},{88,56},{96,... | collective-permute-start | bytes 798728 | tf_op jit(solution)/shard_map/ppermute | solution.py:17
  200.3 27.0 %collective-permute-start.7 = (f32[8,65,128]{2,1,0:T(8,128)}, f32[8,65,128]{2,1,0:T(8,128)}, u32[]{:S(2)}, u32[]{:S(2)}) collective-permute-start(f32[8,65,128]{2,1,0:T(8,128)} %pad_maximum_fusion.7), channel_id=1, source_target_pairs={{0,32},{8,40},{16,48},{24,56},{32,64},{40,72},{48,80},{56,88},{64,... | collective-permute-start | bytes 798728 | tf_op jit(solution)/shard_map/ppermute | solution.py:17
  232.2 21.3 %copy-start.29 = (f32[8,512]{1,0:T(8,128)S(1)}, f32[8,512]{1,0:T(8,128)}, u32[]{:S(2)}) copy-start(f32[8,512]{1,0:T(8,128)} %copy.119) | copy-start | bytes 49156
  232.2 21.3 %copy-start.30 = (f32[8,512]{1,0:T(8,128)S(1)}, f32[8,512]{1,0:T(8,128)}, u32[]{:S(2)}) copy-start(f32[8,512]{1,0:T(8,128)} %copy.117) | copy-start | bytes 49156
  233.0 8.2 %collective-permute-start.10 = (f32[8,65,128]{2,1,0:T(8,128)}, f32[8,65,128]{2,1,0:T(8,128)}, u32[]{:S(2)}, u32[]{:S(2)}) collective-permute-start(f32[8,65,128]{2,1,0:T(8,128)} %pad_maximum_fusion.10), channel_id=1, source_target_pairs={{64,0},{72,8},{80,16},{88,24},{96,32},{104,40},{112,48},{120,56},{... | collective-permute-start | bytes 798728 | tf_op jit(solution)/shard_map/ppermute | solution.py:17
  236.6 10.0 %collective-permute-start.9 = (f32[8,65,128]{2,1,0:T(8,128)}, f32[8,65,128]{2,1,0:T(8,128)}, u32[]{:S(2)}, u32[]{:S(2)}) collective-permute-start(f32[8,65,128]{2,1,0:T(8,128)} %pad_maximum_fusion.9), channel_id=1, source_target_pairs={{0,64},{8,72},{16,80},{24,88},{32,96},{40,104},{48,112},{56,120},{... | collective-permute-start | bytes 798728 | tf_op jit(solution)/shard_map/ppermute | solution.py:17
  250.0 13.2 %collective-permute-start.12 = (f32[8,65,128]{2,1,0:T(8,128)S(1)}, f32[8,65,128]{2,1,0:T(8,128)}, u32[]{:S(2)}, u32[]{:S(2)}) collective-permute-start(f32[8,65,128]{2,1,0:T(8,128)S(1)} %pad_maximum_fusion.12), channel_id=1, source_target_pairs={{128,0},{136,8},{144,16},{152,24},{160,32},{168,40},{176,48},{184,... | collective-permute-start | bytes 798728 | tf_op jit(solution)/shard_map/ppermute | solution.py:17
  262.0 10.6 %collective-permute-start.11 = (f32[8,65,128]{2,1,0:T(8,128)S(1)}, f32[8,65,128]{2,1,0:T(8,128)S(1)}, u32[]{:S(2)}, u32[]{:S(2)}) collective-permute-start(f32[8,65,128]{2,1,0:T(8,128)S(1)} %pad_maximum_fusion.11), channel_id=1, source_target_pairs={{0,128},{8,136},{16,144},{24,152},{32,160},{40,168},{48,176},{56,1... | collective-permute-start | bytes 798728 | tf_op jit(solution)/shard_map/ppermute | solution.py:17
  (52 other events, 411.7 us)
Sparse Core Ops, SparseCore 0:
  27.1 76.9 reduce-scatter.2
  133.6 46.6 reduce-scatter.4

commit v6 on v5

--- a/solution.py
+++ b/solution.py
@@ -126,9 +126,12 @@
     channels = w_x.shape[2]
     heads_here = w_dt.shape[2]
     lagged = conv_x_w.shape[0] - 1
+    row_at = lax.axis_index("row")
+    bc_cols = w_bc.shape[2] // lax.axis_size("row")
+    w_bc_mine = lax.dynamic_slice_in_dim(w_bc, row_at * bc_cols, bc_cols, axis=2)
     x_part, z_part, bc_part, dt_part = [
         jnp.einsum("td,dgc->gtc", tokens, weight, preferred_element_type=jnp.float32)
-        for weight in (w_x, w_z, w_bc, w_dt)
+        for weight in (w_x, w_z, w_bc_mine, w_dt)
     ]
     first = lax.psum_scatter(
         jnp.concatenate([x_part, bc_part, dt_part], axis=2), "col", scatter_dimension=0, tiled=True
@@ -138,8 +141,12 @@
         lax.psum_scatter(z_part, "col", scatter_dimension=0, tiled=True)[0].astype(jnp.bfloat16)
     )
     x_raw = first[:, :channels]
-    bc_raw = first[:, channels : channels + 2 * N]
-    dt_raw = first[:, channels + 2 * N :]
+    bc_mine = first[:, channels : channels + bc_cols]
+    bc_other = lax.ppermute(bc_mine, "row", [(0, 1), (1, 0)])
+    bc_raw = jnp.concatenate(
+        [jnp.where(row_first, bc_mine, bc_other), jnp.where(row_first, bc_other, bc_mine)], axis=1
+    )
+    dt_raw = first[:, channels + bc_cols :]
     positions = jnp.arange(rows_here, dtype=jnp.int32)
     flag_vals = starts == 1
     segment = jnp.cumsum(starts)

time: 300 us -> 285 us (0.950)
  other arithmetic: 66.3 us -> 61.2 us
  matrix products: 43.1 us -> 38.5 us
  waiting for transfers between devices: 86.2 us -> 82.3 us
    dot_general x3, matrix products: 16.5 us -> 11.9 us  [shards(): jnp.einsum('td,dgc->gtc', tokens, weight, preferred_element_type=jnp.floa...]
    reduce_scatter x1, waiting for transfers between devices: 43.8 us -> 39.5 us  [shards(): lax.psum_scatter(jnp.concatenate([x_part, bc_part, dt_part], axis=2), 'co...]
  transfers between devices with their start and end apart: 15 -> 16, of which waited for: 10 -> 10; matrix products, arithmetic and copies ran while one was open for 37% -> 37% of each run, Pallas kernels for 0% -> 0%
where the time goes in v6:
time: 285 us; the launch traced here: 283 us
  waiting for transfers between devices  82.3 us (29%)
  other arithmetic  61.2 us (21%)
  starting transfers between devices  40.5 us (14%)
  matrix products  38.5 us (14%)
  local copies, waits for them, and re-layouts  33.7 us (12%)
  between operations  22.2 us (8%)
  blocking collectives  4.34 us (2%)
    ppermute x12, waiting for transfers between devices, from_behind(): lax.ppermute(value, axis, [(source, source + steps) for source in range(f...  42.1 us
    reduce_scatter x1, waiting for transfers between devices, shards(): lax.psum_scatter(jnp.concatenate([x_part, bc_part, dt_part], axis=2), 'co...  39.5 us
    ppermute x12, starting transfers between devices, from_behind(): lax.ppermute(value, axis, [(source, source + steps) for source in range(f...  38.8 us
    dot_general x3, matrix products, shards(): jnp.einsum('td,dgc->gtc', tokens, weight, preferred_element_type=jnp.floa...  11.9 us
    slice x13, local copies, waits for them, and re-layouts, unpack(): return (packed[:, p_n, 0], packed[:, :p_n], packed[0, p_n, n_n - 1])  11 us
    dot_general x6, matrix products, convolve(): from_edge = jnp.dot(picker, table, preferred_element_type=jnp.float32)  9.17 us
    dot_general x1, matrix products, local_terms(): jnp.einsum('hij,jhp->ihp', mixing, x_vals.astype(jnp.float32), precision=...  8.26 us
    select_n x5, other arithmetic, near_far(): jnp.where(keep, near[1], far_a[:, None, None] * near[1] + far_b)  7.71 us
  transfers between devices with their start and end apart: 16, of which 10 were waited for; matrix products, arithmetic and copies ran while one was open for 37% of the time, Pallas kernels for 0%

profile of v6, /device:TPU:71, one launch (start us, length us, event | category | flops | bytes accessed | tf_op | source)
XLA Modules:
  0.0 282.7 jit_solution(649912298680880907)
XLA Ops:
  11.9 4.5 %fusion.20 = f32[4,512,512]{2,1,0:T(8,128)} fusion(bf16[1024,4,512]{2,1,0:T(4,128)(2,1)S(1)} %copy-done.53, bf16[256,1024]{1,0:T(8,128)(2,1)S(1)} %get-tuple-element.114, bf16[256,1024]{1,0:T(8,128)(2,1)S(1)} %get-tuple-element.113), kind=kOutput, calls=%fused_computation.27 | convolution fusion | flops 2149580800 | bytes 9437184 | tf_op jit(solution)/shard_map/td,dgc->gtc/dot_general | solution.py:133
  17.2 5.4 %pad_maximum_fusion = f32[4,512,648]{2,1,0:T(8,128)} fusion(f32[4,512,8]{2,1,0:T(8,128)S(1)} %bitcast.163, f32[4,512,128]{2,1,0:T(8,128)S(1)} %convolution_bitcast_fusion, f32[4,512,512]{2,1,0:T(8,128)} %fusion.20), kind=kLoop, calls=%fused_computation.12 | loop fusion | flops 2654208 | bytes 10616832 | tf_op jit(solution)/shard_map/concatenate | solution.py:137
  45.1 6.7 %fusion.23 = f32[4,512,512]{2,1,0:T(8,128)} fusion(bf16[1024,4,512]{2,1,0:T(4,128)(2,1)} %param.19, bf16[256,1024]{1,0:T(8,128)(2,1)S(1)} %copy-done.16, bf16[256,1024]{1,0:T(8,128)(2,1)S(1)} %copy-done.14), kind=kOutput, calls=%fused_computation.28 | convolution fusion | flops 2149580800 | bytes 9437184 | tf_op jit(solution)/shard_map/td,dgc->gtc/dot_general | solution.py:133
  51.8 39.5 %reduce-scatter.3.cloned.1.call-done = f32[1,512,648]{2,1,0:T(8,128)} async-done(((f32[4,512,648]{2,1,0:T(8,128)}), f32[1,512,648]{2,1,0:T(8,128)}) %reduce-scatter.3.cloned.1.call-update) | async-done | bytes 1327120 | tf_op jit(solution)/shard_map/reduce_scatter | solution.py:136
  100.4 3.4 %collective-permute-start.1 = (bf16[3,512]{1,0:T(4,128)(2,1)}, bf16[3,512]{1,0:T(4,128)(2,1)}, u32[]{:S(2)}, u32[]{:S(2)}) collective-permute-start(bf16[3,512]{1,0:T(4,128)(2,1)} %slice_select_fusion), channel_id=1, source_target_pairs={{0,8},{8,16},{16,24},{24,32},{32,40},{40,48},{48,56},{56,64},{64,7... | collective-permute-start | bytes 9224 | tf_op jit(solution)/shard_map/ppermute | solution.py:17
  116.4 4.4 %collective-permute-start.3 = (bf16[3,256]{1,0:T(4,128)(2,1)S(1)}, bf16[3,256]{1,0:T(4,128)(2,1)S(1)}, u32[]{:S(2)}, u32[]{:S(2)}) collective-permute-start(bf16[3,256]{1,0:T(4,128)(2,1)S(1)} %fusion.77), channel_id=1, source_target_pairs={{0,8},{8,16},{16,24},{24,32},{32,40},{40,48},{48,56},{56,64},{64,7... | collective-permute-start | bytes 4616 | tf_op jit(solution)/shard_map/ppermute | solution.py:17
  120.9 4.2 %multiply_convert_fusion.1 = bf16[512,512]{1,0:T(8,128)(2,1)} fusion(f32[512,512]{1,0:T(8,128)S(1)} %fusion.57, f32[512,512]{1,0:T(8,128)S(1)} %fusion.59, bf16[512,512]{1,0:T(8,128)(2,1)} %slice.205, bf16[3,512]{1,0:T(4,128)(2,1)} %collective-permute-done.1, f32[512]{0:T(512)} %bitcast.188, f32[512]{0:T(512)} %bitcast.189, f32[512]{0:T(512)} %bitcast.187, ...), kind=kOutput, calls=%fused_computation.54 | convolution fusion | flops 12325376 | bytes 3171840 | tf_op jit(solution)/shard_map/dot_general | solution.py:93
  136.0 3.4 %collective-permute-start.4 = (f32[8,65,128]{2,1,0:T(8,128)S(1)}, f32[8,65,128]{2,1,0:T(8,128)S(1)}, u32[]{:S(2)}, u32[]{:S(2)}) collective-permute-start(f32[8,65,128]{2,1,0:T(8,128)S(1)} %pad_maximum_fusion.4), channel_id=1, source_target_pairs={{0,8},{8,16},{16,24},{24,32},{32,40},{40,48},{48,56},{56,64},{64,7... | collective-permute-start | bytes 798728 | tf_op jit(solution)/shard_map/ppermute | solution.py:17
  142.5 3.6 %collective-permute-done.4 = f32[8,65,128]{2,1,0:T(8,128)S(1)} collective-permute-done((f32[8,65,128]{2,1,0:T(8,128)S(1)}, f32[8,65,128]{2,1,0:T(8,128)S(1)}, u32[]{:S(2)}, u32[]{:S(2)}) %collective-permute-start.4) | collective-permute-done | bytes 266272 | tf_op jit(solution)/shard_map/ppermute | solution.py:17
  150.3 4.9 %collective-permute-start.7 = (f32[8,65,128]{2,1,0:T(8,128)}, f32[8,65,128]{2,1,0:T(8,128)}, u32[]{:S(2)}, u32[]{:S(2)}) collective-permute-start(f32[8,65,128]{2,1,0:T(8,128)} %pad_maximum_fusion.7), channel_id=1, source_target_pairs={{16,0},{24,8},{32,16},{40,24},{48,32},{56,40},{64,48},{72,56},{80,... | collective-permute-start | bytes 798728 | tf_op jit(solution)/shard_map/ppermute | solution.py:17
  156.1 2.6 collective-permute-start.6
  158.7 2.6 fusion.46
  161.3 7.9 %collective-permute-done.7 = f32[8,65,128]{2,1,0:T(8,128)} collective-permute-done((f32[8,65,128]{2,1,0:T(8,128)}, f32[8,65,128]{2,1,0:T(8,128)}, u32[]{:S(2)}, u32[]{:S(2)}) %collective-permute-start.7) | collective-permute-done | bytes 266272 | tf_op jit(solution)/shard_map/ppermute | solution.py:17
  178.3 6.0 %collective-permute-start.9 = (f32[8,65,128]{2,1,0:T(8,128)}, f32[8,65,128]{2,1,0:T(8,128)}, u32[]{:S(2)}, u32[]{:S(2)}) collective-permute-start(f32[8,65,128]{2,1,0:T(8,128)} %pad_maximum_fusion.9), channel_id=1, source_target_pairs={{32,0},{40,8},{48,16},{56,24},{64,32},{72,40},{80,48},{88,56},{96,... | collective-permute-start | bytes 798728 | tf_op jit(solution)/shard_map/ppermute | solution.py:17
  185.2 3.9 %collective-permute-start.8 = (f32[8,65,128]{2,1,0:T(8,128)}, f32[8,65,128]{2,1,0:T(8,128)}, u32[]{:S(2)}, u32[]{:S(2)}) collective-permute-start(f32[8,65,128]{2,1,0:T(8,128)} %pad_maximum_fusion.8), channel_id=1, source_target_pairs={{0,32},{8,40},{16,48},{24,56},{32,64},{40,72},{48,80},{56,88},{64,... | collective-permute-start | bytes 798728 | tf_op jit(solution)/shard_map/ppermute | solution.py:17
  189.0 2.3 fusion.70
  191.3 7.4 %collective-permute-done.9 = f32[8,65,128]{2,1,0:T(8,128)} collective-permute-done((f32[8,65,128]{2,1,0:T(8,128)}, f32[8,65,128]{2,1,0:T(8,128)}, u32[]{:S(2)}, u32[]{:S(2)}) %collective-permute-start.9) | collective-permute-done | bytes 266272 | tf_op jit(solution)/shard_map/ppermute | solution.py:17
  202.1 10.4 %collective-permute-done.8 = f32[8,65,128]{2,1,0:T(8,128)} collective-permute-done((f32[8,65,128]{2,1,0:T(8,128)}, f32[8,65,128]{2,1,0:T(8,128)}, u32[]{:S(2)}, u32[]{:S(2)}) %collective-permute-start.8) | collective-permute-done | bytes 266272 | tf_op jit(solution)/shard_map/ppermute | solution.py:17
  218.2 2.4 collective-permute-start.11
  235.5 3.5 %collective-permute-start.13 = (f32[8,65,128]{2,1,0:T(8,128)}, f32[8,65,128]{2,1,0:T(8,128)}, u32[]{:S(2)}, u32[]{:S(2)}) collective-permute-start(f32[8,65,128]{2,1,0:T(8,128)} %pad_maximum_fusion.13), channel_id=1, source_target_pairs={{128,0},{136,8},{144,16},{152,24},{160,32},{168,40},{176,48},{184,... | collective-permute-start | bytes 798728 | tf_op jit(solution)/shard_map/ppermute | solution.py:17
  239.0 8.3 %fusion.33 = f32[512,8,64]{0,2,1:T(8,128)S(1)} fusion(bf16[512,8,64]{0,2,1:T(8,128)(2,1)} %bitcast.160, f32[8,512]{1,0:T(8,128)S(1)} %copy-done.24, f32[512,512]{1,0:T(8,128)} %fusion.70, f32[8,512]{1,0:T(8,128)S(1)} %copy-done.25, pred[512,512]{1,0:T(8,128)(4,1)} %fusion.45, f32[512,8,64]{0,2,1:T(8,128)} %bitcast.165, f32[512,8]{0,1:T(8,128)S(1)} %copy-done.23), kind=kOutput, calls=%fused_computation.36 | convolution fusion | flops 1621622784 | bytes 3981312 | tf_op jit(solution)/shard_map/hij,jhp->ihp/dot_general | solution.py:38
  252.1 6.8 %collective-permute-done.12 = f32[8,65,128]{2,1,0:T(8,128)S(1)} collective-permute-done((f32[8,65,128]{2,1,0:T(8,128)}, f32[8,65,128]{2,1,0:T(8,128)S(1)}, u32[]{:S(2)}, u32[]{:S(2)}) %collective-permute-start.12) | collective-permute-done | bytes 266272 | tf_op jit(solution)/shard_map/ppermute | solution.py:17
  269.3 4.3 %psum.7 = f32[512]{0:T(512)S(1)} all-reduce(f32[512]{0:T(512)S(1)} %multiply_reduce_fusion), channel_id=1, replica_groups=mesh['seq'=32,'row'=2,'col'=4] {'row'}, use_global_device_ids=true, to_apply=%region_16.17 | all-reduce | flops 512 | bytes 4096 | tf_op jit(solution)/shard_map/psum | solution.py:262
  273.6 2.2 fusion.51
  (299 shorter events, 110.0 us)
Async XLA Ops:
  7.2 84.1 %reduce-scatter.3.cloned.1.call-start = ((), (), s32[]{:S(2)}) async-start(), calls=%async_computation.2 | async-start | bytes 7864320 | tf_op jit(solution)/shard_map/reduce_scatter | solution.py:136
  7.2 2.5 collective-permute-start
  22.7 22.4 %copy-start.14 = (bf16[256,1024]{1,0:T(8,128)(2,1)S(1)}, bf16[256,1024]{1,0:T(8,128)(2,1)}, u32[]{:S(2)}) copy-start(bf16[256,1024]{1,0:T(8,128)(2,1)} %copy-done.13) | copy-start | bytes 1572868
  22.7 22.4 %copy-start.16 = (bf16[256,1024]{1,0:T(8,128)(2,1)S(1)}, bf16[256,1024]{1,0:T(8,128)(2,1)}, u32[]{:S(2)}) copy-start(bf16[256,1024]{1,0:T(8,128)(2,1)} %copy-done.15) | copy-start | bytes 1572868
  22.7 243.0 %reduce-scatter.5.cloned.1.call-start = ((), (), s32[]{:S(2)}) async-start(), calls=%async_computation.3 | async-start | bytes 5242880 | tf_op jit(solution)/shard_map/reduce_scatter | solution.py:141
  34.2 65.6 %copy-start.32 = (pred[3]{0:T(512)(128)(4,1)}, pred[3]{0:T(512)(128)(4,1)S(1)}, u32[]{:S(2)}) copy-start(pred[3]{0:T(512)(128)(4,1)S(1)} %add_compare_fusion) | copy-start | bytes 13
  45.1 49.2 %copy-start.30 = (f32[1,8]{1,0:T(1,128)S(1)}, f32[1,8]{1,0:T(1,128)}, u32[]{:S(2)}) copy-start(f32[1,8]{1,0:T(1,128)} %param.26) | copy-start | bytes 100
  45.1 49.2 %copy-start.31 = (f32[1,8]{1,0:T(1,128)S(1)}, f32[1,8]{1,0:T(1,128)}, u32[]{:S(2)}) copy-start(f32[1,8]{1,0:T(1,128)} %param.27) | copy-start | bytes 100
  51.8 52.0 %copy-start.52 = (pred[4]{0:T(512)(128)(4,1)S(1)}, pred[4]{0:T(512)(128)(4,1)}, u32[]{:S(2)}) copy-start(pred[4]{0:T(512)(128)(4,1)} %broadcast_compare_fusion.6) | copy-start | bytes 16
  98.9 15.8 %collective-permute-start.2 = (bf16[512,128]{1,0:T(8,128)(2,1)}, bf16[512,128]{1,0:T(8,128)(2,1)}, u32[]{:S(2)}, u32[]{:S(2)}) collective-permute-start(bf16[512,128]{1,0:T(8,128)(2,1)} %slice.225), channel_id=1, source_target_pairs={{0,4},{4,0},{1,5},{5,1},{2,6},{6,2},{3,7},{7,3},{8,12},{12,8},{9,1... | collective-permute-start | bytes 393224 | tf_op jit(solution)/shard_map/ppermute | solution.py:145
  100.4 20.4 %collective-permute-start.1 = (bf16[3,512]{1,0:T(4,128)(2,1)}, bf16[3,512]{1,0:T(4,128)(2,1)}, u32[]{:S(2)}, u32[]{:S(2)}) collective-permute-start(bf16[3,512]{1,0:T(4,128)(2,1)} %slice_select_fusion), channel_id=1, source_target_pairs={{0,8},{8,16},{16,24},{24,32},{32,40},{40,48},{48,56},{56,64},{64,7... | collective-permute-start | bytes 9224 | tf_op jit(solution)/shard_map/ppermute | solution.py:17
  116.4 10.0 %collective-permute-start.3 = (bf16[3,256]{1,0:T(4,128)(2,1)S(1)}, bf16[3,256]{1,0:T(4,128)(2,1)S(1)}, u32[]{:S(2)}, u32[]{:S(2)}) collective-permute-start(bf16[3,256]{1,0:T(4,128)(2,1)S(1)} %fusion.77), channel_id=1, source_target_pairs={{0,8},{8,16},{16,24},{24,32},{32,40},{40,48},{48,56},{56,64},{64,7... | collective-permute-start | bytes 4616 | tf_op jit(solution)/shard_map/ppermute | solution.py:17
  131.6 10.0 %collective-permute-start.5 = (f32[8,65,128]{2,1,0:T(8,128)S(1)}, f32[8,65,128]{2,1,0:T(8,128)S(1)}, u32[]{:S(2)}, u32[]{:S(2)}) collective-permute-start(f32[8,65,128]{2,1,0:T(8,128)S(1)} %pad_maximum_fusion.5), channel_id=1, source_target_pairs={{8,0},{16,8},{24,16},{32,24},{40,32},{48,40},{56,48},{64,56},{72,6... | collective-permute-start | bytes 798728 | tf_op jit(solution)/shard_map/ppermute | solution.py:17
  136.0 10.0 %collective-permute-start.4 = (f32[8,65,128]{2,1,0:T(8,128)S(1)}, f32[8,65,128]{2,1,0:T(8,128)S(1)}, u32[]{:S(2)}, u32[]{:S(2)}) collective-permute-start(f32[8,65,128]{2,1,0:T(8,128)S(1)} %pad_maximum_fusion.4), channel_id=1, source_target_pairs={{0,8},{8,16},{16,24},{24,32},{32,40},{40,48},{48,56},{56,64},{64,7... | collective-permute-start | bytes 798728 | tf_op jit(solution)/shard_map/ppermute | solution.py:17
  150.3 18.9 %collective-permute-start.7 = (f32[8,65,128]{2,1,0:T(8,128)}, f32[8,65,128]{2,1,0:T(8,128)}, u32[]{:S(2)}, u32[]{:S(2)}) collective-permute-start(f32[8,65,128]{2,1,0:T(8,128)} %pad_maximum_fusion.7), channel_id=1, source_target_pairs={{16,0},{24,8},{32,16},{40,24},{48,32},{56,40},{64,48},{72,56},{80,... | collective-permute-start | bytes 798728 | tf_op jit(solution)/shard_map/ppermute | solution.py:17
  156.1 16.5 %collective-permute-start.6 = (f32[8,65,128]{2,1,0:T(8,128)}, f32[8,65,128]{2,1,0:T(8,128)}, u32[]{:S(2)}, u32[]{:S(2)}) collective-permute-start(f32[8,65,128]{2,1,0:T(8,128)} %pad_maximum_fusion.6), channel_id=1, source_target_pairs={{0,16},{8,24},{16,32},{24,40},{32,48},{40,56},{48,64},{56,72},{64,... | collective-permute-start | bytes 798728 | tf_op jit(solution)/shard_map/ppermute | solution.py:17
  178.3 20.4 %collective-permute-start.9 = (f32[8,65,128]{2,1,0:T(8,128)}, f32[8,65,128]{2,1,0:T(8,128)}, u32[]{:S(2)}, u32[]{:S(2)}) collective-permute-start(f32[8,65,128]{2,1,0:T(8,128)} %pad_maximum_fusion.9), channel_id=1, source_target_pairs={{32,0},{40,8},{48,16},{56,24},{64,32},{72,40},{80,48},{88,56},{96,... | collective-permute-start | bytes 798728 | tf_op jit(solution)/shard_map/ppermute | solution.py:17
  185.2 27.3 %collective-permute-start.8 = (f32[8,65,128]{2,1,0:T(8,128)}, f32[8,65,128]{2,1,0:T(8,128)}, u32[]{:S(2)}, u32[]{:S(2)}) collective-permute-start(f32[8,65,128]{2,1,0:T(8,128)} %pad_maximum_fusion.8), channel_id=1, source_target_pairs={{0,32},{8,40},{16,48},{24,56},{32,64},{40,72},{48,80},{56,88},{64,... | collective-permute-start | bytes 798728 | tf_op jit(solution)/shard_map/ppermute | solution.py:17
  217.4 21.5 %copy-start.24 = (f32[8,512]{1,0:T(8,128)S(1)}, f32[8,512]{1,0:T(8,128)}, u32[]{:S(2)}) copy-start(f32[8,512]{1,0:T(8,128)} %copy.119) | copy-start | bytes 49156
  217.4 21.5 %copy-start.25 = (f32[8,512]{1,0:T(8,128)S(1)}, f32[8,512]{1,0:T(8,128)}, u32[]{:S(2)}) copy-start(f32[8,512]{1,0:T(8,128)} %copy.117) | copy-start | bytes 49156
  218.2 7.7 %collective-permute-start.11 = (f32[8,65,128]{2,1,0:T(8,128)}, f32[8,65,128]{2,1,0:T(8,128)}, u32[]{:S(2)}, u32[]{:S(2)}) collective-permute-start(f32[8,65,128]{2,1,0:T(8,128)} %pad_maximum_fusion.11), channel_id=1, source_target_pairs={{64,0},{72,8},{80,16},{88,24},{96,32},{104,40},{112,48},{120,56},{... | collective-permute-start | bytes 798728 | tf_op jit(solution)/shard_map/ppermute | solution.py:17
  221.4 9.9 %collective-permute-start.10 = (f32[8,65,128]{2,1,0:T(8,128)}, f32[8,65,128]{2,1,0:T(8,128)}, u32[]{:S(2)}, u32[]{:S(2)}) collective-permute-start(f32[8,65,128]{2,1,0:T(8,128)} %pad_maximum_fusion.10), channel_id=1, source_target_pairs={{0,64},{8,72},{16,80},{24,88},{32,96},{40,104},{48,112},{56,120},{... | collective-permute-start | bytes 798728 | tf_op jit(solution)/shard_map/ppermute | solution.py:17
  235.5 13.9 %collective-permute-start.13 = (f32[8,65,128]{2,1,0:T(8,128)}, f32[8,65,128]{2,1,0:T(8,128)}, u32[]{:S(2)}, u32[]{:S(2)}) collective-permute-start(f32[8,65,128]{2,1,0:T(8,128)} %pad_maximum_fusion.13), channel_id=1, source_target_pairs={{128,0},{136,8},{144,16},{152,24},{160,32},{168,40},{176,48},{184,... | collective-permute-start | bytes 798728 | tf_op jit(solution)/shard_map/ppermute | solution.py:17
  248.1 10.8 %collective-permute-start.12 = (f32[8,65,128]{2,1,0:T(8,128)}, f32[8,65,128]{2,1,0:T(8,128)S(1)}, u32[]{:S(2)}, u32[]{:S(2)}) collective-permute-start(f32[8,65,128]{2,1,0:T(8,128)} %pad_maximum_fusion.12), channel_id=1, source_target_pairs={{0,128},{8,136},{16,144},{24,152},{32,160},{40,168},{48,176},{56,1... | collective-permute-start | bytes 798728 | tf_op jit(solution)/shard_map/ppermute | solution.py:17
  (47 other events, 401.4 us)
Sparse Core Ops, SparseCore 0:
  22.8 68.3 reduce-scatter.2
  113.4 47.8 reduce-scatter.4

commit v7 on v6

--- a/solution.py
+++ b/solution.py
@@ -157,7 +157,9 @@
     segment_last = segment[rows_here - 1]
     send_x = tail_rows(x_raw, x_edges, start_last, segment_last, lagged)
     send_bc = tail_rows(bc_raw, bc_edges, start_last, segment_last, lagged)
-    prior_x, prior_bc = from_behind((send_x, send_bc), "seq", 1)
+    prior_both = from_behind(jnp.concatenate([send_x, send_bc], axis=1), "seq", 1)
+    prior_x = prior_both[:, :channels]
+    prior_bc = prior_both[:, channels:]
     x_conv = convolve(
         x_raw,
         prior_x,

time: 285 us -> 280 us (0.982)
  waiting for transfers between devices: 82.3 us -> 78.3 us
    ppermute x12 -> x11, waiting for transfers between devices: 42.1 us -> 38.5 us  [from_behind(): lax.ppermute(value, axis, [(source, source + steps) for source in range(f...]
    ppermute x12 -> x11, starting transfers between devices: 38.8 us -> 39 us  [from_behind(): lax.ppermute(value, axis, [(source, source + steps) for source in range(f...]
  transfers between devices with their start and end apart: 16 -> 15, of which waited for: 10 -> 11; matrix products, arithmetic and copies ran while one was open for 37% -> 37% of each run, Pallas kernels for 0% -> 0%
where the time goes in v7:
time: 280 us; the launch traced here: 277 us
  waiting for transfers between devices  78.3 us (28%)
  other arithmetic  61.8 us (22%)
  starting transfers between devices  40.7 us (15%)
  matrix products  37.7 us (13%)
  local copies, waits for them, and re-layouts  31.2 us (11%)
  between operations  22 us (8%)
  blocking collectives  5.27 us (2%)
    reduce_scatter x1, waiting for transfers between devices, shards(): lax.psum_scatter(jnp.concatenate([x_part, bc_part, dt_part], axis=2), 'co...  39.1 us
    ppermute x11, starting transfers between devices, from_behind(): lax.ppermute(value, axis, [(source, source + steps) for source in range(f...  39 us
    ppermute x11, waiting for transfers between devices, from_behind(): lax.ppermute(value, axis, [(source, source + steps) for source in range(f...  38.5 us
    dot_general x3, matrix products, shards(): jnp.einsum('td,dgc->gtc', tokens, weight, preferred_element_type=jnp.floa...  11.9 us
    slice x13, local copies, waits for them, and re-layouts, unpack(): return (packed[:, p_n, 0], packed[:, :p_n], packed[0, p_n, n_n - 1])  10.9 us
    dot_general x6, matrix products, convolve(): from_edge = jnp.dot(picker, table, preferred_element_type=jnp.float32)  8.32 us
    dot_general x1, matrix products, local_terms(): jnp.einsum('hij,jhp->ihp', mixing, x_vals.astype(jnp.float32), precision=...  8.26 us
    select_n x5, other arithmetic, near_far(): jnp.where(keep, near[1], far_a[:, None, None] * near[1] + far_b)  7.73 us
  transfers between devices with their start and end apart: 15, of which 11 were waited for; matrix products, arithmetic and copies ran while one was open for 37% of the time, Pallas kernels for 0%

profile of v7, /device:TPU:71, one launch (start us, length us, event | category | flops | bytes accessed | tf_op | source)
XLA Modules:
  0.0 276.9 jit_solution(17017331421776418514)
XLA Ops:
  11.9 4.5 %fusion.20 = f32[4,512,512]{2,1,0:T(8,128)} fusion(bf16[1024,4,512]{2,1,0:T(4,128)(2,1)S(1)} %copy-done.52, bf16[256,1024]{1,0:T(8,128)(2,1)S(1)} %get-tuple-element.116, bf16[256,1024]{1,0:T(8,128)(2,1)S(1)} %get-tuple-element.115), kind=kOutput, calls=%fused_computation.27 | convolution fusion | flops 2149580800 | bytes 9437184 | tf_op jit(solution)/shard_map/td,dgc->gtc/dot_general | solution.py:133
  17.2 5.4 %pad_maximum_fusion = f32[4,512,648]{2,1,0:T(8,128)} fusion(f32[4,512,8]{2,1,0:T(8,128)S(1)} %bitcast.163, f32[4,512,128]{2,1,0:T(8,128)S(1)} %convolution_bitcast_fusion, f32[4,512,512]{2,1,0:T(8,128)} %fusion.20), kind=kLoop, calls=%fused_computation.12 | loop fusion | flops 2654208 | bytes 10616832 | tf_op jit(solution)/shard_map/concatenate | solution.py:137
  45.5 6.7 %fusion.23 = f32[4,512,512]{2,1,0:T(8,128)} fusion(bf16[1024,4,512]{2,1,0:T(4,128)(2,1)} %param.19, bf16[256,1024]{1,0:T(8,128)(2,1)S(1)} %copy-done.16, bf16[256,1024]{1,0:T(8,128)(2,1)S(1)} %copy-done.14), kind=kOutput, calls=%fused_computation.28 | convolution fusion | flops 2149580800 | bytes 9437184 | tf_op jit(solution)/shard_map/td,dgc->gtc/dot_general | solution.py:133
  52.2 39.1 %reduce-scatter.3.cloned.1.call-done = f32[1,512,648]{2,1,0:T(8,128)} async-done(((f32[4,512,648]{2,1,0:T(8,128)}), f32[1,512,648]{2,1,0:T(8,128)}) %reduce-scatter.3.cloned.1.call-update) | async-done | bytes 1327120 | tf_op jit(solution)/shard_map/reduce_scatter | solution.py:136
  109.6 3.4 %collective-permute-start.2 = (bf16[3,768]{1,0:T(4,128)(2,1)S(1)}, bf16[3,768]{1,0:T(4,128)(2,1)S(1)}, u32[]{:S(2)}, u32[]{:S(2)}) collective-permute-start(bf16[3,768]{1,0:T(4,128)(2,1)S(1)} %pad_maximum_fusion.14), channel_id=1, source_target_pairs={{0,8},{8,16},{16,24},{24,32},{32,40},{40,48},{48,56},{56,64},{64,7... | collective-permute-start | bytes 13832 | tf_op jit(solution)/shard_map/ppermute | solution.py:17
  114.9 3.1 %multiply_convert_fusion.1 = bf16[512,512]{1,0:T(8,128)(2,1)} fusion(f32[512,512]{1,0:T(8,128)S(1)} %fusion.57, f32[512,512]{1,0:T(8,128)S(1)} %fusion.59, bf16[512,512]{1,0:T(8,128)(2,1)S(1)} %slice.211, bf16[3,512]{1,0:T(4,128)(2,1)S(1)} %slice.287, f32[512]{0:T(512)} %bitcast.188, f32[512]{0:T(512)} %bitcast.189, f32[512]{0:T(512)} %bitcast.187, ...), kind=kOutput, calls=%fused_computation.54 | convolution fusion | flops 12325376 | bytes 3171840 | tf_op jit(solution)/shard_map/dot_general | solution.py:93
  120.1 2.4 multiply_convert_fusion.2
  129.4 3.7 %collective-permute-start.3 = (f32[8,65,128]{2,1,0:T(8,128)S(1)}, f32[8,65,128]{2,1,0:T(8,128)S(1)}, u32[]{:S(2)}, u32[]{:S(2)}) collective-permute-start(f32[8,65,128]{2,1,0:T(8,128)S(1)} %pad_maximum_fusion.4), channel_id=1, source_target_pairs={{0,8},{8,16},{16,24},{24,32},{32,40},{40,48},{48,56},{56,64},{64,7... | collective-permute-start | bytes 798728 | tf_op jit(solution)/shard_map/ppermute | solution.py:17
  136.2 3.5 %collective-permute-done.3 = f32[8,65,128]{2,1,0:T(8,128)S(1)} collective-permute-done((f32[8,65,128]{2,1,0:T(8,128)S(1)}, f32[8,65,128]{2,1,0:T(8,128)S(1)}, u32[]{:S(2)}, u32[]{:S(2)}) %collective-permute-start.3) | collective-permute-done | bytes 266272 | tf_op jit(solution)/shard_map/ppermute | solution.py:17
  143.9 6.1 %collective-permute-start.6 = (f32[8,65,128]{2,1,0:T(8,128)}, f32[8,65,128]{2,1,0:T(8,128)}, u32[]{:S(2)}, u32[]{:S(2)}) collective-permute-start(f32[8,65,128]{2,1,0:T(8,128)} %pad_maximum_fusion.7), channel_id=1, source_target_pairs={{16,0},{24,8},{32,16},{40,24},{48,32},{56,40},{64,48},{72,56},{80,... | collective-permute-start | bytes 798728 | tf_op jit(solution)/shard_map/ppermute | solution.py:17
  150.8 2.6 collective-permute-start.5
  153.4 2.6 fusion.46
  156.1 8.7 %collective-permute-done.6 = f32[8,65,128]{2,1,0:T(8,128)} collective-permute-done((f32[8,65,128]{2,1,0:T(8,128)}, f32[8,65,128]{2,1,0:T(8,128)}, u32[]{:S(2)}, u32[]{:S(2)}) %collective-permute-start.6) | collective-permute-done | bytes 266272 | tf_op jit(solution)/shard_map/ppermute | solution.py:17
  173.7 5.5 %collective-permute-start.8 = (f32[8,65,128]{2,1,0:T(8,128)}, f32[8,65,128]{2,1,0:T(8,128)}, u32[]{:S(2)}, u32[]{:S(2)}) collective-permute-start(f32[8,65,128]{2,1,0:T(8,128)} %pad_maximum_fusion.9), channel_id=1, source_target_pairs={{32,0},{40,8},{48,16},{56,24},{64,32},{72,40},{80,48},{88,56},{96,... | collective-permute-start | bytes 798728 | tf_op jit(solution)/shard_map/ppermute | solution.py:17
  180.0 4.4 %collective-permute-start.7 = (f32[8,65,128]{2,1,0:T(8,128)}, f32[8,65,128]{2,1,0:T(8,128)}, u32[]{:S(2)}, u32[]{:S(2)}) collective-permute-start(f32[8,65,128]{2,1,0:T(8,128)} %pad_maximum_fusion.8), channel_id=1, source_target_pairs={{0,32},{8,40},{16,48},{24,56},{32,64},{40,72},{48,80},{56,88},{64,... | collective-permute-start | bytes 798728 | tf_op jit(solution)/shard_map/ppermute | solution.py:17
  184.4 2.3 fusion.70
  186.8 3.2 %collective-permute-done.8 = f32[8,65,128]{2,1,0:T(8,128)} collective-permute-done((f32[8,65,128]{2,1,0:T(8,128)}, f32[8,65,128]{2,1,0:T(8,128)}, u32[]{:S(2)}, u32[]{:S(2)}) %collective-permute-start.8) | collective-permute-done | bytes 266272 | tf_op jit(solution)/shard_map/ppermute | solution.py:17
  193.2 11.4 %collective-permute-done.7 = f32[8,65,128]{2,1,0:T(8,128)} collective-permute-done((f32[8,65,128]{2,1,0:T(8,128)}, f32[8,65,128]{2,1,0:T(8,128)}, u32[]{:S(2)}, u32[]{:S(2)}) %collective-permute-start.7) | collective-permute-done | bytes 266272 | tf_op jit(solution)/shard_map/ppermute | solution.py:17
  210.3 5.4 %collective-permute-start.10 = (f32[8,65,128]{2,1,0:T(8,128)}, f32[8,65,128]{2,1,0:T(8,128)}, u32[]{:S(2)}, u32[]{:S(2)}) collective-permute-start(f32[8,65,128]{2,1,0:T(8,128)} %pad_maximum_fusion.11), channel_id=1, source_target_pairs={{64,0},{72,8},{80,16},{88,24},{96,32},{104,40},{112,48},{120,56},{... | collective-permute-start | bytes 798728 | tf_op jit(solution)/shard_map/ppermute | solution.py:17
  229.8 3.3 %collective-permute-start.12 = (f32[8,65,128]{2,1,0:T(8,128)}, f32[8,65,128]{2,1,0:T(8,128)}, u32[]{:S(2)}, u32[]{:S(2)}) collective-permute-start(f32[8,65,128]{2,1,0:T(8,128)} %pad_maximum_fusion.13), channel_id=1, source_target_pairs={{128,0},{136,8},{144,16},{152,24},{160,32},{168,40},{176,48},{184,... | collective-permute-start | bytes 798728 | tf_op jit(solution)/shard_map/ppermute | solution.py:17
  233.2 8.3 %fusion.33 = f32[512,8,64]{0,2,1:T(8,128)S(1)} fusion(bf16[512,8,64]{0,2,1:T(8,128)(2,1)} %bitcast.160, f32[8,512]{1,0:T(8,128)S(1)} %copy-done.21, f32[512,512]{1,0:T(8,128)} %fusion.70, f32[8,512]{1,0:T(8,128)S(1)} %copy-done.22, pred[512,512]{1,0:T(8,128)(4,1)} %fusion.45, f32[512,8,64]{0,2,1:T(8,128)} %bitcast.165, f32[512,8]{0,1:T(8,128)S(1)} %copy-done.20), kind=kOutput, calls=%fused_computation.36 | convolution fusion | flops 1621622784 | bytes 3981312 | tf_op jit(solution)/shard_map/hij,jhp->ihp/dot_general | solution.py:38
  246.3 5.9 %collective-permute-done.11 = f32[8,65,128]{2,1,0:T(8,128)S(1)} collective-permute-done((f32[8,65,128]{2,1,0:T(8,128)}, f32[8,65,128]{2,1,0:T(8,128)S(1)}, u32[]{:S(2)}, u32[]{:S(2)}) %collective-permute-start.11) | collective-permute-done | bytes 266272 | tf_op jit(solution)/shard_map/ppermute | solution.py:17
  262.6 5.3 %psum.7 = f32[512]{0:T(512)S(1)} all-reduce(f32[512]{0:T(512)S(1)} %multiply_reduce_fusion), channel_id=1, replica_groups=mesh['seq'=32,'row'=2,'col'=4] {'row'}, use_global_device_ids=true, to_apply=%region_16.17 | all-reduce | flops 512 | bytes 4096 | tf_op jit(solution)/shard_map/psum | solution.py:264
  267.8 2.2 fusion.51
  (298 shorter events, 106.1 us)
Async XLA Ops:
  7.2 84.1 %reduce-scatter.3.cloned.1.call-start = ((), (), s32[]{:S(2)}) async-start(), calls=%async_computation.2 | async-start | bytes 7864320 | tf_op jit(solution)/shard_map/reduce_scatter | solution.py:136
  7.2 2.5 collective-permute-start
  22.6 22.8 %copy-start.14 = (bf16[256,1024]{1,0:T(8,128)(2,1)S(1)}, bf16[256,1024]{1,0:T(8,128)(2,1)}, u32[]{:S(2)}) copy-start(bf16[256,1024]{1,0:T(8,128)(2,1)} %copy-done.13) | copy-start | bytes 1572868
  22.7 22.8 %copy-start.16 = (bf16[256,1024]{1,0:T(8,128)(2,1)S(1)}, bf16[256,1024]{1,0:T(8,128)(2,1)}, u32[]{:S(2)}) copy-start(bf16[256,1024]{1,0:T(8,128)(2,1)} %copy-done.15) | copy-start | bytes 1572868
  22.7 236.3 %reduce-scatter.5.cloned.1.call-start = ((), (), s32[]{:S(2)}) async-start(), calls=%async_computation.3 | async-start | bytes 5242880 | tf_op jit(solution)/shard_map/reduce_scatter | solution.py:141
  34.2 72.2 %copy-start.29 = (pred[3]{0:T(512)(128)(4,1)}, pred[3]{0:T(512)(128)(4,1)S(1)}, u32[]{:S(2)}) copy-start(pred[3]{0:T(512)(128)(4,1)S(1)} %add_compare_fusion) | copy-start | bytes 13
  45.5 47.9 %copy-start.27 = (f32[1,8]{1,0:T(1,128)S(1)}, f32[1,8]{1,0:T(1,128)}, u32[]{:S(2)}) copy-start(f32[1,8]{1,0:T(1,128)} %param.26) | copy-start | bytes 100
  45.5 47.9 %copy-start.28 = (f32[1,8]{1,0:T(1,128)S(1)}, f32[1,8]{1,0:T(1,128)}, u32[]{:S(2)}) copy-start(f32[1,8]{1,0:T(1,128)} %param.27) | copy-start | bytes 100
  52.2 48.9 %copy-start.36 = (pred[512]{0:T(512)(128)(4,1)S(1)}, pred[512]{0:T(512)(128)(4,1)}, u32[]{:S(2)}) copy-start(pred[512]{0:T(512)(128)(4,1)} %broadcast_compare_fusion.1) | copy-start | bytes 1540
  98.1 9.9 %collective-permute-start.1 = (bf16[512,128]{1,0:T(8,128)(2,1)}, bf16[512,128]{1,0:T(8,128)(2,1)}, u32[]{:S(2)}, u32[]{:S(2)}) collective-permute-start(bf16[512,128]{1,0:T(8,128)(2,1)} %slice.220), channel_id=1, source_target_pairs={{0,4},{4,0},{1,5},{5,1},{2,6},{6,2},{3,7},{7,3},{8,12},{12,8},{9,1... | collective-permute-start | bytes 393224 | tf_op jit(solution)/shard_map/ppermute | solution.py:145
  109.6 4.4 %collective-permute-start.2 = (bf16[3,768]{1,0:T(4,128)(2,1)S(1)}, bf16[3,768]{1,0:T(4,128)(2,1)S(1)}, u32[]{:S(2)}, u32[]{:S(2)}) collective-permute-start(bf16[3,768]{1,0:T(4,128)(2,1)S(1)} %pad_maximum_fusion.14), channel_id=1, source_target_pairs={{0,8},{8,16},{16,24},{24,32},{32,40},{40,48},{48,56},{56,64},{64,7... | collective-permute-start | bytes 13832 | tf_op jit(solution)/shard_map/ppermute | solution.py:17
  124.8 10.5 %collective-permute-start.4 = (f32[8,65,128]{2,1,0:T(8,128)S(1)}, f32[8,65,128]{2,1,0:T(8,128)S(1)}, u32[]{:S(2)}, u32[]{:S(2)}) collective-permute-start(f32[8,65,128]{2,1,0:T(8,128)S(1)} %pad_maximum_fusion.5), channel_id=1, source_target_pairs={{8,0},{16,8},{24,16},{32,24},{40,32},{48,40},{56,48},{64,56},{72,6... | collective-permute-start | bytes 798728 | tf_op jit(solution)/shard_map/ppermute | solution.py:17
  129.4 10.2 %collective-permute-start.3 = (f32[8,65,128]{2,1,0:T(8,128)S(1)}, f32[8,65,128]{2,1,0:T(8,128)S(1)}, u32[]{:S(2)}, u32[]{:S(2)}) collective-permute-start(f32[8,65,128]{2,1,0:T(8,128)S(1)} %pad_maximum_fusion.4), channel_id=1, source_target_pairs={{0,8},{8,16},{16,24},{24,32},{32,40},{40,48},{48,56},{56,64},{64,7... | collective-permute-start | bytes 798728 | tf_op jit(solution)/shard_map/ppermute | solution.py:17
  143.9 20.8 %collective-permute-start.6 = (f32[8,65,128]{2,1,0:T(8,128)}, f32[8,65,128]{2,1,0:T(8,128)}, u32[]{:S(2)}, u32[]{:S(2)}) collective-permute-start(f32[8,65,128]{2,1,0:T(8,128)} %pad_maximum_fusion.7), channel_id=1, source_target_pairs={{16,0},{24,8},{32,16},{40,24},{48,32},{56,40},{64,48},{72,56},{80,... | collective-permute-start | bytes 798728 | tf_op jit(solution)/shard_map/ppermute | solution.py:17
  150.8 17.2 %collective-permute-start.5 = (f32[8,65,128]{2,1,0:T(8,128)}, f32[8,65,128]{2,1,0:T(8,128)}, u32[]{:S(2)}, u32[]{:S(2)}) collective-permute-start(f32[8,65,128]{2,1,0:T(8,128)} %pad_maximum_fusion.6), channel_id=1, source_target_pairs={{0,16},{8,24},{16,32},{24,40},{32,48},{40,56},{48,64},{56,72},{64,... | collective-permute-start | bytes 798728 | tf_op jit(solution)/shard_map/ppermute | solution.py:17
  173.7 16.3 %collective-permute-start.8 = (f32[8,65,128]{2,1,0:T(8,128)}, f32[8,65,128]{2,1,0:T(8,128)}, u32[]{:S(2)}, u32[]{:S(2)}) collective-permute-start(f32[8,65,128]{2,1,0:T(8,128)} %pad_maximum_fusion.9), channel_id=1, source_target_pairs={{32,0},{40,8},{48,16},{56,24},{64,32},{72,40},{80,48},{88,56},{96,... | collective-permute-start | bytes 798728 | tf_op jit(solution)/shard_map/ppermute | solution.py:17
  180.0 24.6 %collective-permute-start.7 = (f32[8,65,128]{2,1,0:T(8,128)}, f32[8,65,128]{2,1,0:T(8,128)}, u32[]{:S(2)}, u32[]{:S(2)}) collective-permute-start(f32[8,65,128]{2,1,0:T(8,128)} %pad_maximum_fusion.8), channel_id=1, source_target_pairs={{0,32},{8,40},{16,48},{24,56},{32,64},{40,72},{48,80},{56,88},{64,... | collective-permute-start | bytes 798728 | tf_op jit(solution)/shard_map/ppermute | solution.py:17
  209.6 23.5 %copy-start.20 = (f32[512,8]{0,1:T(8,128)S(1)}, f32[512,8]{0,1:T(8,128)}, u32[]{:S(2)}) copy-start(f32[512,8]{0,1:T(8,128)} %copy.140) | copy-start | bytes 49156
  209.6 23.5 %copy-start.21 = (f32[8,512]{1,0:T(8,128)S(1)}, f32[8,512]{1,0:T(8,128)}, u32[]{:S(2)}) copy-start(f32[8,512]{1,0:T(8,128)} %copy.139) | copy-start | bytes 49156
  209.6 23.5 %copy-start.22 = (f32[8,512]{1,0:T(8,128)S(1)}, f32[8,512]{1,0:T(8,128)}, u32[]{:S(2)}) copy-start(f32[8,512]{1,0:T(8,128)} %copy.137) | copy-start | bytes 49156
  210.3 9.9 %collective-permute-start.10 = (f32[8,65,128]{2,1,0:T(8,128)}, f32[8,65,128]{2,1,0:T(8,128)}, u32[]{:S(2)}, u32[]{:S(2)}) collective-permute-start(f32[8,65,128]{2,1,0:T(8,128)} %pad_maximum_fusion.11), channel_id=1, source_target_pairs={{64,0},{72,8},{80,16},{88,24},{96,32},{104,40},{112,48},{120,56},{... | collective-permute-start | bytes 798728 | tf_op jit(solution)/shard_map/ppermute | solution.py:17
  216.5 9.1 %collective-permute-start.9 = (f32[8,65,128]{2,1,0:T(8,128)}, f32[8,65,128]{2,1,0:T(8,128)}, u32[]{:S(2)}, u32[]{:S(2)}) collective-permute-start(f32[8,65,128]{2,1,0:T(8,128)} %pad_maximum_fusion.10), channel_id=1, source_target_pairs={{0,64},{8,72},{16,80},{24,88},{32,96},{40,104},{48,112},{56,120},{... | collective-permute-start | bytes 798728 | tf_op jit(solution)/shard_map/ppermute | solution.py:17
  229.8 13.8 %collective-permute-start.12 = (f32[8,65,128]{2,1,0:T(8,128)}, f32[8,65,128]{2,1,0:T(8,128)}, u32[]{:S(2)}, u32[]{:S(2)}) collective-permute-start(f32[8,65,128]{2,1,0:T(8,128)} %pad_maximum_fusion.13), channel_id=1, source_target_pairs={{128,0},{136,8},{144,16},{152,24},{160,32},{168,40},{176,48},{184,... | collective-permute-start | bytes 798728 | tf_op jit(solution)/shard_map/ppermute | solution.py:17
  242.3 9.9 %collective-permute-start.11 = (f32[8,65,128]{2,1,0:T(8,128)}, f32[8,65,128]{2,1,0:T(8,128)S(1)}, u32[]{:S(2)}, u32[]{:S(2)}) collective-permute-start(f32[8,65,128]{2,1,0:T(8,128)} %pad_maximum_fusion.12), channel_id=1, source_target_pairs={{0,128},{8,136},{16,144},{24,152},{32,160},{40,168},{48,176},{56,1... | collective-permute-start | bytes 798728 | tf_op jit(solution)/shard_map/ppermute | solution.py:17
  (45 other events, 379.1 us)
Sparse Core Ops, SparseCore 0:
  22.8 68.4 reduce-scatter.2
  106.5 48.5 reduce-scatter.4

commit v8 on v7

--- a/solution.py
+++ b/solution.py
@@ -141,18 +141,14 @@
         lax.psum_scatter(z_part, "col", scatter_dimension=0, tiled=True)[0].astype(jnp.bfloat16)
     )
     x_raw = first[:, :channels]
-    bc_mine = first[:, channels : channels + bc_cols]
-    bc_other = lax.ppermute(bc_mine, "row", [(0, 1), (1, 0)])
-    bc_raw = jnp.concatenate(
-        [jnp.where(row_first, bc_mine, bc_other), jnp.where(row_first, bc_other, bc_mine)], axis=1
-    )
+    bc_raw = first[:, channels : channels + bc_cols]
     dt_raw = first[:, channels + bc_cols :]
     positions = jnp.arange(rows_here, dtype=jnp.int32)
     flag_vals = starts == 1
     segment = jnp.cumsum(starts)
     start_at = lax.cummax(jnp.where(flag_vals, positions, -lagged), axis=0)
     x_edges = conv_x_edges[:, :, 0]
-    bc_edges = conv_bc_edges[:, :, 0]
+    bc_edges = lax.dynamic_slice_in_dim(conv_bc_edges[:, :, 0], row_at * bc_cols, bc_cols, axis=2)
     start_last = start_at[rows_here - 1]
     segment_last = segment[rows_here - 1]
     send_x = tail_rows(x_raw, x_edges, start_last, segment_last, lagged)
@@ -175,14 +171,18 @@
         bc_raw,
         prior_bc,
         bc_edges,
-        conv_bc_w[:, 0],
-        conv_bc_bias[0],
+        lax.dynamic_slice_in_dim(conv_bc_w[:, 0], row_at * bc_cols, bc_cols, axis=1),
+        lax.dynamic_slice_in_dim(conv_bc_bias[0], row_at * bc_cols, bc_cols, axis=0),
         start_at,
         segment,
         positions,
         lagged,
     )
     x_heads = x_conv.reshape(rows_here, heads_here, P_SIZE)
+    bc_swapped = lax.ppermute(bc_conv, "row", [(0, 1), (1, 0)])
+    bc_conv = jnp.concatenate(
+        [jnp.where(row_first, bc_conv, bc_swapped), jnp.where(row_first, bc_swapped, bc_conv)], axis=1
+    )
     b_proj = bc_conv[:, :N]
     c_proj = bc_conv[:, N:]
     dt_vals = jax.nn.softplus(dt_raw.astype(jnp.float32) + dt_bias[0][None, :])

time: 280 us -> 285 us (1.018)
  other arithmetic: 61.8 us -> 66.4 us
    select_n x4, other arithmetic: 0.02 us -> 3.49 us  [near_far(): jnp.where(keep, near[0], far_a * near[0])]
    mul x3, other arithmetic: 0.01 us -> 3.02 us  [shards(): fwd_ex[0] * early_a]
  transfers between devices with their start and end apart: 15 -> 15, of which waited for: 11 -> 10; matrix products, arithmetic and copies ran while one was open for 37% -> 38% of each run, Pallas kernels for 0% -> 0%
where the time goes in v8:
time: 285 us; the launch traced here: 283 us
  waiting for transfers between devices  77.9 us (27%)
  other arithmetic  66.4 us (23%)
  starting transfers between devices  41.4 us (15%)
  matrix products  36.4 us (13%)
  local copies, waits for them, and re-layouts  32.8 us (12%)
  between operations  22.4 us (8%)
  blocking collectives  5.24 us (2%)
    reduce_scatter x1, waiting for transfers between devices, shards(): lax.psum_scatter(jnp.concatenate([x_part, bc_part, dt_part], axis=2), 'co...  40.5 us
    ppermute x11, starting transfers between devices, from_behind(): lax.ppermute(value, axis, [(source, source + steps) for source in range(f...  39.5 us
    ppermute x11, waiting for transfers between devices, from_behind(): lax.ppermute(value, axis, [(source, source + steps) for source in range(f...  36.8 us
    dot_general x3, matrix products, shards(): jnp.einsum('td,dgc->gtc', tokens, weight, preferred_element_type=jnp.floa...  12 us
    slice x13, local copies, waits for them, and re-layouts, unpack(): return (packed[:, p_n, 0], packed[:, :p_n], packed[0, p_n, n_n - 1])  11.1 us
    select_n x5, other arithmetic, near_far(): jnp.where(keep, near[1], far_a[:, None, None] * near[1] + far_b)  8.73 us
    dot_general x1, matrix products, local_terms(): jnp.einsum('hij,jhp->ihp', mixing, x_vals.astype(jnp.float32), precision=...  8.49 us
    dot_general x6, matrix products, convolve(): from_edge = jnp.dot(picker, table, preferred_element_type=jnp.float32)  6.79 us
  transfers between devices with their start and end apart: 15, of which 10 were waited for; matrix products, arithmetic and copies ran while one was open for 38% of the time, Pallas kernels for 0%

profile of v8, /device:TPU:71, one launch (start us, length us, event | category | flops | bytes accessed | tf_op | source)
XLA Modules:
  0.0 282.7 jit_solution(9550678437329760174)
XLA Ops:
  11.9 4.5 %fusion.20 = f32[4,512,512]{2,1,0:T(8,128)} fusion(bf16[1024,4,512]{2,1,0:T(4,128)(2,1)S(1)} %copy-done.51, bf16[256,1024]{1,0:T(8,128)(2,1)S(1)} %get-tuple-element.116, bf16[256,1024]{1,0:T(8,128)(2,1)S(1)} %get-tuple-element.115), kind=kOutput, calls=%fused_computation.27 | convolution fusion | flops 2149580800 | bytes 9437184 | tf_op jit(solution)/shard_map/td,dgc->gtc/dot_general | solution.py:133
  17.2 5.4 %pad_maximum_fusion = f32[4,512,648]{2,1,0:T(8,128)} fusion(f32[4,512,8]{2,1,0:T(8,128)S(1)} %bitcast.177, f32[4,512,128]{2,1,0:T(8,128)S(1)} %convolution_bitcast_fusion, f32[4,512,512]{2,1,0:T(8,128)} %fusion.20), kind=kLoop, calls=%fused_computation.12 | loop fusion | flops 2654208 | bytes 10616832 | tf_op jit(solution)/shard_map/concatenate | solution.py:137
  43.9 6.8 %fusion.23 = f32[4,512,512]{2,1,0:T(8,128)} fusion(bf16[1024,4,512]{2,1,0:T(4,128)(2,1)} %param.19, bf16[256,1024]{1,0:T(8,128)(2,1)S(1)} %copy-done.16, bf16[256,1024]{1,0:T(8,128)(2,1)S(1)} %copy-done.14), kind=kOutput, calls=%fused_computation.28 | convolution fusion | flops 2149580800 | bytes 9437184 | tf_op jit(solution)/shard_map/td,dgc->gtc/dot_general | solution.py:133
  50.7 40.5 %reduce-scatter.3.cloned.1.call-done = f32[1,512,648]{2,1,0:T(8,128)} async-done(((f32[4,512,648]{2,1,0:T(8,128)}), f32[1,512,648]{2,1,0:T(8,128)}) %reduce-scatter.3.cloned.1.call-update) | async-done | bytes 1327120 | tf_op jit(solution)/shard_map/reduce_scatter | solution.py:136
  98.1 3.4 %collective-permute-start.1 = (bf16[3,640]{1,0:T(4,128)(2,1)}, bf16[3,640]{1,0:T(4,128)(2,1)}, u32[]{:S(2)}, u32[]{:S(2)}) collective-permute-start(bf16[3,640]{1,0:T(4,128)(2,1)} %pad_maximum_fusion.14), channel_id=1, source_target_pairs={{0,8},{8,16},{16,24},{24,32},{32,40},{40,48},{48,56},{56,64},{64,7... | collective-permute-start | bytes 11528 | tf_op jit(solution)/shard_map/ppermute | solution.py:17
  115.8 2.3 multiply_convert_fusion.1
  127.1 4.3 %collective-permute-start.3 = (f32[8,65,128]{2,1,0:T(8,128)S(1)}, f32[8,65,128]{2,1,0:T(8,128)S(1)}, u32[]{:S(2)}, u32[]{:S(2)}) collective-permute-start(f32[8,65,128]{2,1,0:T(8,128)S(1)} %pad_maximum_fusion.3), channel_id=1, source_target_pairs={{0,8},{8,16},{16,24},{24,32},{32,40},{40,48},{48,56},{56,64},{64,7... | collective-permute-start | bytes 798728 | tf_op jit(solution)/shard_map/ppermute | solution.py:17
  131.4 3.0 %collective-permute-done.4 = f32[8,65,128]{2,1,0:T(8,128)S(1)} collective-permute-done((f32[8,65,128]{2,1,0:T(8,128)S(1)}, f32[8,65,128]{2,1,0:T(8,128)S(1)}, u32[]{:S(2)}, u32[]{:S(2)}) %collective-permute-start.4) | collective-permute-done | bytes 266272 | tf_op jit(solution)/shard_map/ppermute | solution.py:17
  143.3 5.7 %collective-permute-start.6 = (f32[8,65,128]{2,1,0:T(8,128)}, f32[8,65,128]{2,1,0:T(8,128)}, u32[]{:S(2)}, u32[]{:S(2)}) collective-permute-start(f32[8,65,128]{2,1,0:T(8,128)} %pad_maximum_fusion.6), channel_id=1, source_target_pairs={{16,0},{24,8},{32,16},{40,24},{48,32},{56,40},{64,48},{72,56},{80,... | collective-permute-start | bytes 798728 | tf_op jit(solution)/shard_map/ppermute | solution.py:17
  149.9 3.7 %collective-permute-start.5 = (f32[8,65,128]{2,1,0:T(8,128)}, f32[8,65,128]{2,1,0:T(8,128)}, u32[]{:S(2)}, u32[]{:S(2)}) collective-permute-start(f32[8,65,128]{2,1,0:T(8,128)} %pad_maximum_fusion.5), channel_id=1, source_target_pairs={{0,16},{8,24},{16,32},{24,40},{32,48},{40,56},{48,64},{56,72},{64,... | collective-permute-start | bytes 798728 | tf_op jit(solution)/shard_map/ppermute | solution.py:17
  153.6 2.5 fusion.46
  156.1 8.7 %collective-permute-done.6 = f32[8,65,128]{2,1,0:T(8,128)} collective-permute-done((f32[8,65,128]{2,1,0:T(8,128)}, f32[8,65,128]{2,1,0:T(8,128)}, u32[]{:S(2)}, u32[]{:S(2)}) %collective-permute-start.6) | collective-permute-done | bytes 266272 | tf_op jit(solution)/shard_map/ppermute | solution.py:17
  176.5 4.3 %collective-permute-start.8 = (f32[8,65,128]{2,1,0:T(8,128)}, f32[8,65,128]{2,1,0:T(8,128)}, u32[]{:S(2)}, u32[]{:S(2)}) collective-permute-start(f32[8,65,128]{2,1,0:T(8,128)} %pad_maximum_fusion.8), channel_id=1, source_target_pairs={{32,0},{40,8},{48,16},{56,24},{64,32},{72,40},{80,48},{88,56},{96,... | collective-permute-start | bytes 798728 | tf_op jit(solution)/shard_map/ppermute | solution.py:17
  181.6 5.6 %collective-permute-start.7 = (f32[8,65,128]{2,1,0:T(8,128)}, f32[8,65,128]{2,1,0:T(8,128)}, u32[]{:S(2)}, u32[]{:S(2)}) collective-permute-start(f32[8,65,128]{2,1,0:T(8,128)} %pad_maximum_fusion.7), channel_id=1, source_target_pairs={{0,32},{8,40},{16,48},{24,56},{32,64},{40,72},{48,80},{56,88},{64,... | collective-permute-start | bytes 798728 | tf_op jit(solution)/shard_map/ppermute | solution.py:17
  187.2 2.2 fusion.72
  189.4 4.1 %collective-permute-done.8 = f32[8,65,128]{2,1,0:T(8,128)} collective-permute-done((f32[8,65,128]{2,1,0:T(8,128)}, f32[8,65,128]{2,1,0:T(8,128)}, u32[]{:S(2)}, u32[]{:S(2)}) %collective-permute-start.8) | collective-permute-done | bytes 266272 | tf_op jit(solution)/shard_map/ppermute | solution.py:17
  197.0 11.2 %collective-permute-done.7 = f32[8,65,128]{2,1,0:T(8,128)} collective-permute-done((f32[8,65,128]{2,1,0:T(8,128)}, f32[8,65,128]{2,1,0:T(8,128)}, u32[]{:S(2)}, u32[]{:S(2)}) %collective-permute-start.7) | collective-permute-done | bytes 266272 | tf_op jit(solution)/shard_map/ppermute | solution.py:17
  216.2 4.6 %collective-permute-start.10 = (f32[8,65,128]{2,1,0:T(8,128)}, f32[8,65,128]{2,1,0:T(8,128)}, u32[]{:S(2)}, u32[]{:S(2)}) collective-permute-start(f32[8,65,128]{2,1,0:T(8,128)} %pad_maximum_fusion.10), channel_id=1, source_target_pairs={{64,0},{72,8},{80,16},{88,24},{96,32},{104,40},{112,48},{120,56},{... | collective-permute-start | bytes 798728 | tf_op jit(solution)/shard_map/ppermute | solution.py:17
  235.4 3.4 %collective-permute-start.12 = (f32[8,65,128]{2,1,0:T(8,128)S(1)}, f32[8,65,128]{2,1,0:T(8,128)}, u32[]{:S(2)}, u32[]{:S(2)}) collective-permute-start(f32[8,65,128]{2,1,0:T(8,128)S(1)} %pad_maximum_fusion.12), channel_id=1, source_target_pairs={{128,0},{136,8},{144,16},{152,24},{160,32},{168,40},{176,48},{184,... | collective-permute-start | bytes 798728 | tf_op jit(solution)/shard_map/ppermute | solution.py:17
  238.8 8.5 %fusion.33 = f32[512,8,64]{0,2,1:T(8,128)S(1)} fusion(bf16[512,8,64]{0,2,1:T(8,128)(2,1)} %bitcast.174, f32[8,512]{1,0:T(8,128)} %copy.139, f32[512,512]{1,0:T(8,128)} %fusion.72, f32[8,512]{1,0:T(8,128)} %copy.137, pred[512,512]{1,0:T(8,128)(4,1)} %fusion.45, f32[512,8,64]{0,2,1:T(8,128)} %bitcast.179, f32[512,8]{0,1:T(8,128)} %copy.140), kind=kOutput, calls=%fused_computation.36 | convolution fusion | flops 1621622784 | bytes 3981312 | tf_op jit(solution)/shard_map/hij,jhp->ihp/dot_general | solution.py:38
  252.6 5.4 %collective-permute-done.11 = f32[8,65,128]{2,1,0:T(8,128)S(1)} collective-permute-done((f32[8,65,128]{2,1,0:T(8,128)}, f32[8,65,128]{2,1,0:T(8,128)S(1)}, u32[]{:S(2)}, u32[]{:S(2)}) %collective-permute-start.11) | collective-permute-done | bytes 266272 | tf_op jit(solution)/shard_map/ppermute | solution.py:17
  262.6 2.2 select_bitcast_fusion
  268.4 5.2 %psum.7 = f32[512]{0:T(512)S(1)} all-reduce(f32[512]{0:T(512)S(1)} %multiply_reduce_fusion), channel_id=1, replica_groups=mesh['seq'=32,'row'=2,'col'=4] {'row'}, use_global_device_ids=true, to_apply=%region_16.17 | all-reduce | flops 512 | bytes 4096 | tf_op jit(solution)/shard_map/psum | solution.py:264
  273.6 2.2 fusion.51
  (300 shorter events, 110.5 us)
Async XLA Ops:
  7.2 84.1 %reduce-scatter.3.cloned.1.call-start = ((), (), s32[]{:S(2)}) async-start(), calls=%async_computation.2 | async-start | bytes 7864320 | tf_op jit(solution)/shard_map/reduce_scatter | solution.py:136
  7.2 2.5 collective-permute-start
  22.6 17.1 %copy-start.20 = (bf16[4,1,512]{2,0,1:T(4,128)(2,1)S(1)}, bf16[4,1,512]{2,0,1:T(4,128)(2,1)}, u32[]{:S(2)}) copy-start(bf16[4,1,512]{2,0,1:T(4,128)(2,1)} %param.22) | copy-start | bytes 12292
  22.6 21.3 %copy-start.14 = (bf16[256,1024]{1,0:T(8,128)(2,1)S(1)}, bf16[256,1024]{1,0:T(8,128)(2,1)}, u32[]{:S(2)}) copy-start(bf16[256,1024]{1,0:T(8,128)(2,1)} %copy-done.13) | copy-start | bytes 1572868
  22.6 21.3 %copy-start.16 = (bf16[256,1024]{1,0:T(8,128)(2,1)S(1)}, bf16[256,1024]{1,0:T(8,128)(2,1)}, u32[]{:S(2)}) copy-start(bf16[256,1024]{1,0:T(8,128)(2,1)} %copy-done.15) | copy-start | bytes 1572868
  22.7 242.1 %reduce-scatter.5.cloned.1.call-start = ((), (), s32[]{:S(2)}) async-start(), calls=%async_computation.3 | async-start | bytes 5242880 | tf_op jit(solution)/shard_map/reduce_scatter | solution.py:141
  43.9 48.8 %copy-start.31 = (f32[1,8]{1,0:T(1,128)S(1)}, f32[1,8]{1,0:T(1,128)}, u32[]{:S(2)}) copy-start(f32[1,8]{1,0:T(1,128)} %param.26) | copy-start | bytes 100
  43.9 48.8 %copy-start.32 = (f32[1,8]{1,0:T(1,128)S(1)}, f32[1,8]{1,0:T(1,128)}, u32[]{:S(2)}) copy-start(f32[1,8]{1,0:T(1,128)} %param.27) | copy-start | bytes 100
  98.1 13.3 %collective-permute-start.1 = (bf16[3,640]{1,0:T(4,128)(2,1)}, bf16[3,640]{1,0:T(4,128)(2,1)}, u32[]{:S(2)}, u32[]{:S(2)}) collective-permute-start(bf16[3,640]{1,0:T(4,128)(2,1)} %pad_maximum_fusion.14), channel_id=1, source_target_pairs={{0,8},{8,16},{16,24},{24,32},{32,40},{40,48},{48,56},{56,64},{64,7... | collective-permute-start | bytes 11528 | tf_op jit(solution)/shard_map/ppermute | solution.py:17
  113.9 17.4 %copy-start.11 = (bf16[512,128]{1,0:T(8,128)(2,1)}, bf16[512,128]{1,0:T(8,128)(2,1)S(1)}, u32[]{:S(2)}) copy-start(bf16[512,128]{1,0:T(8,128)(2,1)S(1)} %multiply_convert_fusion.2) | copy-start | bytes 393220
  113.9 6.3 %collective-permute-start.2 = (bf16[512,128]{1,0:T(8,128)(2,1)S(1)}, bf16[512,128]{1,0:T(8,128)(2,1)S(1)}, u32[]{:S(2)}, u32[]{:S(2)}) collective-permute-start(bf16[512,128]{1,0:T(8,128)(2,1)S(1)} %multiply_convert_fusion.2), channel_id=1, source_target_pairs={{0,4},{4,0},{1,5},{5,1},{2,6},{6,2},{3,7},{7,3},{8,12},{12,8},{9,1... | collective-permute-start | bytes 393224 | tf_op jit(solution)/shard_map/ppermute | solution.py:182
  120.3 19.6 %copy-start.33 = (f32[8]{0:T(128)S(1)}, f32[8]{0:T(128)}, u32[]{:S(2)}) copy-start(f32[8]{0:T(128)} %fusion.76) | copy-start | bytes 100
  122.5 11.9 %collective-permute-start.4 = (f32[8,65,128]{2,1,0:T(8,128)S(1)}, f32[8,65,128]{2,1,0:T(8,128)S(1)}, u32[]{:S(2)}, u32[]{:S(2)}) collective-permute-start(f32[8,65,128]{2,1,0:T(8,128)S(1)} %pad_maximum_fusion.4), channel_id=1, source_target_pairs={{8,0},{16,8},{24,16},{32,24},{40,32},{48,40},{56,48},{64,56},{72,6... | collective-permute-start | bytes 798728 | tf_op jit(solution)/shard_map/ppermute | solution.py:17
  127.1 10.6 %collective-permute-start.3 = (f32[8,65,128]{2,1,0:T(8,128)S(1)}, f32[8,65,128]{2,1,0:T(8,128)S(1)}, u32[]{:S(2)}, u32[]{:S(2)}) collective-permute-start(f32[8,65,128]{2,1,0:T(8,128)S(1)} %pad_maximum_fusion.3), channel_id=1, source_target_pairs={{0,8},{8,16},{16,24},{24,32},{32,40},{40,48},{48,56},{56,64},{64,7... | collective-permute-start | bytes 798728 | tf_op jit(solution)/shard_map/ppermute | solution.py:17
  143.3 21.6 %collective-permute-start.6 = (f32[8,65,128]{2,1,0:T(8,128)}, f32[8,65,128]{2,1,0:T(8,128)}, u32[]{:S(2)}, u32[]{:S(2)}) collective-permute-start(f32[8,65,128]{2,1,0:T(8,128)} %pad_maximum_fusion.6), channel_id=1, source_target_pairs={{16,0},{24,8},{32,16},{40,24},{48,32},{56,40},{64,48},{72,56},{80,... | collective-permute-start | bytes 798728 | tf_op jit(solution)/shard_map/ppermute | solution.py:17
  149.9 18.6 %collective-permute-start.5 = (f32[8,65,128]{2,1,0:T(8,128)}, f32[8,65,128]{2,1,0:T(8,128)}, u32[]{:S(2)}, u32[]{:S(2)}) collective-permute-start(f32[8,65,128]{2,1,0:T(8,128)} %pad_maximum_fusion.5), channel_id=1, source_target_pairs={{0,16},{8,24},{16,32},{24,40},{32,48},{40,56},{48,64},{56,72},{64,... | collective-permute-start | bytes 798728 | tf_op jit(solution)/shard_map/ppermute | solution.py:17
  176.5 17.1 %collective-permute-start.8 = (f32[8,65,128]{2,1,0:T(8,128)}, f32[8,65,128]{2,1,0:T(8,128)}, u32[]{:S(2)}, u32[]{:S(2)}) collective-permute-start(f32[8,65,128]{2,1,0:T(8,128)} %pad_maximum_fusion.8), channel_id=1, source_target_pairs={{32,0},{40,8},{48,16},{56,24},{64,32},{72,40},{80,48},{88,56},{96,... | collective-permute-start | bytes 798728 | tf_op jit(solution)/shard_map/ppermute | solution.py:17
  181.6 26.6 %collective-permute-start.7 = (f32[8,65,128]{2,1,0:T(8,128)}, f32[8,65,128]{2,1,0:T(8,128)}, u32[]{:S(2)}, u32[]{:S(2)}) collective-permute-start(f32[8,65,128]{2,1,0:T(8,128)} %pad_maximum_fusion.7), channel_id=1, source_target_pairs={{0,32},{8,40},{16,48},{24,56},{32,64},{40,72},{48,80},{56,88},{64,... | collective-permute-start | bytes 798728 | tf_op jit(solution)/shard_map/ppermute | solution.py:17
  216.2 9.1 %collective-permute-start.10 = (f32[8,65,128]{2,1,0:T(8,128)}, f32[8,65,128]{2,1,0:T(8,128)}, u32[]{:S(2)}, u32[]{:S(2)}) collective-permute-start(f32[8,65,128]{2,1,0:T(8,128)} %pad_maximum_fusion.10), channel_id=1, source_target_pairs={{64,0},{72,8},{80,16},{88,24},{96,32},{104,40},{112,48},{120,56},{... | collective-permute-start | bytes 798728 | tf_op jit(solution)/shard_map/ppermute | solution.py:17
  221.6 9.1 %collective-permute-start.9 = (f32[8,65,128]{2,1,0:T(8,128)}, f32[8,65,128]{2,1,0:T(8,128)}, u32[]{:S(2)}, u32[]{:S(2)}) collective-permute-start(f32[8,65,128]{2,1,0:T(8,128)} %pad_maximum_fusion.9), channel_id=1, source_target_pairs={{0,64},{8,72},{16,80},{24,88},{32,96},{40,104},{48,112},{56,120},{... | collective-permute-start | bytes 798728 | tf_op jit(solution)/shard_map/ppermute | solution.py:17
  235.4 14.0 %collective-permute-start.12 = (f32[8,65,128]{2,1,0:T(8,128)S(1)}, f32[8,65,128]{2,1,0:T(8,128)}, u32[]{:S(2)}, u32[]{:S(2)}) collective-permute-start(f32[8,65,128]{2,1,0:T(8,128)S(1)} %pad_maximum_fusion.12), channel_id=1, source_target_pairs={{128,0},{136,8},{144,16},{152,24},{160,32},{168,40},{176,48},{184,... | collective-permute-start | bytes 798728 | tf_op jit(solution)/shard_map/ppermute | solution.py:17
  238.8 19.3 %copy-start.3 = (bf16[512,512]{0,1:T(8,128)(2,1)S(1)}, bf16[512,512]{0,1:T(8,128)(2,1)}, u32[]{:S(2)}) copy-start(bf16[512,512]{0,1:T(8,128)(2,1)} %copy-done.2) | copy-start | bytes 1572868
  238.8 19.3 %copy-start.44 = (f32[1,8]{1,0:T(1,128)S(1)}, f32[1,8]{1,0:T(1,128)}, u32[]{:S(2)}) copy-start(f32[1,8]{1,0:T(1,128)} %param.28) | copy-start | bytes 100
  248.1 9.9 %collective-permute-start.11 = (f32[8,65,128]{2,1,0:T(8,128)}, f32[8,65,128]{2,1,0:T(8,128)S(1)}, u32[]{:S(2)}, u32[]{:S(2)}) collective-permute-start(f32[8,65,128]{2,1,0:T(8,128)} %pad_maximum_fusion.11), channel_id=1, source_target_pairs={{0,128},{8,136},{16,144},{24,152},{32,160},{40,168},{48,176},{56,1... | collective-permute-start | bytes 798728 | tf_op jit(solution)/shard_map/ppermute | solution.py:17
  (45 other events, 354.3 us)
Sparse Core Ops, SparseCore 0:
  22.8 68.3 reduce-scatter.2
  109.7 48.5 reduce-scatter.4

commit v9 on v7

--- a/solution.py
+++ b/solution.py
@@ -208,51 +208,44 @@
         )
         return jnp.concatenate([state, aux[:, None, :]], axis=1)
 
-    def unpack(packed):
-        return packed[:, p_n, 0], packed[:, :p_n], packed[0, p_n, n_n - 1]
-
-    fwd_in = (decay_all * ones, state_add)
-    fwd_ex = (ones, zeros_state)
-    bwd_in = (jnp.exp(end_zero), seg_ends[0], has_start)
-    bwd_ex = (ones, zeros_state, jnp.zeros((), jnp.float32))
+    row_ids = jnp.arange(p_n + 1, dtype=jnp.int32)[None, :, None]
+    lane_ids = jnp.arange(n_n, dtype=jnp.int32)[None, None, :]
+    keep_b = (row_ids < p_n).astype(jnp.float32)
+    keep_bm = ((row_ids < p_n) | (lane_ids >= n_n // 2)).astype(jnp.float32)
+
+    def decay_of(packed):
+        return packed[:, p_n, 0][:, None, None]
+
+    fwd_in = pack(decay_all * ones, state_add, 0.0)
+    fwd_ex = pack(ones, zeros_state, 0.0)
+    bwd_in = pack(jnp.exp(end_zero), seg_ends[0], has_start)
+    bwd_ex = pack(ones, zeros_state, 0.0)
     shift = 1
     while shift < seq_count:
         last = 2 * shift >= seq_count
-        got_f = from_behind(pack(fwd_in[0], fwd_in[1], 0.0), "seq", shift)
-        got_b = from_behind(pack(*bwd_in), "seq", -shift)
-        early_a, early_b, _ = unpack(got_f)
-        late_a, late_b, late_m = unpack(got_b)
+        got_f = from_behind(fwd_in, "seq", shift)
+        got_b = from_behind(bwd_in, "seq", -shift)
         late_ok = seq_at + shift < seq_count
-        fwd_ex = (
-            fwd_ex[0] * early_a,
-            fwd_ex[0][:, None, None] * early_b + fwd_ex[1],
-        )
-
-        def near_far(near, far_a, far_b, far_m):
-            keep = (near[2] > 0.5) | jnp.logical_not(late_ok)
-            return (
-                jnp.where(keep, near[0], far_a * near[0]),
-                jnp.where(keep, near[1], far_a[:, None, None] * near[1] + far_b),
-                jnp.where(keep, near[2], far_m),
-            )
-
-        bwd_ex = near_far(bwd_ex, late_a, late_b, late_m)
+        fwd_ex = decay_of(fwd_ex) * got_f + fwd_ex * keep_b
+
+        def near_far(near):
+            keep = (near[0, p_n, n_n - 1] > 0.5) | jnp.logical_not(late_ok)
+            return jnp.where(keep, near, decay_of(got_b) * near + got_b * keep_bm)
+
+        bwd_ex = near_far(bwd_ex)
         if not last:
-            fwd_in = (
-                fwd_in[0] * early_a,
-                fwd_in[0][:, None, None] * early_b + fwd_in[1],
-            )
-            bwd_in = near_far(bwd_in, late_a, late_b, late_m)
+            fwd_in = decay_of(fwd_in) * got_f + fwd_in * keep_b
+            bwd_in = near_far(bwd_in)
         fwd_in, fwd_ex, bwd_in, bwd_ex = lax.optimization_barrier((fwd_in, fwd_ex, bwd_in, bwd_ex))
         shift *= 2
-    state_in = fwd_ex[1]
+    state_in = fwd_ex[:, :p_n]
     carried_in = jnp.einsum("tn,hpn->thp", c_proj.astype(jnp.float32), state_in, precision=PRECISE)
     y_full = (
         y_part
         + carried[:, :, None] * carried_in
         + d_skip[0][None, :, None] * x_heads.astype(jnp.float32)
     )
-    tail_state = bwd_ex[0][:, None, None] * state_add + bwd_ex[1]
+    tail_state = decay_of(bwd_ex) * state_add + bwd_ex[:, :p_n]
     slot_ids = jnp.arange(1, init_vals.shape[0] + 1, dtype=jnp.int32)
     finals = jnp.where(
         (slot_ids < started)[:, None, None, None],

time: 280 us -> 283 us (1.011)
  the two profiles are of different devices: /device:TPU:71 before, /device:TPU:35 now
where the time goes in v9:
time: 283 us; the launch traced here: 280 us
  waiting for transfers between devices  63.6 us (22%)
  other arithmetic  60.7 us (21%)
  starting transfers between devices  46.2 us (16%)
  matrix products  43.6 us (15%)
  local copies, waits for them, and re-layouts  39.5 us (14%)
  between operations  22.6 us (8%)
  blocking collectives  4.03 us (1%)
    ppermute x11, starting transfers between devices, from_behind(): lax.ppermute(value, axis, [(source, source + steps) for source in range(f...  44.6 us
    reduce_scatter x1, waiting for transfers between devices, shards(): lax.psum_scatter(jnp.concatenate([x_part, bc_part, dt_part], axis=2), 'co...  36.3 us
    ppermute x11, waiting for transfers between devices, from_behind(): lax.ppermute(value, axis, [(source, source + steps) for source in range(f...  26.7 us
    dot_general x3, matrix products, shards(): jnp.einsum('td,dgc->gtc', tokens, weight, preferred_element_type=jnp.floa...  13 us
    slice x14, local copies, waits for them, and re-layouts, decay_of(): return packed[:, p_n, 0][:, None, None]  11.9 us
    dot_general x6, matrix products, convolve(): from_edge = jnp.dot(picker, table, preferred_element_type=jnp.float32)  10.6 us
    select_n x5, other arithmetic, near_far(): return jnp.where(keep, near, decay_of(got_b) * near + got_b * keep_bm)  10.1 us
    dot_general x1, matrix products, local_terms(): jnp.einsum('hij,jhp->ihp', mixing, x_vals.astype(jnp.float32), precision=...  8.88 us
  transfers between devices with their start and end apart: 15, of which 9 were waited for; matrix products, arithmetic and copies ran while one was open for 41% of the time, Pallas kernels for 0%

profile of v9, /device:TPU:35, one launch (start us, length us, event | category | flops | bytes accessed | tf_op | source)
XLA Modules:
  0.0 280.2 jit_solution(1594426849255433343)
XLA Ops:
  12.9 4.5 %fusion.20 = f32[4,512,512]{2,1,0:T(8,128)} fusion(bf16[1024,4,512]{2,1,0:T(4,128)(2,1)S(1)} %copy-done.49, bf16[256,1024]{1,0:T(8,128)(2,1)S(1)} %get-tuple-element.66, bf16[256,1024]{1,0:T(8,128)(2,1)S(1)} %get-tuple-element.65), kind=kOutput, calls=%fused_computation.27 | convolution fusion | flops 2149580800 | bytes 9437184 | tf_op jit(solution)/shard_map/td,dgc->gtc/dot_general | solution.py:133
  18.2 5.7 %pad_maximum_fusion = f32[4,512,648]{2,1,0:T(8,128)} fusion(f32[4,512,8]{2,1,0:T(8,128)S(1)} %bitcast.152, f32[4,512,128]{2,1,0:T(8,128)} %convolution_bitcast_fusion, f32[4,512,512]{2,1,0:T(8,128)} %fusion.20), kind=kLoop, calls=%fused_computation.12 | loop fusion | flops 2654208 | bytes 10616832 | tf_op jit(solution)/shard_map/concatenate | solution.py:137
  49.9 6.8 %fusion.23 = f32[4,512,512]{2,1,0:T(8,128)} fusion(bf16[1024,4,512]{2,1,0:T(4,128)(2,1)} %param.19, bf16[256,1024]{1,0:T(8,128)(2,1)S(1)} %copy-done.17, bf16[256,1024]{1,0:T(8,128)(2,1)S(1)} %copy-done.15), kind=kOutput, calls=%fused_computation.28 | convolution fusion | flops 2149580800 | bytes 9437184 | tf_op jit(solution)/shard_map/td,dgc->gtc/dot_general | solution.py:133
  56.7 36.3 %reduce-scatter.3.cloned.1.call-done = f32[1,512,648]{2,1,0:T(8,128)} async-done(((f32[4,512,648]{2,1,0:T(8,128)}), f32[1,512,648]{2,1,0:T(8,128)}) %reduce-scatter.3.cloned.1.call-update) | async-done | bytes 1327120 | tf_op jit(solution)/shard_map/reduce_scatter | solution.py:136
  108.3 3.4 %collective-permute-start.2 = (bf16[3,768]{1,0:T(4,128)(2,1)S(1)}, bf16[3,768]{1,0:T(4,128)(2,1)S(1)}, u32[]{:S(2)}, u32[]{:S(2)}) collective-permute-start(bf16[3,768]{1,0:T(4,128)(2,1)S(1)} %pad_maximum_fusion.6), channel_id=1, source_target_pairs={{0,8},{8,16},{16,24},{24,32},{32,40},{40,48},{48,56},{56,64},{64,7... | collective-permute-start | bytes 13832 | tf_op jit(solution)/shard_map/ppermute | solution.py:17
  112.8 3.5 %multiply_convert_fusion.1 = bf16[512,512]{1,0:T(8,128)(2,1)} fusion(f32[512,512]{1,0:T(8,128)} %fusion.56, f32[512,512]{1,0:T(8,128)} %fusion.58, bf16[512,512]{1,0:T(8,128)(2,1)S(1)} %slice-done, bf16[3,512]{1,0:T(4,128)(2,1)S(1)} %slice.293, f32[512]{0:T(512)S(1)} %bitcast.173, f32[512]{0:T(512)S(1)} %bitcast.174, f32[512]{0:T(512)S(1)} %bitcast.172, ...), kind=kOutput, calls=%fused_computation.54 | convolution fusion | flops 12325376 | bytes 3171840 | tf_op jit(solution)/shard_map/dot_general | solution.py:93
  118.8 2.2 multiply_convert_fusion.2
  125.4 3.2 %collective-permute-start.3 = (f32[8,65,128]{2,1,0:T(8,128)}, f32[8,65,128]{2,1,0:T(8,128)}, u32[]{:S(2)}, u32[]{:S(2)}) collective-permute-start(f32[8,65,128]{2,1,0:T(8,128)} %pad_maximum_fusion.4), channel_id=1, source_target_pairs={{0,8},{8,16},{16,24},{24,32},{32,40},{40,48},{48,56},{56,64},{64,7... | collective-permute-start | bytes 798728 | tf_op jit(solution)/shard_map/ppermute | solution.py:17
  129.3 3.1 %collective-permute-start.4 = (f32[8,65,128]{2,1,0:T(8,128)}, f32[8,65,128]{2,1,0:T(8,128)}, u32[]{:S(2)}, u32[]{:S(2)}) collective-permute-start(f32[8,65,128]{2,1,0:T(8,128)} %pad_maximum_fusion.5), channel_id=1, source_target_pairs={{8,0},{16,8},{24,16},{32,24},{40,32},{48,40},{56,48},{64,56},{72,6... | collective-permute-start | bytes 798728 | tf_op jit(solution)/shard_map/ppermute | solution.py:17
  140.6 2.2 add_select_fusion.7
  142.8 7.8 %collective-permute-start.6 = (f32[8,65,128]{2,1,0:T(8,128)}, f32[8,65,128]{2,1,0:T(8,128)}, u32[]{:S(2)}, u32[]{:S(2)}) collective-permute-start(f32[8,65,128]{2,1,0:T(8,128)} %get-tuple-element.25), channel_id=1, source_target_pairs={{16,0},{24,8},{32,16},{40,24},{48,32},{56,40},{64,48},{72,56},{80,... | collective-permute-start | bytes 798728 | tf_op jit(solution)/shard_map/ppermute | solution.py:17
  150.6 4.3 %fusion.46 = f32[512,3,8,64]{0,3,2,1:T(8,128)} fusion(f32[3,1,8,64,128]{4,3,2,1,0:T(8,128)} %param.31, bf16[512,256]{1,0:T(8,128)(2,1)} %copy-done.5), kind=kOutput, calls=%fused_computation.58 | convolution fusion | flops 1207959552 | bytes 4063232 | tf_op jit(solution)/shard_map/tn,shpn->tshp/dot_general | solution.py:39
  164.0 9.1 %collective-permute-done.5 = f32[8,65,128]{2,1,0:T(8,128)} collective-permute-done((f32[8,65,128]{2,1,0:T(8,128)}, f32[8,65,128]{2,1,0:T(8,128)}, u32[]{:S(2)}, u32[]{:S(2)}) %collective-permute-start.5) | collective-permute-done | bytes 266272 | tf_op jit(solution)/shard_map/ppermute | solution.py:17
  177.3 3.6 %collective-permute-start.8 = (f32[8,65,128]{2,1,0:T(8,128)}, f32[8,65,128]{2,1,0:T(8,128)}, u32[]{:S(2)}, u32[]{:S(2)}) collective-permute-start(f32[8,65,128]{2,1,0:T(8,128)} %get-tuple-element.29), channel_id=1, source_target_pairs={{32,0},{40,8},{48,16},{56,24},{64,32},{72,40},{80,48},{88,56},{96,... | collective-permute-start | bytes 798728 | tf_op jit(solution)/shard_map/ppermute | solution.py:17
  182.1 5.6 %collective-permute-start.7 = (f32[8,65,128]{2,1,0:T(8,128)}, f32[8,65,128]{2,1,0:T(8,128)}, u32[]{:S(2)}, u32[]{:S(2)}) collective-permute-start(f32[8,65,128]{2,1,0:T(8,128)} %get-tuple-element.27), channel_id=1, source_target_pairs={{0,32},{8,40},{16,48},{24,56},{32,64},{40,72},{48,80},{56,88},{64,... | collective-permute-start | bytes 798728 | tf_op jit(solution)/shard_map/ppermute | solution.py:17
  192.7 10.5 %collective-permute-done.8 = f32[8,65,128]{2,1,0:T(8,128)} collective-permute-done((f32[8,65,128]{2,1,0:T(8,128)}, f32[8,65,128]{2,1,0:T(8,128)}, u32[]{:S(2)}, u32[]{:S(2)}) %collective-permute-start.8) | collective-permute-done | bytes 266272 | tf_op jit(solution)/shard_map/ppermute | solution.py:17
  204.1 2.9 %collective-permute-done.7 = f32[8,65,128]{2,1,0:T(8,128)} collective-permute-done((f32[8,65,128]{2,1,0:T(8,128)}, f32[8,65,128]{2,1,0:T(8,128)}, u32[]{:S(2)}, u32[]{:S(2)}) %collective-permute-start.7) | collective-permute-done | bytes 266272 | tf_op jit(solution)/shard_map/ppermute | solution.py:17
  213.1 3.4 %fusion.19 = f32[512,512]{0,1:T(8,128)} fusion(f32[512,3,8,64]{0,3,2,1:T(8,128)} %fusion.46, f32[512,3]{0,1:T(4,128)S(1)} %copy-done.22), kind=kLoop, calls=%fused_computation.26 | loop fusion | flops 1310720 | bytes 4200448
  216.5 5.6 %collective-permute-start.9 = (f32[8,65,128]{2,1,0:T(8,128)}, f32[8,65,128]{2,1,0:T(8,128)}, u32[]{:S(2)}, u32[]{:S(2)}) collective-permute-start(f32[8,65,128]{2,1,0:T(8,128)} %get-tuple-element.31), channel_id=1, source_target_pairs={{0,64},{8,72},{16,80},{24,88},{32,96},{40,104},{48,112},{56,120},{... | collective-permute-start | bytes 798728 | tf_op jit(solution)/shard_map/ppermute | solution.py:17
  233.8 7.1 %collective-permute-start.11 = (f32[8,65,128]{2,1,0:T(8,128)}, f32[8,65,128]{2,1,0:T(8,128)}, u32[]{:S(2)}, u32[]{:S(2)}) collective-permute-start(f32[8,65,128]{2,1,0:T(8,128)} %get-tuple-element.35), channel_id=1, source_target_pairs={{0,128},{8,136},{16,144},{24,152},{32,160},{40,168},{48,176},{56,1... | collective-permute-start | bytes 798728 | tf_op jit(solution)/shard_map/ppermute | solution.py:17
  240.9 8.9 %fusion.33 = f32[512,8,64]{0,2,1:T(8,128)} fusion(bf16[512,8,64]{0,2,1:T(8,128)(2,1)S(1)} %bitcast.149, f32[8,512]{1,0:T(8,128)S(1)} %copy.139, f32[512,512]{1,0:T(8,128)} %fusion.69, f32[8,512]{1,0:T(8,128)S(1)} %copy.137, pred[512,512]{1,0:T(8,128)(4,1)S(1)} %copy-done.18, f32[512,8,64]{0,2,1:T(8,128)} %bitcast.154, f32[512,8]{0,1:T(8,128)S(1)} %copy.140), kind=kOutput, calls=%fused_computation.36 | convolution fusion | flops 1621622784 | bytes 3981312 | tf_op jit(solution)/shard_map/hij,jhp->ihp/dot_general | solution.py:38
  256.0 2.9 %fusion.32 = f32[512,8,64]{0,2,1:T(8,128)} fusion(f32[512,8,64]{0,2,1:T(8,128)} %fusion.33, f32[8]{0:T(128)S(1)} %bitcast.181, f32[512,8]{0,1:T(8,128)S(1)} %copy.141, f32[8,65,128]{2,1,0:T(8,128)S(1)} %multiply_add_fusion, bf16[512,8,64]{0,2,1:T(8,128)(2,1)S(1)} %bitcast.150, bf16[512,256]{1,0:T(8,128)(2,1)S(1)} %copy-done.6), kind=kOutput, calls=%fused_computation.35 | convolution fusion | flops 403963904 | bytes 3031552 | tf_op jit(solution)/shard_map/tn,hpn->thp/dot_general | solution.py:242
  267.1 4.0 %psum.7 = f32[512]{0:T(512)S(1)} all-reduce(f32[512]{0:T(512)S(1)} %multiply_reduce_fusion), channel_id=1, replica_groups=mesh['seq'=32,'row'=2,'col'=4] {'row'}, use_global_device_ids=true, to_apply=%region_16.17 | all-reduce | flops 512 | bytes 4096 | tf_op jit(solution)/shard_map/psum | solution.py:257
  271.2 2.2 fusion.51
  (272 shorter events, 108.7 us)
Async XLA Ops:
  7.2 85.8 %reduce-scatter.3.cloned.1.call-start = ((), (), s32[]{:S(2)}) async-start(), calls=%async_computation.2 | async-start | bytes 7864320 | tf_op jit(solution)/shard_map/reduce_scatter | solution.py:136
  7.2 2.5 collective-permute-start
  23.9 19.5 %copy-start.23 = (bf16[4,1,512]{2,0,1:T(4,128)(2,1)S(1)}, bf16[4,1,512]{2,0,1:T(4,128)(2,1)}, u32[]{:S(2)}) copy-start(bf16[4,1,512]{2,0,1:T(4,128)(2,1)} %param.22) | copy-start | bytes 12292
  23.9 25.9 %copy-start.15 = (bf16[256,1024]{1,0:T(8,128)(2,1)S(1)}, bf16[256,1024]{1,0:T(8,128)(2,1)}, u32[]{:S(2)}) copy-start(bf16[256,1024]{1,0:T(8,128)(2,1)} %copy-done.14) | copy-start | bytes 1572868
  24.0 25.9 %copy-start.17 = (bf16[256,1024]{1,0:T(8,128)(2,1)S(1)}, bf16[256,1024]{1,0:T(8,128)(2,1)}, u32[]{:S(2)}) copy-start(bf16[256,1024]{1,0:T(8,128)(2,1)} %copy-done.16) | copy-start | bytes 1572868
  24.0 240.6 %reduce-scatter.5.cloned.1.call-start = ((), (), s32[]{:S(2)}) async-start(), calls=%async_computation.3 | async-start | bytes 5242880 | tf_op jit(solution)/shard_map/reduce_scatter | solution.py:141
  37.3 66.4 %copy-start.29 = (pred[3]{0:T(512)(128)(4,1)}, pred[3]{0:T(512)(128)(4,1)S(1)}, u32[]{:S(2)}) copy-start(pred[3]{0:T(512)(128)(4,1)S(1)} %add_compare_fusion) | copy-start | bytes 13
  49.8 45.6 %copy-start.27 = (f32[1,8]{1,0:T(1,128)S(1)}, f32[1,8]{1,0:T(1,128)}, u32[]{:S(2)}) copy-start(f32[1,8]{1,0:T(1,128)} %param.26) | copy-start | bytes 100
  49.8 45.6 %copy-start.28 = (f32[1,8]{1,0:T(1,128)S(1)}, f32[1,8]{1,0:T(1,128)}, u32[]{:S(2)}) copy-start(f32[1,8]{1,0:T(1,128)} %param.27) | copy-start | bytes 100
  100.5 5.5 %collective-permute-start.1 = (bf16[512,128]{1,0:T(8,128)(2,1)}, bf16[512,128]{1,0:T(8,128)(2,1)S(1)}, u32[]{:S(2)}, u32[]{:S(2)}) collective-permute-start(bf16[512,128]{1,0:T(8,128)(2,1)} %slice.225), channel_id=1, source_target_pairs={{0,4},{4,0},{1,5},{5,1},{2,6},{6,2},{3,7},{7,3},{8,12},{12,8},{9,1... | collective-permute-start | bytes 393224 | tf_op jit(solution)/shard_map/ppermute | solution.py:145
  108.3 4.4 %collective-permute-start.2 = (bf16[3,768]{1,0:T(4,128)(2,1)S(1)}, bf16[3,768]{1,0:T(4,128)(2,1)S(1)}, u32[]{:S(2)}, u32[]{:S(2)}) collective-permute-start(bf16[3,768]{1,0:T(4,128)(2,1)S(1)} %pad_maximum_fusion.6), channel_id=1, source_target_pairs={{0,8},{8,16},{16,24},{24,32},{32,40},{40,48},{48,56},{56,64},{64,7... | collective-permute-start | bytes 13832 | tf_op jit(solution)/shard_map/ppermute | solution.py:17
  125.4 15.2 %collective-permute-start.3 = (f32[8,65,128]{2,1,0:T(8,128)}, f32[8,65,128]{2,1,0:T(8,128)}, u32[]{:S(2)}, u32[]{:S(2)}) collective-permute-start(f32[8,65,128]{2,1,0:T(8,128)} %pad_maximum_fusion.4), channel_id=1, source_target_pairs={{0,8},{8,16},{16,24},{24,32},{32,40},{40,48},{48,56},{56,64},{64,7... | collective-permute-start | bytes 798728 | tf_op jit(solution)/shard_map/ppermute | solution.py:17
  129.3 10.4 %collective-permute-start.4 = (f32[8,65,128]{2,1,0:T(8,128)}, f32[8,65,128]{2,1,0:T(8,128)}, u32[]{:S(2)}, u32[]{:S(2)}) collective-permute-start(f32[8,65,128]{2,1,0:T(8,128)} %pad_maximum_fusion.5), channel_id=1, source_target_pairs={{8,0},{16,8},{24,16},{32,24},{40,32},{48,40},{56,48},{64,56},{72,6... | collective-permute-start | bytes 798728 | tf_op jit(solution)/shard_map/ppermute | solution.py:17
  142.8 38.0 %copy-start.6 = (bf16[512,256]{1,0:T(8,128)(2,1)S(1)}, bf16[512,256]{1,0:T(8,128)(2,1)}, u32[]{:S(2)}) copy-start(bf16[512,256]{1,0:T(8,128)(2,1)} %copy-done.5) | copy-start | bytes 786436
  142.8 20.3 %collective-permute-start.6 = (f32[8,65,128]{2,1,0:T(8,128)}, f32[8,65,128]{2,1,0:T(8,128)}, u32[]{:S(2)}, u32[]{:S(2)}) collective-permute-start(f32[8,65,128]{2,1,0:T(8,128)} %get-tuple-element.25), channel_id=1, source_target_pairs={{16,0},{24,8},{32,16},{40,24},{48,32},{56,40},{64,48},{72,56},{80,... | collective-permute-start | bytes 798728 | tf_op jit(solution)/shard_map/ppermute | solution.py:17
  154.9 58.2 %copy-start.22 = (f32[512,3]{0,1:T(4,128)S(1)}, f32[512,3]{0,1:T(4,128)}, u32[]{:S(2)}) copy-start(f32[512,3]{0,1:T(4,128)} %copy.160) | copy-start | bytes 18436
  154.9 18.3 %collective-permute-start.5 = (f32[8,65,128]{2,1,0:T(8,128)}, f32[8,65,128]{2,1,0:T(8,128)}, u32[]{:S(2)}, u32[]{:S(2)}) collective-permute-start(f32[8,65,128]{2,1,0:T(8,128)} %get-tuple-element.23), channel_id=1, source_target_pairs={{0,16},{8,24},{16,32},{24,40},{32,48},{40,56},{48,64},{56,72},{64,... | collective-permute-start | bytes 798728 | tf_op jit(solution)/shard_map/ppermute | solution.py:17
  177.3 25.9 %collective-permute-start.8 = (f32[8,65,128]{2,1,0:T(8,128)}, f32[8,65,128]{2,1,0:T(8,128)}, u32[]{:S(2)}, u32[]{:S(2)}) collective-permute-start(f32[8,65,128]{2,1,0:T(8,128)} %get-tuple-element.29), channel_id=1, source_target_pairs={{32,0},{40,8},{48,16},{56,24},{64,32},{72,40},{80,48},{88,56},{96,... | collective-permute-start | bytes 798728 | tf_op jit(solution)/shard_map/ppermute | solution.py:17
  182.1 24.9 %collective-permute-start.7 = (f32[8,65,128]{2,1,0:T(8,128)}, f32[8,65,128]{2,1,0:T(8,128)}, u32[]{:S(2)}, u32[]{:S(2)}) collective-permute-start(f32[8,65,128]{2,1,0:T(8,128)} %get-tuple-element.27), channel_id=1, source_target_pairs={{0,32},{8,40},{16,48},{24,56},{32,64},{40,72},{48,80},{56,88},{64,... | collective-permute-start | bytes 798728 | tf_op jit(solution)/shard_map/ppermute | solution.py:17
  209.1 31.8 %copy-start.18 = (pred[512,512]{1,0:T(8,128)(4,1)S(1)}, pred[512,512]{1,0:T(8,128)(4,1)}, u32[]{:S(2)}) copy-start(pred[512,512]{1,0:T(8,128)(4,1)} %fusion.45) | copy-start | bytes 786436
  211.2 16.1 %collective-permute-start.10 = (f32[8,65,128]{2,1,0:T(8,128)}, f32[8,65,128]{2,1,0:T(8,128)}, u32[]{:S(2)}, u32[]{:S(2)}) collective-permute-start(f32[8,65,128]{2,1,0:T(8,128)} %get-tuple-element.33), channel_id=1, source_target_pairs={{64,0},{72,8},{80,16},{88,24},{96,32},{104,40},{112,48},{120,56},{... | collective-permute-start | bytes 798728 | tf_op jit(solution)/shard_map/ppermute | solution.py:17
  216.5 11.8 %collective-permute-start.9 = (f32[8,65,128]{2,1,0:T(8,128)}, f32[8,65,128]{2,1,0:T(8,128)}, u32[]{:S(2)}, u32[]{:S(2)}) collective-permute-start(f32[8,65,128]{2,1,0:T(8,128)} %get-tuple-element.31), channel_id=1, source_target_pairs={{0,64},{8,72},{16,80},{24,88},{32,96},{40,104},{48,112},{56,120},{... | collective-permute-start | bytes 798728 | tf_op jit(solution)/shard_map/ppermute | solution.py:17
  232.5 19.5 %collective-permute-start.12 = (f32[8,65,128]{2,1,0:T(8,128)}, f32[8,65,128]{2,1,0:T(8,128)}, u32[]{:S(2)}, u32[]{:S(2)}) collective-permute-start(f32[8,65,128]{2,1,0:T(8,128)} %get-tuple-element.37), channel_id=1, source_target_pairs={{128,0},{136,8},{144,16},{152,24},{160,32},{168,40},{176,48},{184,... | collective-permute-start | bytes 798728 | tf_op jit(solution)/shard_map/ppermute | solution.py:17
  233.8 19.2 %collective-permute-start.11 = (f32[8,65,128]{2,1,0:T(8,128)}, f32[8,65,128]{2,1,0:T(8,128)}, u32[]{:S(2)}, u32[]{:S(2)}) collective-permute-start(f32[8,65,128]{2,1,0:T(8,128)} %get-tuple-element.35), channel_id=1, source_target_pairs={{0,128},{8,136},{16,144},{24,152},{32,160},{40,168},{48,176},{56,1... | collective-permute-start | bytes 798728 | tf_op jit(solution)/shard_map/ppermute | solution.py:17
  (43 other events, 379.0 us)
Sparse Core Ops, SparseCore 0:
  24.1 68.8 reduce-scatter.2
  103.8 48.5 reduce-scatter.4

commit v10 on v7

--- a/solution.py
+++ b/solution.py
@@ -261,7 +261,7 @@
     )
     gated = y_full.reshape(rows_here, channels) * jax.nn.silu(z_gate.astype(jnp.float32))
     partial_sq = jnp.sum(gated * gated, axis=-1)
-    total_sq = lax.psum(partial_sq, "row")
+    total_sq = partial_sq + lax.ppermute(partial_sq, "row", [(0, 1), (1, 0)])
     mean_sq = total_sq / (channels * lax.axis_size("row"))
     gated_out = (gated * lax.rsqrt(mean_sq + EPSILON)[:, None] * norm_gain[0][None, :]).astype(
         jnp.bfloat16

time: 280 us -> 269 us (0.961)
  other arithmetic: 61.8 us -> 54.6 us
  blocking collectives: 5.27 us -> 0 us
    psum x1 -> x0, blocking collectives: 5.27 us -> none  [shards(): total_sq = lax.psum(partial_sq, 'row')]
  transfers between devices with their start and end apart: 15 -> 16, of which waited for: 11 -> 11; matrix products, arithmetic and copies ran while one was open for 37% -> 34% of each run, Pallas kernels for 0% -> 0%
where the time goes in v10:
time: 269 us; the launch traced here: 267 us
  waiting for transfers between devices  78.7 us (29%)
  other arithmetic  54.6 us (20%)
  starting transfers between devices  42.4 us (16%)
  matrix products  39.9 us (15%)
  local copies, waits for them, and re-layouts  28.6 us (11%)
  between operations  22.9 us (9%)
    reduce_scatter x1, waiting for transfers between devices, shards(): lax.psum_scatter(jnp.concatenate([x_part, bc_part, dt_part], axis=2), 'co...  40.5 us
    ppermute x11, starting transfers between devices, from_behind(): lax.ppermute(value, axis, [(source, source + steps) for source in range(f...  38.1 us
    ppermute x11, waiting for transfers between devices, from_behind(): lax.ppermute(value, axis, [(source, source + steps) for source in range(f...  37.4 us
    slice x13, local copies, waits for them, and re-layouts, unpack(): return (packed[:, p_n, 0], packed[:, :p_n], packed[0, p_n, n_n - 1])  13.5 us
    dot_general x3, matrix products, shards(): jnp.einsum('td,dgc->gtc', tokens, weight, preferred_element_type=jnp.floa...  12.1 us
    dot_general x6, matrix products, convolve(): from_edge = jnp.dot(picker, table, preferred_element_type=jnp.float32)  10.4 us
    select_n x5, other arithmetic, near_far(): jnp.where(keep, near[1], far_a[:, None, None] * near[1] + far_b)  8.78 us
    dot_general x1, matrix products, local_terms(): jnp.einsum('hij,jhp->ihp', mixing, x_vals.astype(jnp.float32), precision=...  8.26 us
  transfers between devices with their start and end apart: 16, of which 11 were waited for; matrix products, arithmetic and copies ran while one was open for 34% of the time, Pallas kernels for 0%

profile of v10, /device:TPU:71, one launch (start us, length us, event | category | flops | bytes accessed | tf_op | source)
XLA Modules:
  0.0 267.0 jit_solution(2387239584150033172)
XLA Ops:
  12.1 4.5 %fusion.20 = f32[4,512,512]{2,1,0:T(8,128)} fusion(bf16[1024,4,512]{2,1,0:T(4,128)(2,1)S(1)} %copy-done.42, bf16[256,1024]{1,0:T(8,128)(2,1)S(1)} %get-tuple-element.116, bf16[256,1024]{1,0:T(8,128)(2,1)S(1)} %get-tuple-element.115), kind=kOutput, calls=%fused_computation.27 | convolution fusion | flops 2149580800 | bytes 9437184 | tf_op jit(solution)/shard_map/td,dgc->gtc/dot_general | solution.py:133
  17.3 5.4 %pad_maximum_fusion = f32[4,512,648]{2,1,0:T(8,128)} fusion(f32[4,512,8]{2,1,0:T(8,128)S(1)} %bitcast.163, f32[4,512,128]{2,1,0:T(8,128)S(1)} %convolution_bitcast_fusion, f32[4,512,512]{2,1,0:T(8,128)} %fusion.20), kind=kLoop, calls=%fused_computation.12 | loop fusion | flops 2654208 | bytes 10616832 | tf_op jit(solution)/shard_map/concatenate | solution.py:137
  44.2 6.8 %fusion.23 = f32[4,512,512]{2,1,0:T(8,128)} fusion(bf16[1024,4,512]{2,1,0:T(4,128)(2,1)} %param.19, bf16[256,1024]{1,0:T(8,128)(2,1)S(1)} %copy-done.15, bf16[256,1024]{1,0:T(8,128)(2,1)S(1)} %get-tuple-element.115), kind=kOutput, calls=%fused_computation.28 | convolution fusion | flops 2149580800 | bytes 9437184 | tf_op jit(solution)/shard_map/td,dgc->gtc/dot_general | solution.py:133
  51.1 40.5 %reduce-scatter.3.cloned.1.call-done = f32[1,512,648]{2,1,0:T(8,128)} async-done(((f32[4,512,648]{2,1,0:T(8,128)}), f32[1,512,648]{2,1,0:T(8,128)}) %reduce-scatter.3.cloned.1.call-update) | async-done | bytes 1327120 | tf_op jit(solution)/shard_map/reduce_scatter | solution.py:136
  97.9 3.4 %collective-permute-start.2 = (bf16[3,768]{1,0:T(4,128)(2,1)S(1)}, bf16[3,768]{1,0:T(4,128)(2,1)S(1)}, u32[]{:S(2)}, u32[]{:S(2)}) collective-permute-start(bf16[3,768]{1,0:T(4,128)(2,1)S(1)} %pad_maximum_fusion.14), channel_id=1, source_target_pairs={{0,8},{8,16},{16,24},{24,32},{32,40},{40,48},{48,56},{56,64},{64,7... | collective-permute-start | bytes 13832 | tf_op jit(solution)/shard_map/ppermute | solution.py:17
  104.1 4.4 %multiply_convert_fusion.1 = bf16[512,512]{1,0:T(8,128)(2,1)} fusion(f32[512,512]{1,0:T(8,128)} %fusion.57, f32[512,512]{1,0:T(8,128)S(1)} %fusion.59, bf16[512,512]{1,0:T(8,128)(2,1)} %slice.211, bf16[3,512]{1,0:T(4,128)(2,1)S(1)} %slice.287, f32[512]{0:T(512)} %bitcast.188, f32[512]{0:T(512)} %bitcast.189, f32[512]{0:T(512)} %bitcast.187, ...), kind=kOutput, calls=%fused_computation.54 | convolution fusion | flops 12325376 | bytes 3171840 | tf_op jit(solution)/shard_map/dot_general | solution.py:93
  110.6 2.1 multiply_convert_fusion.2
  112.7 2.1 fusion.11
  120.2 4.2 %collective-permute-start.3 = (f32[8,65,128]{2,1,0:T(8,128)}, f32[8,65,128]{2,1,0:T(8,128)}, u32[]{:S(2)}, u32[]{:S(2)}) collective-permute-start(f32[8,65,128]{2,1,0:T(8,128)} %pad_maximum_fusion.4), channel_id=1, source_target_pairs={{0,8},{8,16},{16,24},{24,32},{32,40},{40,48},{48,56},{56,64},{64,7... | collective-permute-start | bytes 798728 | tf_op jit(solution)/shard_map/ppermute | solution.py:17
  135.8 5.6 %collective-permute-start.6 = (f32[8,65,128]{2,1,0:T(8,128)}, f32[8,65,128]{2,1,0:T(8,128)}, u32[]{:S(2)}, u32[]{:S(2)}) collective-permute-start(f32[8,65,128]{2,1,0:T(8,128)} %pad_maximum_fusion.7), channel_id=1, source_target_pairs={{16,0},{24,8},{32,16},{40,24},{48,32},{56,40},{64,48},{72,56},{80,... | collective-permute-start | bytes 798728 | tf_op jit(solution)/shard_map/ppermute | solution.py:17
  142.2 3.7 %collective-permute-start.5 = (f32[8,65,128]{2,1,0:T(8,128)}, f32[8,65,128]{2,1,0:T(8,128)}, u32[]{:S(2)}, u32[]{:S(2)}) collective-permute-start(f32[8,65,128]{2,1,0:T(8,128)} %pad_maximum_fusion.6), channel_id=1, source_target_pairs={{0,16},{8,24},{16,32},{24,40},{32,48},{40,56},{48,64},{56,72},{64,... | collective-permute-start | bytes 798728 | tf_op jit(solution)/shard_map/ppermute | solution.py:17
  145.9 2.6 fusion.46
  148.6 8.6 %collective-permute-done.6 = f32[8,65,128]{2,1,0:T(8,128)} collective-permute-done((f32[8,65,128]{2,1,0:T(8,128)}, f32[8,65,128]{2,1,0:T(8,128)}, u32[]{:S(2)}, u32[]{:S(2)}) %collective-permute-start.6) | collective-permute-done | bytes 266272 | tf_op jit(solution)/shard_map/ppermute | solution.py:17
  166.5 4.3 %collective-permute-start.8 = (f32[8,65,128]{2,1,0:T(8,128)}, f32[8,65,128]{2,1,0:T(8,128)}, u32[]{:S(2)}, u32[]{:S(2)}) collective-permute-start(f32[8,65,128]{2,1,0:T(8,128)} %pad_maximum_fusion.9), channel_id=1, source_target_pairs={{32,0},{40,8},{48,16},{56,24},{64,32},{72,40},{80,48},{88,56},{96,... | collective-permute-start | bytes 798728 | tf_op jit(solution)/shard_map/ppermute | solution.py:17
  171.6 5.5 %collective-permute-start.7 = (f32[8,65,128]{2,1,0:T(8,128)}, f32[8,65,128]{2,1,0:T(8,128)}, u32[]{:S(2)}, u32[]{:S(2)}) collective-permute-start(f32[8,65,128]{2,1,0:T(8,128)} %pad_maximum_fusion.8), channel_id=1, source_target_pairs={{0,32},{8,40},{16,48},{24,56},{32,64},{40,72},{48,80},{56,88},{64,... | collective-permute-start | bytes 798728 | tf_op jit(solution)/shard_map/ppermute | solution.py:17
  177.2 2.3 fusion.70
  179.5 7.8 %collective-permute-done.8 = f32[8,65,128]{2,1,0:T(8,128)} collective-permute-done((f32[8,65,128]{2,1,0:T(8,128)}, f32[8,65,128]{2,1,0:T(8,128)}, u32[]{:S(2)}, u32[]{:S(2)}) %collective-permute-start.8) | collective-permute-done | bytes 266272 | tf_op jit(solution)/shard_map/ppermute | solution.py:17
  190.9 9.5 %collective-permute-done.7 = f32[8,65,128]{2,1,0:T(8,128)} collective-permute-done((f32[8,65,128]{2,1,0:T(8,128)}, f32[8,65,128]{2,1,0:T(8,128)}, u32[]{:S(2)}, u32[]{:S(2)}) %collective-permute-start.7) | collective-permute-done | bytes 266272 | tf_op jit(solution)/shard_map/ppermute | solution.py:17
  206.2 2.9 %collective-permute-start.10 = (f32[8,65,128]{2,1,0:T(8,128)}, f32[8,65,128]{2,1,0:T(8,128)}, u32[]{:S(2)}, u32[]{:S(2)}) collective-permute-start(f32[8,65,128]{2,1,0:T(8,128)} %pad_maximum_fusion.11), channel_id=1, source_target_pairs={{64,0},{72,8},{80,16},{88,24},{96,32},{104,40},{112,48},{120,56},{... | collective-permute-start | bytes 798728 | tf_op jit(solution)/shard_map/ppermute | solution.py:17
  223.8 3.7 %collective-permute-start.12 = (f32[8,65,128]{2,1,0:T(8,128)}, f32[8,65,128]{2,1,0:T(8,128)}, u32[]{:S(2)}, u32[]{:S(2)}) collective-permute-start(f32[8,65,128]{2,1,0:T(8,128)} %pad_maximum_fusion.13), channel_id=1, source_target_pairs={{128,0},{136,8},{144,16},{152,24},{160,32},{168,40},{176,48},{184,... | collective-permute-start | bytes 798728 | tf_op jit(solution)/shard_map/ppermute | solution.py:17
  227.5 8.3 %fusion.33 = f32[512,8,64]{0,2,1:T(8,128)S(1)} fusion(bf16[512,8,64]{0,2,1:T(8,128)(2,1)} %bitcast.160, f32[8,512]{1,0:T(8,128)S(1)} %copy.139, f32[512,512]{1,0:T(8,128)} %fusion.70, f32[8,512]{1,0:T(8,128)S(1)} %copy.137, pred[512,512]{1,0:T(8,128)(4,1)} %fusion.45, f32[512,8,64]{0,2,1:T(8,128)} %bitcast.165, f32[512,8]{0,1:T(8,128)S(1)} %copy.140), kind=kOutput, calls=%fused_computation.36 | convolution fusion | flops 1621622784 | bytes 3981312 | tf_op jit(solution)/shard_map/hij,jhp->ihp/dot_general | solution.py:38
  240.6 6.5 %collective-permute-done.11 = f32[8,65,128]{2,1,0:T(8,128)S(1)} collective-permute-done((f32[8,65,128]{2,1,0:T(8,128)}, f32[8,65,128]{2,1,0:T(8,128)S(1)}, u32[]{:S(2)}, u32[]{:S(2)}) %collective-permute-start.11) | collective-permute-done | bytes 266272 | tf_op jit(solution)/shard_map/ppermute | solution.py:17
  254.2 2.6 collective-permute-start.13
  256.8 2.2 select_bitcast_fusion
  (279 shorter events, 94.5 us)
Async XLA Ops:
  7.2 84.4 %reduce-scatter.3.cloned.1.call-start = ((), (), s32[]{:S(2)}) async-start(), calls=%async_computation.2 | async-start | bytes 7864320 | tf_op jit(solution)/shard_map/reduce_scatter | solution.py:136
  7.2 2.6 collective-permute-start
  22.8 16.0 %copy-start.18 = (bf16[4,1,512]{2,0,1:T(4,128)(2,1)S(1)}, bf16[4,1,512]{2,0,1:T(4,128)(2,1)}, u32[]{:S(2)}) copy-start(bf16[4,1,512]{2,0,1:T(4,128)(2,1)} %param.22) | copy-start | bytes 12292
  22.8 21.5 %copy-start.15 = (bf16[256,1024]{1,0:T(8,128)(2,1)S(1)}, bf16[256,1024]{1,0:T(8,128)(2,1)}, u32[]{:S(2)}) copy-start(bf16[256,1024]{1,0:T(8,128)(2,1)} %copy-done.14) | copy-start | bytes 1572868
  22.8 229.6 %reduce-scatter.5.cloned.1.call-start = ((), (), s32[]{:S(2)}) async-start(), calls=%async_computation.3 | async-start | bytes 5242880 | tf_op jit(solution)/shard_map/reduce_scatter | solution.py:141
  34.3 63.1 %copy-start.23 = (pred[3]{0:T(512)(128)(4,1)}, pred[3]{0:T(512)(128)(4,1)S(1)}, u32[]{:S(2)}) copy-start(pred[3]{0:T(512)(128)(4,1)S(1)} %broadcast_compare_fusion.5) | copy-start | bytes 13
  44.2 48.8 %copy-start.21 = (f32[1,8]{1,0:T(1,128)S(1)}, f32[1,8]{1,0:T(1,128)}, u32[]{:S(2)}) copy-start(f32[1,8]{1,0:T(1,128)} %param.26) | copy-start | bytes 100
  44.2 48.9 %copy-start.22 = (f32[1,8]{1,0:T(1,128)S(1)}, f32[1,8]{1,0:T(1,128)}, u32[]{:S(2)}) copy-start(f32[1,8]{1,0:T(1,128)} %param.27) | copy-start | bytes 100
  95.9 1.8 collective-permute-start.1
  97.9 6.0 %collective-permute-start.2 = (bf16[3,768]{1,0:T(4,128)(2,1)S(1)}, bf16[3,768]{1,0:T(4,128)(2,1)S(1)}, u32[]{:S(2)}, u32[]{:S(2)}) collective-permute-start(bf16[3,768]{1,0:T(4,128)(2,1)S(1)} %pad_maximum_fusion.14), channel_id=1, source_target_pairs={{0,8},{8,16},{16,24},{24,32},{32,40},{40,48},{48,56},{56,64},{64,7... | collective-permute-start | bytes 13832 | tf_op jit(solution)/shard_map/ppermute | solution.py:17
  115.0 11.2 %collective-permute-start.4 = (f32[8,65,128]{2,1,0:T(8,128)S(1)}, f32[8,65,128]{2,1,0:T(8,128)}, u32[]{:S(2)}, u32[]{:S(2)}) collective-permute-start(f32[8,65,128]{2,1,0:T(8,128)S(1)} %pad_maximum_fusion.5), channel_id=1, source_target_pairs={{8,0},{16,8},{24,16},{32,24},{40,32},{48,40},{56,48},{64,56},{72,6... | collective-permute-start | bytes 798728 | tf_op jit(solution)/shard_map/ppermute | solution.py:17
  120.2 10.2 %collective-permute-start.3 = (f32[8,65,128]{2,1,0:T(8,128)}, f32[8,65,128]{2,1,0:T(8,128)}, u32[]{:S(2)}, u32[]{:S(2)}) collective-permute-start(f32[8,65,128]{2,1,0:T(8,128)} %pad_maximum_fusion.4), channel_id=1, source_target_pairs={{0,8},{8,16},{16,24},{24,32},{32,40},{40,48},{48,56},{56,64},{64,7... | collective-permute-start | bytes 798728 | tf_op jit(solution)/shard_map/ppermute | solution.py:17
  135.8 21.4 %collective-permute-start.6 = (f32[8,65,128]{2,1,0:T(8,128)}, f32[8,65,128]{2,1,0:T(8,128)}, u32[]{:S(2)}, u32[]{:S(2)}) collective-permute-start(f32[8,65,128]{2,1,0:T(8,128)} %pad_maximum_fusion.7), channel_id=1, source_target_pairs={{16,0},{24,8},{32,16},{40,24},{48,32},{56,40},{64,48},{72,56},{80,... | collective-permute-start | bytes 798728 | tf_op jit(solution)/shard_map/ppermute | solution.py:17
  142.2 18.6 %collective-permute-start.5 = (f32[8,65,128]{2,1,0:T(8,128)}, f32[8,65,128]{2,1,0:T(8,128)}, u32[]{:S(2)}, u32[]{:S(2)}) collective-permute-start(f32[8,65,128]{2,1,0:T(8,128)} %pad_maximum_fusion.6), channel_id=1, source_target_pairs={{0,16},{8,24},{16,32},{24,40},{32,48},{40,56},{48,64},{56,72},{64,... | collective-permute-start | bytes 798728 | tf_op jit(solution)/shard_map/ppermute | solution.py:17
  166.5 20.8 %collective-permute-start.8 = (f32[8,65,128]{2,1,0:T(8,128)}, f32[8,65,128]{2,1,0:T(8,128)}, u32[]{:S(2)}, u32[]{:S(2)}) collective-permute-start(f32[8,65,128]{2,1,0:T(8,128)} %pad_maximum_fusion.9), channel_id=1, source_target_pairs={{32,0},{40,8},{48,16},{56,24},{64,32},{72,40},{80,48},{88,56},{96,... | collective-permute-start | bytes 798728 | tf_op jit(solution)/shard_map/ppermute | solution.py:17
  171.6 28.8 %collective-permute-start.7 = (f32[8,65,128]{2,1,0:T(8,128)}, f32[8,65,128]{2,1,0:T(8,128)}, u32[]{:S(2)}, u32[]{:S(2)}) collective-permute-start(f32[8,65,128]{2,1,0:T(8,128)} %pad_maximum_fusion.8), channel_id=1, source_target_pairs={{0,32},{8,40},{16,48},{24,56},{32,64},{40,72},{48,80},{56,88},{64,... | collective-permute-start | bytes 798728 | tf_op jit(solution)/shard_map/ppermute | solution.py:17
  206.2 8.1 %collective-permute-start.10 = (f32[8,65,128]{2,1,0:T(8,128)}, f32[8,65,128]{2,1,0:T(8,128)}, u32[]{:S(2)}, u32[]{:S(2)}) collective-permute-start(f32[8,65,128]{2,1,0:T(8,128)} %pad_maximum_fusion.11), channel_id=1, source_target_pairs={{64,0},{72,8},{80,16},{88,24},{96,32},{104,40},{112,48},{120,56},{... | collective-permute-start | bytes 798728 | tf_op jit(solution)/shard_map/ppermute | solution.py:17
  209.9 9.7 %collective-permute-start.9 = (f32[8,65,128]{2,1,0:T(8,128)}, f32[8,65,128]{2,1,0:T(8,128)}, u32[]{:S(2)}, u32[]{:S(2)}) collective-permute-start(f32[8,65,128]{2,1,0:T(8,128)} %pad_maximum_fusion.10), channel_id=1, source_target_pairs={{0,64},{8,72},{16,80},{24,88},{32,96},{40,104},{48,112},{56,120},{... | collective-permute-start | bytes 798728 | tf_op jit(solution)/shard_map/ppermute | solution.py:17
  223.8 14.1 %collective-permute-start.12 = (f32[8,65,128]{2,1,0:T(8,128)}, f32[8,65,128]{2,1,0:T(8,128)}, u32[]{:S(2)}, u32[]{:S(2)}) collective-permute-start(f32[8,65,128]{2,1,0:T(8,128)} %pad_maximum_fusion.13), channel_id=1, source_target_pairs={{128,0},{136,8},{144,16},{152,24},{160,32},{168,40},{176,48},{184,... | collective-permute-start | bytes 798728 | tf_op jit(solution)/shard_map/ppermute | solution.py:17
  227.5 19.7 %copy-start.3 = (bf16[512,512]{0,1:T(8,128)(2,1)S(1)}, bf16[512,512]{0,1:T(8,128)(2,1)}, u32[]{:S(2)}) copy-start(bf16[512,512]{0,1:T(8,128)(2,1)} %copy-done.2) | copy-start | bytes 1572868
  227.5 19.7 %copy-start.12 = (bf16[512,256]{1,0:T(8,128)(2,1)S(1)}, bf16[512,256]{1,0:T(8,128)(2,1)}, u32[]{:S(2)}) copy-start(bf16[512,256]{1,0:T(8,128)(2,1)} %copy-done.11) | copy-start | bytes 786436
  227.5 19.7 %copy-start.35 = (f32[1,8]{1,0:T(1,128)S(1)}, f32[1,8]{1,0:T(1,128)}, u32[]{:S(2)}) copy-start(f32[1,8]{1,0:T(1,128)} %param.28) | copy-start | bytes 100
  236.6 10.5 %collective-permute-start.11 = (f32[8,65,128]{2,1,0:T(8,128)}, f32[8,65,128]{2,1,0:T(8,128)S(1)}, u32[]{:S(2)}, u32[]{:S(2)}) collective-permute-start(f32[8,65,128]{2,1,0:T(8,128)} %pad_maximum_fusion.12), channel_id=1, source_target_pairs={{0,128},{8,136},{16,144},{24,152},{32,160},{40,168},{48,176},{56,1... | collective-permute-start | bytes 798728 | tf_op jit(solution)/shard_map/ppermute | solution.py:17
  254.2 4.9 %collective-permute-start.13 = (f32[512]{0:T(512)S(1)}, f32[512]{0:T(512)S(1)}, u32[]{:S(2)}, u32[]{:S(2)}) collective-permute-start(f32[512]{0:T(512)S(1)} %multiply_reduce_fusion), channel_id=1, source_target_pairs={{0,4},{4,0},{1,5},{5,1},{2,6},{6,2},{3,7},{7,3},{8,12},{12,8},{9,1... | collective-permute-start | bytes 6152 | tf_op jit(solution)/shard_map/ppermute | solution.py:264
  (36 other events, 248.6 us)
Sparse Core Ops, SparseCore 0:
  22.9 68.5 reduce-scatter.2
  125.2 49.0 reduce-scatter.4
